TPU v7x, 128 devices: a whole 4x4x4 slice. The times are simulated.
128 devices in a mesh: tm: 16 (over z, x), space: 8 (over y, core).
Axes of the slice: x: 4, y: 4, z: 4, core: 2. Of those that a mesh axis runs over, the one named last changes fastest.
Arguments:
- query_states: bfloat16 [16, 2048, 2560], P('tm', 'space'), may hold values from -45 to 45
- key_states: bfloat16 [16, 2048, 2560], P('tm', 'space'), may hold values from -4 to 4
- value_states: bfloat16 [16, 2048, 2560], P('tm', 'space'), may hold values from -6 to 6
- history: int32 [16], P('tm'), may hold values from 0 to 2, as said below
- neighbours: int32 [16, 8, 2], P('tm', 'space'), may hold values 0 or 1
Outputs:
- attended: bfloat16 [16, 2048, 2560], P('tm', 'space')
Inputs may be any that keep to these rules, and one draw needn't show every extreme that they name: Some segment has history exactly 2 in every draw.
All inputs are finite; a program needn't handle non-finite values. No bound on the sum of `neighbours` on one device may be relied on, other than what follows from the above.
Results may differ from a plain program's by a relative error of at most 0.005.
Values may be sent and summed in bfloat16 or wider, within the bound.
No kernel may reach another device: no remote copies, remote signals or barrier semaphores. Data moves between devices by JAX's collectives and lax.ppermute only.
A program may use at most 128 MiB of HBM per device.

v0:
```python
import jax
import jax.numpy as jnp
from jax import lax
from jax.experimental import pallas as pl
from jax.experimental.pallas import tpu as pltpu
from jax.sharding import PartitionSpec as P

HEAD_DIM = 128
HG = 5
CHUNKS = 2
NEG = -1e30
EXTRA = 16


def _attn_kernel(flags_ref, q_ref, kl_ref, kc_ref, kr_ref, vl_ref, vc_ref, vr_ref, o_ref, col_ref):
    hg = q_ref.shape[1] // HEAD_DIM
    rows = q_ref.shape[0]
    lanes = o_ref.shape[1]
    inv_root = 1.0 / HEAD_DIM**0.5
    seg_ok = flags_ref[1] == 1

    @pl.when(seg_ok)
    def _():
        bias_l = jnp.where(flags_ref[0] == 1, 0.0, NEG).astype(jnp.float32)
        bias_r = jnp.where(flags_ref[2] == 1, 0.0, NEG).astype(jnp.float32)
        col_ref[...] = jnp.zeros_like(col_ref)
        for h in range(hg):
            cols = slice(h * HEAD_DIM, (h + 1) * HEAD_DIM)
            q = q_ref[:, cols]

            def scores(k_ref):
                return (
                    lax.dot_general(
                        q, k_ref[:, cols], (((1,), (1,)), ((), ())), preferred_element_type=jnp.float32
                    )
                    * inv_root
                )

            s_l = scores(kl_ref) + bias_l
            s_c = scores(kc_ref)
            s_r = scores(kr_ref) + bias_r
            top = jnp.maximum(
                jnp.maximum(s_l.max(axis=1, keepdims=True), s_c.max(axis=1, keepdims=True)),
                s_r.max(axis=1, keepdims=True),
            )
            shift = top.astype(jnp.bfloat16).astype(jnp.float32)
            p_l = jnp.exp(s_l - shift)
            p_c = jnp.exp(s_c - shift)
            p_r = jnp.exp(s_r - shift)
            denom = (
                p_l.sum(axis=1, keepdims=True) + p_c.sum(axis=1, keepdims=True) + p_r.sum(axis=1, keepdims=True)
            )
            acc = jnp.dot(p_l.astype(jnp.bfloat16), vl_ref[:, cols], preferred_element_type=jnp.float32)
            acc += jnp.dot(p_c.astype(jnp.bfloat16), vc_ref[:, cols], preferred_element_type=jnp.float32)
            acc += jnp.dot(p_r.astype(jnp.bfloat16), vr_ref[:, cols], preferred_element_type=jnp.float32)
            o_ref[0:rows, cols] = (acc / denom).astype(o_ref.dtype)
            den_hi = denom.astype(jnp.bfloat16).astype(jnp.float32)
            col_ref[:, h : h + 1] = shift
            col_ref[:, hg + h : hg + h + 1] = den_hi
            col_ref[:, 2 * hg + h : 2 * hg + h + 1] = denom - den_hi
        stats = jnp.transpose(col_ref[...])[0:EXTRA, :]
        o_ref[rows : rows + EXTRA, 0:rows] = stats.astype(o_ref.dtype)
        o_ref[rows : rows + EXTRA, rows:lanes] = jnp.zeros((EXTRA, lanes - rows), o_ref.dtype)

    @pl.when(jnp.logical_not(seg_ok))
    def _():
        row = lax.broadcasted_iota(jnp.int32, o_ref.shape, 0)
        empty = (row >= rows) & (row < rows + hg)
        o_ref[...] = jnp.where(empty, NEG, 0.0).astype(o_ref.dtype)


def attend(flags, q, k, v, kv_l, kv_r, width, base, q_base):
    rows = k.shape[0]
    heads = width // HEAD_DIM
    groups = heads // HG
    lanes = HG * HEAD_DIM
    q_spec = pl.BlockSpec((rows, lanes), lambda g, f: (0, g + q_base))
    kv_spec = pl.BlockSpec((rows, lanes), lambda g, f: (0, g + base))
    side_k = pl.BlockSpec((None, rows, lanes), lambda g, f: (0, 0, g + base))
    side_v = pl.BlockSpec((None, rows, lanes), lambda g, f: (1, 0, g + base))
    return pl.pallas_call(
        _attn_kernel,
        out_shape=jax.ShapeDtypeStruct((rows + EXTRA, width), jnp.bfloat16),
        grid_spec=pltpu.PrefetchScalarGridSpec(
            num_scalar_prefetch=1,
            grid=(groups,),
            in_specs=[q_spec, side_k, kv_spec, side_k, side_v, kv_spec, side_v],
            out_specs=pl.BlockSpec((rows + EXTRA, lanes), lambda g, f: (0, g)),
            scratch_shapes=[pltpu.VMEM((rows, 128), jnp.float32)],
        ),
        cost_estimate=pl.CostEstimate(
            flops=4 * rows * 3 * rows * HEAD_DIM * heads,
            transcendentals=rows * 3 * rows * heads,
            bytes_accessed=2 * rows * width * 2 + 6 * rows * width * 2,
        ),
    )(flags, q, kv_l, k, kv_r, kv_l, v, kv_r)


def _merge_weights(valid_ref, a_ref, b_ref, wt_ref):
    rows = wt_ref.shape[1]
    hg = a_ref.shape[1] // HEAD_DIM
    def stats(ref):
        block = ref[rows : rows + EXTRA, 0:rows].astype(jnp.float32)
        return block[0:hg], block[hg : 2 * hg] + block[2 * hg : 3 * hg]

    a_top, a_den = stats(a_ref)
    ok = valid_ref[0] == 1
    b_top, b_den = stats(b_ref)
    b_top = jnp.where(ok, b_top, NEG)
    b_den = jnp.where(ok, b_den, 0.0)
    top = jnp.maximum(a_top, b_top)
    a_w = jnp.exp(a_top - top) * a_den
    b_w = jnp.exp(b_top - top) * b_den
    total = a_w + b_w
    safe = jnp.where(total > 0.0, total, 1.0)
    wt_ref[0:hg, :] = a_w / safe
    wt_ref[8 : 8 + hg, :] = b_w / safe
    return top, total, jnp.transpose(wt_ref[...])


def _merge_body(a_ref, b_ref, o_ref, w, hg, rows):
    for h in range(hg):
        cols = slice(h * HEAD_DIM, (h + 1) * HEAD_DIM)
        o = a_ref[0:rows, cols].astype(jnp.float32) * w[:, h : h + 1]
        o = o + b_ref[0:rows, cols].astype(jnp.float32) * w[:, 8 + h : 9 + h]
        o_ref[0:rows, cols] = o.astype(o_ref.dtype)


def _merge_kernel(valid_ref, a_ref, b_ref, o_ref, wt_ref):
    rows = wt_ref.shape[1]
    lanes = o_ref.shape[1]
    hg = lanes // HEAD_DIM
    top, total, w = _merge_weights(valid_ref, a_ref, b_ref, wt_ref)
    _merge_body(a_ref, b_ref, o_ref, w, hg, rows)
    hi = total.astype(jnp.bfloat16).astype(jnp.float32)
    pad = jnp.zeros((EXTRA - 3 * hg, rows), jnp.float32)
    block = jnp.concatenate([top, hi, total - hi, pad], axis=0)
    o_ref[rows : rows + EXTRA, 0:rows] = block.astype(o_ref.dtype)
    o_ref[rows : rows + EXTRA, rows:lanes] = jnp.zeros((EXTRA, lanes - rows), o_ref.dtype)


def _final_kernel(valid_ref, a_ref, b_ref, *rest):
    o_ref, wt_ref = rest[-2], rest[-1]
    rows = wt_ref.shape[1]
    _, _, w = _merge_weights(valid_ref, a_ref, b_ref, wt_ref)
    _merge_body(a_ref, b_ref, o_ref, w, o_ref.shape[1] // HEAD_DIM, rows)


def merge(valid, a, b, base, final=False, buf=None):
    ext, width = b.shape
    rows = ext - EXTRA
    groups = width // HEAD_DIM // HG
    lanes = HG * HEAD_DIM
    a_spec = pl.BlockSpec((ext, lanes), lambda g, v: (0, g + base))
    b_spec = pl.BlockSpec((ext, lanes), lambda g, v: (0, g))
    in_specs = [a_spec, b_spec]
    operands = [valid, a, b]
    aliases = {}
    if final:
        kernel = _final_kernel
        out_shape = jax.ShapeDtypeStruct((rows, a.shape[1]), jnp.bfloat16)
        out_spec = pl.BlockSpec((rows, lanes), lambda g, v: (0, g + base))
        if buf is not None:
            in_specs.append(pl.BlockSpec(memory_space=pl.ANY))
            operands.append(buf)
            aliases = {3: 0}
    else:
        kernel = _merge_kernel
        out_shape = jax.ShapeDtypeStruct((ext, width), jnp.bfloat16)
        out_spec = b_spec
    return pl.pallas_call(
        kernel,
        out_shape=out_shape,
        grid_spec=pltpu.PrefetchScalarGridSpec(
            num_scalar_prefetch=1,
            grid=(groups,),
            in_specs=in_specs,
            out_specs=out_spec,
            scratch_shapes=[pltpu.VMEM((128, rows), jnp.float32)],
        ),
        input_output_aliases=aliases,
        cost_estimate=pl.CostEstimate(
            flops=4 * rows * width, transcendentals=0, bytes_accessed=3 * rows * width * 2
        ),
    )(*operands)


def shift_tm(x, by):
    size = lax.axis_size("tm")
    pairs = [(i, i + by) for i in range(size) if 0 <= i + by < size]
    return lax.ppermute(x, "tm", pairs)


def on_device(query_states, key_states, value_states, history, neighbours):
    _, rows, width = query_states.shape
    seg = lax.axis_index("tm")
    tile = lax.axis_index("space")
    tiles = lax.axis_size("space")
    q = query_states[0]
    k = key_states[0]
    v = value_states[0]
    tile_l = tile > 0
    tile_r = tile < tiles - 1

    def flags_for(m, d):
        m = m.astype(jnp.int32)
        return jnp.stack(
            [
                ((m[1] == 1) & tile_l).astype(jnp.int32),
                (m[0] >= d).astype(jnp.int32),
                ((m[2] == 1) & tile_r).astype(jnp.int32),
            ]
        )

    meta = jnp.concatenate([history.reshape(1), neighbours.reshape(2)]).astype(jnp.bfloat16)
    chunk_w = width // CHUNKS
    groups_c = chunk_w // HEAD_DIM // HG
    meta_rows = jnp.zeros((EXTRA, chunk_w), jnp.bfloat16).at[0, 0:3].set(meta)
    sends = [jnp.concatenate([q[:, :chunk_w], meta_rows], axis=0)]
    sends += [q[:, c * chunk_w : (c + 1) * chunk_w] for c in range(1, CHUNKS)]
    q1s = [shift_tm(x, -1) for x in sends]

    kv = jnp.stack([k, v])
    kv_l = lax.ppermute(kv, "space", [(i, i + 1) for i in range(tiles - 1)])
    kv_r = lax.ppermute(kv, "space", [(i + 1, i) for i in range(tiles - 1)])

    f1 = flags_for(q1s[0][rows, 0:3], 1)
    p_self = attend(flags_for(meta, 0), q, k, v, kv_l, kv_r, width, 0, 0)
    p1s, q2s = [], []
    for c in range(CHUNKS):
        p1 = attend(f1, q1s[c], k, v, kv_l, kv_r, chunk_w, c * groups_c, 0)
        if c == 0:
            relay, p1 = lax.optimization_barrier((q1s[c], p1))
        else:
            relay, p1, p_self = lax.optimization_barrier((q1s[c], p1, p_self))
        p1s.append(p1)
        q2s.append(shift_tm(relay, -1))

    valid = (seg >= 1).astype(jnp.int32).reshape(1)
    f2 = flags_for(q2s[0][rows, 0:3], 2)
    result = None
    for c in range(CHUNKS):
        base = c * groups_c
        p2 = attend(f2, q2s[c], k, v, kv_l, kv_r, chunk_w, base, 0)
        p2_in = shift_tm(p2, 1)
        pc = merge(valid, p1s[c], p2_in, 0)
        pc_in = shift_tm(pc, 1)
        result = merge(valid, p_self, pc_in, base, final=True, buf=result)
    return result.reshape(1, rows, width)


def solution(mesh):
    placed = (
        P("tm", "space", None),
        P("tm", "space", None),
        P("tm", "space", None),
        P("tm"),
        P("tm", "space", None),
    )
    return jax.shard_map(
        on_device, mesh=mesh, in_specs=placed, out_specs=P("tm", "space", None), check_vma=False
    )
```

profile of v0, /device:TPU:112, one launch (start us, length us, event | category | flops | bytes accessed | tf_op | source)
XLA Modules:
  0.0 156.4 jit_solution(1508773435320938279)
XLA Ops:
  0.0 2.6 %constant_dynamic-update-slice_fusion.1 = bf16[2,256,2560]{2,1,0:T(8,128)(2,1)} fusion(bf16[1,256,2560]{2,1,0:T(8,128)(2,1)} %param.8), kind=kLoop, calls=%fused_computation.10 | loop fusion | bytes 2621440
  3.7 1.9 %collective-permute-start.3 = (bf16[2,256,2560]{2,1,0:T(8,128)(2,1)}, bf16[2,256,2560]{2,1,0:T(8,128)(2,1)S(1)}, u32[]{:S(2)}, u32[]{:S(2)}) collective-permute-start(bf16[2,256,2560]{2,1,0:T(8,128)(2,1)} %constant_dynamic-update-slice_fusion), channel_id=1, source_target_pairs={{1,0},{2,1},{3,2},{4,3},{5,4},{6,5},{7,6},{9,8},{10,9},{11,10},{12... | collective-permute-start | bytes 7864328 | tf_op jit(solution)/shard_map/ppermute | solution.py:225
  5.7 2.4 %collective-permute-start.2 = (bf16[2,256,2560]{2,1,0:T(8,128)(2,1)}, bf16[2,256,2560]{2,1,0:T(8,128)(2,1)}, u32[]{:S(2)}, u32[]{:S(2)}) collective-permute-start(bf16[2,256,2560]{2,1,0:T(8,128)(2,1)} %constant_dynamic-update-slice_fusion), channel_id=1, source_target_pairs={{0,1},{1,2},{2,3},{3,4},{4,5},{5,6},{6,7},{8,9},{9,10},{10,11},{11... | collective-permute-start | bytes 7864328 | tf_op jit(solution)/shard_map/ppermute | solution.py:224
  10.7 4.5 %collective-permute-start.1 = (bf16[272,1280]{1,0:T(8,128)(2,1)}, bf16[272,1280]{1,0:T(8,128)(2,1)S(1)}, u32[]{:S(2)}, u32[]{:S(2)}) collective-permute-start(bf16[272,1280]{1,0:T(8,128)(2,1)} %pad_maximum_fusion), channel_id=1, source_target_pairs={{8,0},{16,8},{24,16},{32,24},{40,32},{48,40},{56,48},{64,56},{72,6... | collective-permute-start | bytes 2088968 | tf_op jit(solution)/shard_map/ppermute | solution.py:191
  15.2 2.7 %collective-permute-start = (bf16[256,1280]{1,0:T(8,128)(2,1)}, bf16[256,1280]{1,0:T(8,128)(2,1)}, u32[]{:S(2)}, u32[]{:S(2)}) collective-permute-start(bf16[256,1280]{1,0:T(8,128)(2,1)} %get-tuple-element.28), channel_id=1, source_target_pairs={{8,0},{16,8},{24,16},{32,24},{40,32},{48,40},{56,48},{64,56},{72,6... | collective-permute-start | bytes 1966088 | tf_op jit(solution)/shard_map/ppermute | solution.py:191
  17.9 13.4 %collective-permute-done.1.q_ref = bf16[272,1280]{1,0:T(8,128)(2,1)S(1)} collective-permute-done((bf16[272,1280]{1,0:T(8,128)(2,1)}, bf16[272,1280]{1,0:T(8,128)(2,1)S(1)}, u32[]{:S(2)}, u32[]{:S(2)}) %collective-permute-start.1) | collective-permute-done | bytes 696352 | tf_op jit(solution)/shard_map/ppermute | solution.py:191
  35.1 3.8 %collective-permute-done.2.kl_ref.vl_ref = bf16[2,256,2560]{2,1,0:T(8,128)(2,1)} collective-permute-done((bf16[2,256,2560]{2,1,0:T(8,128)(2,1)}, bf16[2,256,2560]{2,1,0:T(8,128)(2,1)}, u32[]{:S(2)}, u32[]{:S(2)}) %collective-permute-start.2) | collective-permute-done | bytes 2621472 | tf_op jit(solution)/shard_map/ppermute | solution.py:224
  39.0 7.6 %shard_map.57.a_ref = bf16[272,1280]{1,0:T(8,128)(2,1)} custom-call(s32[3]{0:T(128)} %add_convert_fusion.flags_ref, bf16[272,1280]{1,0:T(8,128)(2,1)} %copy-done.3, bf16[2,256,2560]{2,1,0:T(8,128)(2,1)} %collective-permute-done.2.kl_ref.vl_ref, bf16[256,2560]{1,0:T(8,128)(2,1)} %bitcast.24, bf16[2,256,2560]{2,1,0:T(8,128)(2,1)} %copy-done, ...), custom_call_target="tpu_custom_call" | custom-call | flops 1006632960 | bytes 5242880 | tf_op jit(solution)/shard_map/pallas_call | solution.py:81
  46.5 4.5 %collective-permute-start.4 = (bf16[272,1280]{1,0:T(8,128)(2,1)}, bf16[272,1280]{1,0:T(8,128)(2,1)S(1)}, u32[]{:S(2)}, u32[]{:S(2)}) collective-permute-start(bf16[272,1280]{1,0:T(8,128)(2,1)} %copy-done.3), channel_id=1, source_target_pairs={{8,0},{16,8},{24,16},{32,24},{40,32},{48,40},{56,48},{64,56},{72,6... | collective-permute-start | bytes 2088968 | tf_op jit(solution)/shard_map/ppermute | solution.py:191
  54.1 7.5 %shard_map.55.a_ref = bf16[272,1280]{1,0:T(8,128)(2,1)} custom-call(s32[3]{0:T(128)} %add_convert_fusion.flags_ref, bf16[256,1280]{1,0:T(8,128)(2,1)} %collective-permute-done.q_ref, bf16[2,256,2560]{2,1,0:T(8,128)(2,1)} %collective-permute-done.2.kl_ref.vl_ref, bf16[256,2560]{1,0:T(8,128)(2,1)} %bitcast.25, bf16[2,256,2560]{2,1,0:T(8,128)(2,1)} %copy-done, ...), custom_call_target="tpu_custom_call" | custom-call | flops 1006632960 | bytes 5242880 | tf_op jit(solution)/shard_map/pallas_call | solution.py:81
  61.7 12.1 %shard_map.56.a_ref = bf16[272,2560]{1,0:T(8,128)(2,1)} custom-call(s32[3]{0:T(128)} %add_convert_fusion.1.flags_ref, bf16[256,2560]{1,0:T(8,128)(2,1)} %bitcast.34, bf16[2,256,2560]{2,1,0:T(8,128)(2,1)} %collective-permute-done.2.kl_ref.vl_ref, bf16[256,2560]{1,0:T(8,128)(2,1)} %bitcast.26, bf16[2,256,2560]{2,1,0:T(8,128)(2,1)} %copy-done, ...), custom_call_target="tpu_custom_call" | custom-call | flops 2013265920 | bytes 10485760 | tf_op jit(solution)/shard_map/pallas_call | solution.py:81
  73.8 1.9 %collective-permute-start.5 = (bf16[256,1280]{1,0:T(8,128)(2,1)}, bf16[256,1280]{1,0:T(8,128)(2,1)S(1)}, u32[]{:S(2)}, u32[]{:S(2)}) collective-permute-start(bf16[256,1280]{1,0:T(8,128)(2,1)} %collective-permute-done.q_ref), channel_id=1, source_target_pairs={{8,0},{16,8},{24,16},{32,24},{40,32},{48,40},{56,48},{64,56},{72,6... | collective-permute-start | bytes 1966088 | tf_op jit(solution)/shard_map/ppermute | solution.py:191
  79.0 7.7 %shard_map.60 = bf16[272,1280]{1,0:T(8,128)(2,1)} custom-call(s32[3]{0:T(128)} %add_convert_fusion.2.flags_ref, bf16[272,1280]{1,0:T(8,128)(2,1)} %copy-done.4, bf16[2,256,2560]{2,1,0:T(8,128)(2,1)} %collective-permute-done.2.kl_ref.vl_ref, bf16[256,2560]{1,0:T(8,128)(2,1)} %bitcast.27, bf16[2,256,2560]{2,1,0:T(8,128)(2,1)} %copy-done, ...), custom_call_target="tpu_custom_call" | custom-call | flops 1006632960 | bytes 5242880 | tf_op jit(solution)/shard_map/pallas_call | solution.py:81
  86.7 2.1 %collective-permute-start.8 = (bf16[272,1280]{1,0:T(8,128)(2,1)}, bf16[272,1280]{1,0:T(8,128)(2,1)S(1)}, u32[]{:S(2)}, u32[]{:S(2)}) collective-permute-start(bf16[272,1280]{1,0:T(8,128)(2,1)} %shard_map.60), channel_id=1, source_target_pairs={{0,8},{8,16},{16,24},{24,32},{32,40},{40,48},{48,56},{56,64},{64,7... | collective-permute-start | bytes 2088968 | tf_op jit(solution)/shard_map/ppermute | solution.py:191
  88.8 3.2 %collective-permute-done.5.q_ref = bf16[256,1280]{1,0:T(8,128)(2,1)S(1)} collective-permute-done((bf16[256,1280]{1,0:T(8,128)(2,1)}, bf16[256,1280]{1,0:T(8,128)(2,1)S(1)}, u32[]{:S(2)}, u32[]{:S(2)}) %collective-permute-start.5) | collective-permute-done | bytes 655392 | tf_op jit(solution)/shard_map/ppermute | solution.py:191
  92.9 7.6 %shard_map.58 = bf16[272,1280]{1,0:T(8,128)(2,1)} custom-call(s32[3]{0:T(128)} %add_convert_fusion.2.flags_ref, bf16[256,1280]{1,0:T(8,128)(2,1)} %copy-done.9, bf16[2,256,2560]{2,1,0:T(8,128)(2,1)} %collective-permute-done.2.kl_ref.vl_ref, bf16[256,2560]{1,0:T(8,128)(2,1)} %bitcast.28, bf16[2,256,2560]{2,1,0:T(8,128)(2,1)} %copy-done, ...), custom_call_target="tpu_custom_call" | custom-call | flops 1006632960 | bytes 5242880 | tf_op jit(solution)/shard_map/pallas_call | solution.py:81
  102.4 7.1 %collective-permute-done.8.b_ref = bf16[272,1280]{1,0:T(8,128)(2,1)S(1)} collective-permute-done((bf16[272,1280]{1,0:T(8,128)(2,1)}, bf16[272,1280]{1,0:T(8,128)(2,1)S(1)}, u32[]{:S(2)}, u32[]{:S(2)}) %collective-permute-start.8) | collective-permute-done | bytes 696352 | tf_op jit(solution)/shard_map/ppermute | solution.py:191
  110.4 2.9 %shard_map.61 = bf16[272,1280]{1,0:T(8,128)(2,1)} custom-call(s32[1]{0:T(128)} %bitcast.valid_ref, bf16[272,1280]{1,0:T(8,128)(2,1)} %shard_map.57.a_ref, bf16[272,1280]{1,0:T(8,128)(2,1)} %copy-done.7), custom_call_target="tpu_custom_call" | custom-call | flops 1310720 | bytes 1966080 | tf_op jit(solution)/shard_map/pallas_call | solution.py:171
  115.2 9.2 %collective-permute-done.6.b_ref = bf16[272,1280]{1,0:T(8,128)(2,1)S(1)} collective-permute-done((bf16[272,1280]{1,0:T(8,128)(2,1)}, bf16[272,1280]{1,0:T(8,128)(2,1)S(1)}, u32[]{:S(2)}, u32[]{:S(2)}) %collective-permute-start.6) | collective-permute-done | bytes 696352 | tf_op jit(solution)/shard_map/ppermute | solution.py:191
  125.2 2.9 %shard_map.59 = bf16[272,1280]{1,0:T(8,128)(2,1)} custom-call(s32[1]{0:T(128)} %bitcast.valid_ref, bf16[272,1280]{1,0:T(8,128)(2,1)} %shard_map.55.a_ref, bf16[272,1280]{1,0:T(8,128)(2,1)} %copy-done.8), custom_call_target="tpu_custom_call" | custom-call | flops 1310720 | bytes 1966080 | tf_op jit(solution)/shard_map/pallas_call | solution.py:171
  130.1 9.2 %collective-permute-done.9.b_ref = bf16[272,1280]{1,0:T(8,128)(2,1)S(1)} collective-permute-done((bf16[272,1280]{1,0:T(8,128)(2,1)}, bf16[272,1280]{1,0:T(8,128)(2,1)S(1)}, u32[]{:S(2)}, u32[]{:S(2)}) %collective-permute-start.9) | collective-permute-done | bytes 696352 | tf_op jit(solution)/shard_map/ppermute | solution.py:191
  140.2 2.9 %shard_map.62.rest_0_ = bf16[256,2560]{1,0:T(8,128)(2,1)} custom-call(s32[1]{0:T(128)} %bitcast.valid_ref, bf16[272,2560]{1,0:T(8,128)(2,1)} %shard_map.56.a_ref, bf16[272,1280]{1,0:T(8,128)(2,1)} %copy-done.6), custom_call_target="tpu_custom_call" | custom-call | flops 1310720 | bytes 1966080 | tf_op jit(solution)/shard_map/pallas_call | solution.py:171
  143.1 9.6 %collective-permute-done.7.b_ref = bf16[272,1280]{1,0:T(8,128)(2,1)S(1)} collective-permute-done((bf16[272,1280]{1,0:T(8,128)(2,1)}, bf16[272,1280]{1,0:T(8,128)(2,1)S(1)}, u32[]{:S(2)}, u32[]{:S(2)}) %collective-permute-start.7) | collective-permute-done | bytes 696352 | tf_op jit(solution)/shard_map/ppermute | solution.py:191
  153.5 2.9 %shard_map.63 = bf16[256,2560]{1,0:T(8,128)(2,1)} custom-call(s32[1]{0:T(128)} %bitcast.valid_ref, bf16[272,2560]{1,0:T(8,128)(2,1)} %shard_map.56.a_ref, bf16[272,1280]{1,0:T(8,128)(2,1)} %copy-done.5, bf16[256,2560]{1,0:T(8,128)(2,1)} %shard_map.62.rest_0_), custom_call_target="tpu_custom_call", output_to_operand_aliasing={{}: (3, {})} | custom-call | flops 1310720 | bytes 1966080 | tf_op jit(solution)/shard_map/pallas_call | solution.py:171
  (42 shorter events, 17.6 us)
Async XLA Ops:
  0.0 2.6 %copy-start.1 = (bf16[1,256,2560]{2,1,0:T(8,128)(2,1)S(1)}, bf16[1,256,2560]{2,1,0:T(8,128)(2,1)}, u32[]{:S(2)}) copy-start(bf16[1,256,2560]{2,1,0:T(8,128)(2,1)} %param.9) | copy-start | bytes 3932164
  2.6 6.1 %copy-start.10 = (s32[1,1,2]{2,1,0:T(1,128)S(1)}, s32[1,1,2]{2,1,0:T(1,128)}, u32[]{:S(2)}) copy-start(s32[1,1,2]{2,1,0:T(1,128)} %param.11) | copy-start | bytes 28
  2.6 6.2 %copy-start.2 = (bf16[1,256,2560]{2,1,0:T(8,128)(2,1)S(1)}, bf16[1,256,2560]{2,1,0:T(8,128)(2,1)}, u32[]{:S(2)}) copy-start(bf16[1,256,2560]{2,1,0:T(8,128)(2,1)} %param.7) | copy-start | bytes 3932164
  3.7 31.4 %collective-permute-start.3 = (bf16[2,256,2560]{2,1,0:T(8,128)(2,1)}, bf16[2,256,2560]{2,1,0:T(8,128)(2,1)S(1)}, u32[]{:S(2)}, u32[]{:S(2)}) collective-permute-start(bf16[2,256,2560]{2,1,0:T(8,128)(2,1)} %constant_dynamic-update-slice_fusion), channel_id=1, source_target_pairs={{1,0},{2,1},{3,2},{4,3},{5,4},{6,5},{7,6},{9,8},{10,9},{11,10},{12... | collective-permute-start | bytes 7864328 | tf_op jit(solution)/shard_map/ppermute | solution.py:225
  5.7 33.3 %collective-permute-start.2 = (bf16[2,256,2560]{2,1,0:T(8,128)(2,1)}, bf16[2,256,2560]{2,1,0:T(8,128)(2,1)}, u32[]{:S(2)}, u32[]{:S(2)}) collective-permute-start(bf16[2,256,2560]{2,1,0:T(8,128)(2,1)} %constant_dynamic-update-slice_fusion), channel_id=1, source_target_pairs={{0,1},{1,2},{2,3},{3,4},{4,5},{5,6},{6,7},{8,9},{9,10},{10,11},{11... | collective-permute-start | bytes 7864328 | tf_op jit(solution)/shard_map/ppermute | solution.py:224
  10.7 20.7 %collective-permute-start.1 = (bf16[272,1280]{1,0:T(8,128)(2,1)}, bf16[272,1280]{1,0:T(8,128)(2,1)S(1)}, u32[]{:S(2)}, u32[]{:S(2)}) collective-permute-start(bf16[272,1280]{1,0:T(8,128)(2,1)} %pad_maximum_fusion), channel_id=1, source_target_pairs={{8,0},{16,8},{24,16},{32,24},{40,32},{48,40},{56,48},{64,56},{72,6... | collective-permute-start | bytes 2088968 | tf_op jit(solution)/shard_map/ppermute | solution.py:191
  15.2 39.0 %collective-permute-start = (bf16[256,1280]{1,0:T(8,128)(2,1)}, bf16[256,1280]{1,0:T(8,128)(2,1)}, u32[]{:S(2)}, u32[]{:S(2)}) collective-permute-start(bf16[256,1280]{1,0:T(8,128)(2,1)} %get-tuple-element.28), channel_id=1, source_target_pairs={{8,0},{16,8},{24,16},{32,24},{40,32},{48,40},{56,48},{64,56},{72,6... | collective-permute-start | bytes 1966088 | tf_op jit(solution)/shard_map/ppermute | solution.py:191
  31.3 7.6 %copy-start.3 = (bf16[272,1280]{1,0:T(8,128)(2,1)}, bf16[272,1280]{1,0:T(8,128)(2,1)S(1)}, u32[]{:S(2)}) copy-start(bf16[272,1280]{1,0:T(8,128)(2,1)S(1)} %collective-permute-done.1.q_ref) | copy-start | bytes 2088964
  35.1 3.8 %copy-start = (bf16[2,256,2560]{2,1,0:T(8,128)(2,1)}, bf16[2,256,2560]{2,1,0:T(8,128)(2,1)S(1)}, u32[]{:S(2)}) copy-start(bf16[2,256,2560]{2,1,0:T(8,128)(2,1)S(1)} %collective-permute-done.3.kr_ref.vr_ref) | copy-start | bytes 7864324
  46.5 29.2 %collective-permute-start.4 = (bf16[272,1280]{1,0:T(8,128)(2,1)}, bf16[272,1280]{1,0:T(8,128)(2,1)S(1)}, u32[]{:S(2)}, u32[]{:S(2)}) collective-permute-start(bf16[272,1280]{1,0:T(8,128)(2,1)} %copy-done.3), channel_id=1, source_target_pairs={{8,0},{16,8},{24,16},{32,24},{40,32},{48,40},{56,48},{64,56},{72,6... | collective-permute-start | bytes 2088968 | tf_op jit(solution)/shard_map/ppermute | solution.py:191
  73.8 18.2 %collective-permute-start.5 = (bf16[256,1280]{1,0:T(8,128)(2,1)}, bf16[256,1280]{1,0:T(8,128)(2,1)S(1)}, u32[]{:S(2)}, u32[]{:S(2)}) collective-permute-start(bf16[256,1280]{1,0:T(8,128)(2,1)} %collective-permute-done.q_ref), channel_id=1, source_target_pairs={{8,0},{16,8},{24,16},{32,24},{40,32},{48,40},{56,48},{64,56},{72,6... | collective-permute-start | bytes 1966088 | tf_op jit(solution)/shard_map/ppermute | solution.py:191
  75.7 3.3 %copy-start.4 = (bf16[272,1280]{1,0:T(8,128)(2,1)}, bf16[272,1280]{1,0:T(8,128)(2,1)S(1)}, u32[]{:S(2)}) copy-start(bf16[272,1280]{1,0:T(8,128)(2,1)S(1)} %collective-permute-done.4.q_ref) | copy-start | bytes 2088964
  86.7 22.7 %collective-permute-start.8 = (bf16[272,1280]{1,0:T(8,128)(2,1)}, bf16[272,1280]{1,0:T(8,128)(2,1)S(1)}, u32[]{:S(2)}, u32[]{:S(2)}) collective-permute-start(bf16[272,1280]{1,0:T(8,128)(2,1)} %shard_map.60), channel_id=1, source_target_pairs={{0,8},{8,16},{16,24},{24,32},{32,40},{40,48},{48,56},{56,64},{64,7... | collective-permute-start | bytes 2088968 | tf_op jit(solution)/shard_map/ppermute | solution.py:191
  92.0 0.9 copy-start.9
  100.4 23.9 %collective-permute-start.6 = (bf16[272,1280]{1,0:T(8,128)(2,1)}, bf16[272,1280]{1,0:T(8,128)(2,1)S(1)}, u32[]{:S(2)}, u32[]{:S(2)}) collective-permute-start(bf16[272,1280]{1,0:T(8,128)(2,1)} %shard_map.58), channel_id=1, source_target_pairs={{0,8},{8,16},{16,24},{24,32},{32,40},{40,48},{48,56},{56,64},{64,7... | collective-permute-start | bytes 2088968 | tf_op jit(solution)/shard_map/ppermute | solution.py:191
  109.5 0.9 copy-start.7
  113.3 26.0 %collective-permute-start.9 = (bf16[272,1280]{1,0:T(8,128)(2,1)}, bf16[272,1280]{1,0:T(8,128)(2,1)S(1)}, u32[]{:S(2)}, u32[]{:S(2)}) collective-permute-start(bf16[272,1280]{1,0:T(8,128)(2,1)} %shard_map.61), channel_id=1, source_target_pairs={{0,8},{8,16},{16,24},{24,32},{32,40},{40,48},{48,56},{56,64},{64,7... | collective-permute-start | bytes 2088968 | tf_op jit(solution)/shard_map/ppermute | solution.py:191
  124.4 0.8 copy-start.8
  128.2 24.5 %collective-permute-start.7 = (bf16[272,1280]{1,0:T(8,128)(2,1)}, bf16[272,1280]{1,0:T(8,128)(2,1)S(1)}, u32[]{:S(2)}, u32[]{:S(2)}) collective-permute-start(bf16[272,1280]{1,0:T(8,128)(2,1)} %shard_map.59), channel_id=1, source_target_pairs={{0,8},{8,16},{16,24},{24,32},{32,40},{40,48},{48,56},{56,64},{64,7... | collective-permute-start | bytes 2088968 | tf_op jit(solution)/shard_map/ppermute | solution.py:191
  139.3 0.9 copy-start.6
  152.7 0.9 copy-start.5
where the time goes:
time: 157 us; the launch traced here: 156 us
  waiting for transfers between devices  56.1 us (36%)
  Pallas kernels  54.2 us (35%)
  starting transfers between devices  25.8 us (16%)
  local copies, waits for them, and re-layouts  11.1 us (7%)
  between operations  6.52 us (4%)
  other arithmetic  2.81 us (2%)
    ppermute x8, waiting for transfers between devices, shift_tm(): return lax.ppermute(x, 'tm', pairs)  51.7 us
    pallas_call x5, Pallas kernels, attend(): pl.pallas_call(_attn_kernel, out_shape=jax.ShapeDtypeStruct((rows + EXTRA...  42.5 us
    ppermute x8, starting transfers between devices, shift_tm(): return lax.ppermute(x, 'tm', pairs)  21.4 us
    pallas_call x4, Pallas kernels, merge(): pl.pallas_call(kernel, out_shape=out_shape, grid_spec=pltpu.PrefetchScala...  11.7 us
    unnamed x23, local copies, waits for them, and re-layouts  6.93 us
    ppermute x1, waiting for transfers between devices, on_device(): kv_l = lax.ppermute(kv, 'space', [(i, i + 1) for i in range(tiles - 1)])  3.82 us
  transfers between devices with their start and end apart: 10, of which 8 were waited for; matrix products, arithmetic and copies ran while one was open for 4% of the time, Pallas kernels for 33%

commit v1 on v0

--- a/solution.py
+++ b/solution.py
@@ -12,7 +12,21 @@
 EXTRA = 16
 
 
-def _attn_kernel(flags_ref, q_ref, kl_ref, kc_ref, kr_ref, vl_ref, vc_ref, vr_ref, o_ref, col_ref):
+def _store_stats(o_ref, st_ref, t, hg, rows):
+    hi = t[0 : 2 * hg].astype(jnp.bfloat16).astype(jnp.float32)
+    st_ref[...] = jnp.zeros_like(st_ref)
+    st_ref[0 : 2 * hg, 0:rows] = hi
+    st_ref[0 : 2 * hg, rows : 2 * rows] = t[0 : 2 * hg] - hi
+    o_ref[rows : rows + EXTRA, :] = st_ref[...].astype(o_ref.dtype)
+
+
+def _load_stats(ref, hg, rows):
+    block = ref[rows : rows + EXTRA, :].astype(jnp.float32)
+    full = block[0 : 2 * hg, 0:rows] + block[0 : 2 * hg, rows : 2 * rows]
+    return full[0:hg], full[hg : 2 * hg]
+
+
+def _attn_kernel(flags_ref, q_ref, kl_ref, kc_ref, kr_ref, vl_ref, vc_ref, vr_ref, o_ref, col_ref, st_ref):
     hg = q_ref.shape[1] // HEAD_DIM
     rows = q_ref.shape[0]
     lanes = o_ref.shape[1]
@@ -43,7 +57,7 @@
                 jnp.maximum(s_l.max(axis=1, keepdims=True), s_c.max(axis=1, keepdims=True)),
                 s_r.max(axis=1, keepdims=True),
             )
-            shift = top.astype(jnp.bfloat16).astype(jnp.float32)
+            shift = top
             p_l = jnp.exp(s_l - shift)
             p_c = jnp.exp(s_c - shift)
             p_r = jnp.exp(s_r - shift)
@@ -54,18 +68,15 @@
             acc += jnp.dot(p_c.astype(jnp.bfloat16), vc_ref[:, cols], preferred_element_type=jnp.float32)
             acc += jnp.dot(p_r.astype(jnp.bfloat16), vr_ref[:, cols], preferred_element_type=jnp.float32)
             o_ref[0:rows, cols] = (acc / denom).astype(o_ref.dtype)
-            den_hi = denom.astype(jnp.bfloat16).astype(jnp.float32)
             col_ref[:, h : h + 1] = shift
-            col_ref[:, hg + h : hg + h + 1] = den_hi
-            col_ref[:, 2 * hg + h : 2 * hg + h + 1] = denom - den_hi
-        stats = jnp.transpose(col_ref[...])[0:EXTRA, :]
-        o_ref[rows : rows + EXTRA, 0:rows] = stats.astype(o_ref.dtype)
-        o_ref[rows : rows + EXTRA, rows:lanes] = jnp.zeros((EXTRA, lanes - rows), o_ref.dtype)
+            col_ref[:, hg + h : hg + h + 1] = denom
+        _store_stats(o_ref, st_ref, jnp.transpose(col_ref[...]), hg, rows)
 
     @pl.when(jnp.logical_not(seg_ok))
     def _():
         row = lax.broadcasted_iota(jnp.int32, o_ref.shape, 0)
-        empty = (row >= rows) & (row < rows + hg)
+        lane = lax.broadcasted_iota(jnp.int32, o_ref.shape, 1)
+        empty = (row >= rows) & (row < rows + hg) & (lane < rows)
         o_ref[...] = jnp.where(empty, NEG, 0.0).astype(o_ref.dtype)
 
 
@@ -86,7 +97,7 @@
             grid=(groups,),
             in_specs=[q_spec, side_k, kv_spec, side_k, side_v, kv_spec, side_v],
             out_specs=pl.BlockSpec((rows + EXTRA, lanes), lambda g, f: (0, g)),
-            scratch_shapes=[pltpu.VMEM((rows, 128), jnp.float32)],
+            scratch_shapes=[pltpu.VMEM((rows, 128), jnp.float32), pltpu.VMEM((EXTRA, lanes), jnp.float32)],
         ),
         cost_estimate=pl.CostEstimate(
             flops=4 * rows * 3 * rows * HEAD_DIM * heads,
@@ -99,13 +110,9 @@
 def _merge_weights(valid_ref, a_ref, b_ref, wt_ref):
     rows = wt_ref.shape[1]
     hg = a_ref.shape[1] // HEAD_DIM
-    def stats(ref):
-        block = ref[rows : rows + EXTRA, 0:rows].astype(jnp.float32)
-        return block[0:hg], block[hg : 2 * hg] + block[2 * hg : 3 * hg]
-
-    a_top, a_den = stats(a_ref)
+    a_top, a_den = _load_stats(a_ref, hg, rows)
     ok = valid_ref[0] == 1
-    b_top, b_den = stats(b_ref)
+    b_top, b_den = _load_stats(b_ref, hg, rows)
     b_top = jnp.where(ok, b_top, NEG)
     b_den = jnp.where(ok, b_den, 0.0)
     top = jnp.maximum(a_top, b_top)
@@ -126,17 +133,14 @@
         o_ref[0:rows, cols] = o.astype(o_ref.dtype)
 
 
-def _merge_kernel(valid_ref, a_ref, b_ref, o_ref, wt_ref):
+def _merge_kernel(valid_ref, a_ref, b_ref, o_ref, wt_ref, st_ref):
     rows = wt_ref.shape[1]
-    lanes = o_ref.shape[1]
-    hg = lanes // HEAD_DIM
+    hg = o_ref.shape[1] // HEAD_DIM
     top, total, w = _merge_weights(valid_ref, a_ref, b_ref, wt_ref)
     _merge_body(a_ref, b_ref, o_ref, w, hg, rows)
-    hi = total.astype(jnp.bfloat16).astype(jnp.float32)
-    pad = jnp.zeros((EXTRA - 3 * hg, rows), jnp.float32)
-    block = jnp.concatenate([top, hi, total - hi, pad], axis=0)
-    o_ref[rows : rows + EXTRA, 0:rows] = block.astype(o_ref.dtype)
-    o_ref[rows : rows + EXTRA, rows:lanes] = jnp.zeros((EXTRA, lanes - rows), o_ref.dtype)
+    wt_ref[0:hg, :] = top
+    wt_ref[hg : 2 * hg, :] = total
+    _store_stats(o_ref, st_ref, wt_ref[...], hg, rows)
 
 
 def _final_kernel(valid_ref, a_ref, b_ref, *rest):
@@ -176,7 +180,8 @@
             grid=(groups,),
             in_specs=in_specs,
             out_specs=out_spec,
-            scratch_shapes=[pltpu.VMEM((128, rows), jnp.float32)],
+            scratch_shapes=[pltpu.VMEM((128, rows), jnp.float32)]
+            + ([] if final else [pltpu.VMEM((EXTRA, lanes), jnp.float32)]),
         ),
         input_output_aliases=aliases,
         cost_estimate=pl.CostEstimate(
@@ -229,10 +234,7 @@
     p1s, q2s = [], []
     for c in range(CHUNKS):
         p1 = attend(f1, q1s[c], k, v, kv_l, kv_r, chunk_w, c * groups_c, 0)
-        if c == 0:
-            relay, p1 = lax.optimization_barrier((q1s[c], p1))
-        else:
-            relay, p1, p_self = lax.optimization_barrier((q1s[c], p1, p_self))
+        relay, p1 = lax.optimization_barrier((q1s[c], p1))
         p1s.append(p1)
         q2s.append(shift_tm(relay, -1))
 
@@ -241,7 +243,10 @@
     result = None
     for c in range(CHUNKS):
         base = c * groups_c
-        p2 = attend(f2, q2s[c], k, v, kv_l, kv_r, chunk_w, base, 0)
+        q2 = q2s[c]
+        if c == 0:
+            q2, p_self = lax.optimization_barrier((q2, p_self))
+        p2 = attend(f2, q2, k, v, kv_l, kv_r, chunk_w, base, 0)
         p2_in = shift_tm(p2, 1)
         pc = merge(valid, p1s[c], p2_in, 0)
         pc_in = shift_tm(pc, 1)

time: 157 us -> 155 us (0.987)
  Pallas kernels: 54.2 us -> 46.5 us
  waiting for transfers between devices: 56.1 us -> 58.9 us
  starting transfers between devices: 25.8 us -> 27.8 us
    pallas_call x5, Pallas kernels: 42.5 us -> 34.8 us  [attend(): pl.pallas_call(_attn_kernel, out_shape=jax.ShapeDtypeStruct((rows + EXTRA...]
    ppermute x8, waiting for transfers between devices: 51.7 us -> 54.6 us  [shift_tm(): return lax.ppermute(x, 'tm', pairs)]
    ppermute x8, starting transfers between devices: 21.4 us -> 23.4 us  [shift_tm(): return lax.ppermute(x, 'tm', pairs)]
  transfers between devices with their start and end apart: 10 -> 10, of which waited for: 8 -> 7; matrix products, arithmetic and copies ran while one was open for 4% -> 4% of each run, Pallas kernels for 33% -> 28%
where the time goes in v1:
time: 155 us; the launch traced here: 154 us
  waiting for transfers between devices  58.9 us (38%)
  Pallas kernels  46.5 us (30%)
  starting transfers between devices  27.8 us (18%)
  local copies, waits for them, and re-layouts  11.1 us (7%)
  between operations  6.52 us (4%)
  other arithmetic  2.81 us (2%)
    ppermute x8, waiting for transfers between devices, shift_tm(): return lax.ppermute(x, 'tm', pairs)  54.6 us
    pallas_call x5, Pallas kernels, attend(): pl.pallas_call(_attn_kernel, out_shape=jax.ShapeDtypeStruct((rows + EXTRA...  34.8 us
    ppermute x8, starting transfers between devices, shift_tm(): return lax.ppermute(x, 'tm', pairs)  23.4 us
    pallas_call x4, Pallas kernels, merge(): pl.pallas_call(kernel, out_shape=out_shape, grid_spec=pltpu.PrefetchScala...  11.7 us
    unnamed x23, local copies, waits for them, and re-layouts  6.92 us
    ppermute x1, waiting for transfers between devices, on_device(): kv_l = lax.ppermute(kv, 'space', [(i, i + 1) for i in range(tiles - 1)])  3.82 us
  transfers between devices with their start and end apart: 10, of which 7 were waited for; matrix products, arithmetic and copies ran while one was open for 4% of the time, Pallas kernels for 28%

profile of v1, /device:TPU:112, one launch (start us, length us, event | category | flops | bytes accessed | tf_op | source)
XLA Modules:
  0.0 153.6 jit_solution(2667838439443902583)
XLA Ops:
  0.0 2.6 %constant_dynamic-update-slice_fusion.1 = bf16[2,256,2560]{2,1,0:T(8,128)(2,1)} fusion(bf16[1,256,2560]{2,1,0:T(8,128)(2,1)} %param.8), kind=kLoop, calls=%fused_computation.10 | loop fusion | bytes 2621440
  3.7 1.9 %collective-permute-start.2 = (bf16[2,256,2560]{2,1,0:T(8,128)(2,1)}, bf16[2,256,2560]{2,1,0:T(8,128)(2,1)S(1)}, u32[]{:S(2)}, u32[]{:S(2)}) collective-permute-start(bf16[2,256,2560]{2,1,0:T(8,128)(2,1)} %constant_dynamic-update-slice_fusion), channel_id=1, source_target_pairs={{1,0},{2,1},{3,2},{4,3},{5,4},{6,5},{7,6},{9,8},{10,9},{11,10},{12... | collective-permute-start | bytes 7864328 | tf_op jit(solution)/shard_map/ppermute | solution.py:230
  5.7 2.4 %collective-permute-start.1 = (bf16[2,256,2560]{2,1,0:T(8,128)(2,1)}, bf16[2,256,2560]{2,1,0:T(8,128)(2,1)}, u32[]{:S(2)}, u32[]{:S(2)}) collective-permute-start(bf16[2,256,2560]{2,1,0:T(8,128)(2,1)} %constant_dynamic-update-slice_fusion), channel_id=1, source_target_pairs={{0,1},{1,2},{2,3},{3,4},{4,5},{5,6},{6,7},{8,9},{9,10},{10,11},{11... | collective-permute-start | bytes 7864328 | tf_op jit(solution)/shard_map/ppermute | solution.py:229
  10.7 4.5 %collective-permute-start = (bf16[272,1280]{1,0:T(8,128)(2,1)}, bf16[272,1280]{1,0:T(8,128)(2,1)S(1)}, u32[]{:S(2)}, u32[]{:S(2)}) collective-permute-start(bf16[272,1280]{1,0:T(8,128)(2,1)} %pad_maximum_fusion), channel_id=1, source_target_pairs={{8,0},{16,8},{24,16},{32,24},{40,32},{48,40},{56,48},{64,56},{72,6... | collective-permute-start | bytes 2088968 | tf_op jit(solution)/shard_map/ppermute | solution.py:196
  15.2 2.7 %collective-permute-start.4 = (bf16[256,1280]{1,0:T(8,128)(2,1)}, bf16[256,1280]{1,0:T(8,128)(2,1)}, u32[]{:S(2)}, u32[]{:S(2)}) collective-permute-start(bf16[256,1280]{1,0:T(8,128)(2,1)} %get-tuple-element.29), channel_id=1, source_target_pairs={{8,0},{16,8},{24,16},{32,24},{40,32},{48,40},{56,48},{64,56},{72,6... | collective-permute-start | bytes 1966088 | tf_op jit(solution)/shard_map/ppermute | solution.py:196
  17.9 13.4 %collective-permute-done.q_ref = bf16[272,1280]{1,0:T(8,128)(2,1)S(1)} collective-permute-done((bf16[272,1280]{1,0:T(8,128)(2,1)}, bf16[272,1280]{1,0:T(8,128)(2,1)S(1)}, u32[]{:S(2)}, u32[]{:S(2)}) %collective-permute-start) | collective-permute-done | bytes 696352 | tf_op jit(solution)/shard_map/ppermute | solution.py:196
  35.1 3.8 %collective-permute-done.1.kl_ref.vl_ref = bf16[2,256,2560]{2,1,0:T(8,128)(2,1)} collective-permute-done((bf16[2,256,2560]{2,1,0:T(8,128)(2,1)}, bf16[2,256,2560]{2,1,0:T(8,128)(2,1)}, u32[]{:S(2)}, u32[]{:S(2)}) %collective-permute-start.1) | collective-permute-done | bytes 2621472 | tf_op jit(solution)/shard_map/ppermute | solution.py:229
  39.0 7.5 %shard_map.55.a_ref = bf16[272,1280]{1,0:T(8,128)(2,1)} custom-call(s32[3]{0:T(128)} %add_convert_fusion.flags_ref, bf16[272,1280]{1,0:T(8,128)(2,1)} %copy-done.3, bf16[2,256,2560]{2,1,0:T(8,128)(2,1)} %collective-permute-done.1.kl_ref.vl_ref, bf16[256,2560]{1,0:T(8,128)(2,1)} %bitcast.24, bf16[2,256,2560]{2,1,0:T(8,128)(2,1)} %copy-done, ...), custom_call_target="tpu_custom_call" | custom-call | flops 1006632960 | bytes 5242880 | tf_op jit(solution)/shard_map/pallas_call | solution.py:92
  46.5 4.5 %collective-permute-start.3 = (bf16[272,1280]{1,0:T(8,128)(2,1)}, bf16[272,1280]{1,0:T(8,128)(2,1)S(1)}, u32[]{:S(2)}, u32[]{:S(2)}) collective-permute-start(bf16[272,1280]{1,0:T(8,128)(2,1)} %copy-done.3), channel_id=1, source_target_pairs={{8,0},{16,8},{24,16},{32,24},{40,32},{48,40},{56,48},{64,56},{72,6... | collective-permute-start | bytes 2088968 | tf_op jit(solution)/shard_map/ppermute | solution.py:196
  54.1 7.5 %shard_map.57.a_ref = bf16[272,1280]{1,0:T(8,128)(2,1)} custom-call(s32[3]{0:T(128)} %add_convert_fusion.flags_ref, bf16[256,1280]{1,0:T(8,128)(2,1)} %collective-permute-done.4.q_ref, bf16[2,256,2560]{2,1,0:T(8,128)(2,1)} %collective-permute-done.1.kl_ref.vl_ref, bf16[256,2560]{1,0:T(8,128)(2,1)} %bitcast.25, bf16[2,256,2560]{2,1,0:T(8,128)(2,1)} %copy-done, ...), custom_call_target="tpu_custom_call" | custom-call | flops 1006632960 | bytes 5242880 | tf_op jit(solution)/shard_map/pallas_call | solution.py:92
  61.6 2.7 %collective-permute-start.5 = (bf16[256,1280]{1,0:T(8,128)(2,1)}, bf16[256,1280]{1,0:T(8,128)(2,1)S(1)}, u32[]{:S(2)}, u32[]{:S(2)}) collective-permute-start(bf16[256,1280]{1,0:T(8,128)(2,1)} %collective-permute-done.4.q_ref), channel_id=1, source_target_pairs={{8,0},{16,8},{24,16},{32,24},{40,32},{48,40},{56,48},{64,56},{72,6... | collective-permute-start | bytes 1966088 | tf_op jit(solution)/shard_map/ppermute | solution.py:196
  64.3 12.1 %shard_map.56.a_ref = bf16[272,2560]{1,0:T(8,128)(2,1)} custom-call(s32[3]{0:T(128)} %add_convert_fusion.1.flags_ref, bf16[256,2560]{1,0:T(8,128)(2,1)} %bitcast.34, bf16[2,256,2560]{2,1,0:T(8,128)(2,1)} %collective-permute-done.1.kl_ref.vl_ref, bf16[256,2560]{1,0:T(8,128)(2,1)} %bitcast.26, bf16[2,256,2560]{2,1,0:T(8,128)(2,1)} %copy-done, ...), custom_call_target="tpu_custom_call" | custom-call | flops 2013265920 | bytes 10485760 | tf_op jit(solution)/shard_map/pallas_call | solution.py:92
  79.8 3.8 %shard_map.60 = bf16[272,1280]{1,0:T(8,128)(2,1)} custom-call(s32[3]{0:T(128)} %add_convert_fusion.2.flags_ref, bf16[272,1280]{1,0:T(8,128)(2,1)} %copy-done.4, bf16[2,256,2560]{2,1,0:T(8,128)(2,1)} %collective-permute-done.1.kl_ref.vl_ref, bf16[256,2560]{1,0:T(8,128)(2,1)} %bitcast.27, bf16[2,256,2560]{2,1,0:T(8,128)(2,1)} %copy-done, ...), custom_call_target="tpu_custom_call" | custom-call | flops 1006632960 | bytes 5242880 | tf_op jit(solution)/shard_map/pallas_call | solution.py:92
  83.6 3.3 %collective-permute-start.8 = (bf16[272,1280]{1,0:T(8,128)(2,1)}, bf16[272,1280]{1,0:T(8,128)(2,1)S(1)}, u32[]{:S(2)}, u32[]{:S(2)}) collective-permute-start(bf16[272,1280]{1,0:T(8,128)(2,1)} %shard_map.60), channel_id=1, source_target_pairs={{0,8},{8,16},{16,24},{24,32},{32,40},{40,48},{48,56},{56,64},{64,7... | collective-permute-start | bytes 2088968 | tf_op jit(solution)/shard_map/ppermute | solution.py:196
  87.7 3.8 %shard_map.58 = bf16[272,1280]{1,0:T(8,128)(2,1)} custom-call(s32[3]{0:T(128)} %add_convert_fusion.2.flags_ref, bf16[256,1280]{1,0:T(8,128)(2,1)} %copy-done.9, bf16[2,256,2560]{2,1,0:T(8,128)(2,1)} %collective-permute-done.1.kl_ref.vl_ref, bf16[256,2560]{1,0:T(8,128)(2,1)} %bitcast.28, bf16[2,256,2560]{2,1,0:T(8,128)(2,1)} %copy-done, ...), custom_call_target="tpu_custom_call" | custom-call | flops 1006632960 | bytes 5242880 | tf_op jit(solution)/shard_map/pallas_call | solution.py:92
  91.5 1.9 %collective-permute-start.6 = (bf16[272,1280]{1,0:T(8,128)(2,1)}, bf16[272,1280]{1,0:T(8,128)(2,1)S(1)}, u32[]{:S(2)}, u32[]{:S(2)}) collective-permute-start(bf16[272,1280]{1,0:T(8,128)(2,1)} %shard_map.58), channel_id=1, source_target_pairs={{0,8},{8,16},{16,24},{24,32},{32,40},{40,48},{48,56},{56,64},{64,7... | collective-permute-start | bytes 2088968 | tf_op jit(solution)/shard_map/ppermute | solution.py:196
  93.4 13.2 %collective-permute-done.8.b_ref = bf16[272,1280]{1,0:T(8,128)(2,1)S(1)} collective-permute-done((bf16[272,1280]{1,0:T(8,128)(2,1)}, bf16[272,1280]{1,0:T(8,128)(2,1)S(1)}, u32[]{:S(2)}, u32[]{:S(2)}) %collective-permute-start.8) | collective-permute-done | bytes 696352 | tf_op jit(solution)/shard_map/ppermute | solution.py:196
  107.5 2.9 %shard_map.61 = bf16[272,1280]{1,0:T(8,128)(2,1)} custom-call(s32[1]{0:T(128)} %bitcast.valid_ref, bf16[272,1280]{1,0:T(8,128)(2,1)} %shard_map.55.a_ref, bf16[272,1280]{1,0:T(8,128)(2,1)} %copy-done.7), custom_call_target="tpu_custom_call" | custom-call | flops 1310720 | bytes 1966080 | tf_op jit(solution)/shard_map/pallas_call | solution.py:175
  112.3 9.2 %collective-permute-done.6.b_ref = bf16[272,1280]{1,0:T(8,128)(2,1)S(1)} collective-permute-done((bf16[272,1280]{1,0:T(8,128)(2,1)}, bf16[272,1280]{1,0:T(8,128)(2,1)S(1)}, u32[]{:S(2)}, u32[]{:S(2)}) %collective-permute-start.6) | collective-permute-done | bytes 696352 | tf_op jit(solution)/shard_map/ppermute | solution.py:196
  122.4 3.0 %shard_map.59 = bf16[272,1280]{1,0:T(8,128)(2,1)} custom-call(s32[1]{0:T(128)} %bitcast.valid_ref, bf16[272,1280]{1,0:T(8,128)(2,1)} %shard_map.57.a_ref, bf16[272,1280]{1,0:T(8,128)(2,1)} %copy-done.8), custom_call_target="tpu_custom_call" | custom-call | flops 1310720 | bytes 1966080 | tf_op jit(solution)/shard_map/pallas_call | solution.py:175
  127.2 9.2 %collective-permute-done.9.b_ref = bf16[272,1280]{1,0:T(8,128)(2,1)S(1)} collective-permute-done((bf16[272,1280]{1,0:T(8,128)(2,1)}, bf16[272,1280]{1,0:T(8,128)(2,1)S(1)}, u32[]{:S(2)}, u32[]{:S(2)}) %collective-permute-start.9) | collective-permute-done | bytes 696352 | tf_op jit(solution)/shard_map/ppermute | solution.py:196
  137.3 2.9 %shard_map.62.rest_0_ = bf16[256,2560]{1,0:T(8,128)(2,1)} custom-call(s32[1]{0:T(128)} %bitcast.valid_ref, bf16[272,2560]{1,0:T(8,128)(2,1)} %shard_map.56.a_ref, bf16[272,1280]{1,0:T(8,128)(2,1)} %copy-done.6), custom_call_target="tpu_custom_call" | custom-call | flops 1310720 | bytes 1966080 | tf_op jit(solution)/shard_map/pallas_call | solution.py:175
  140.2 9.6 %collective-permute-done.7.b_ref = bf16[272,1280]{1,0:T(8,128)(2,1)S(1)} collective-permute-done((bf16[272,1280]{1,0:T(8,128)(2,1)}, bf16[272,1280]{1,0:T(8,128)(2,1)S(1)}, u32[]{:S(2)}, u32[]{:S(2)}) %collective-permute-start.7) | collective-permute-done | bytes 696352 | tf_op jit(solution)/shard_map/ppermute | solution.py:196
  150.7 2.9 %shard_map.63 = bf16[256,2560]{1,0:T(8,128)(2,1)} custom-call(s32[1]{0:T(128)} %bitcast.valid_ref, bf16[272,2560]{1,0:T(8,128)(2,1)} %shard_map.56.a_ref, bf16[272,1280]{1,0:T(8,128)(2,1)} %copy-done.5, bf16[256,2560]{1,0:T(8,128)(2,1)} %shard_map.62.rest_0_), custom_call_target="tpu_custom_call", output_to_operand_aliasing={{}: (3, {})} | custom-call | flops 1310720 | bytes 1966080 | tf_op jit(solution)/shard_map/pallas_call | solution.py:175
  (42 shorter events, 15.6 us)
Async XLA Ops:
  0.0 2.6 %copy-start.1 = (bf16[1,256,2560]{2,1,0:T(8,128)(2,1)S(1)}, bf16[1,256,2560]{2,1,0:T(8,128)(2,1)}, u32[]{:S(2)}) copy-start(bf16[1,256,2560]{2,1,0:T(8,128)(2,1)} %param.9) | copy-start | bytes 3932164
  2.6 6.1 %copy-start.10 = (s32[1,1,2]{2,1,0:T(1,128)S(1)}, s32[1,1,2]{2,1,0:T(1,128)}, u32[]{:S(2)}) copy-start(s32[1,1,2]{2,1,0:T(1,128)} %param.11) | copy-start | bytes 28
  2.6 6.2 %copy-start.2 = (bf16[1,256,2560]{2,1,0:T(8,128)(2,1)S(1)}, bf16[1,256,2560]{2,1,0:T(8,128)(2,1)}, u32[]{:S(2)}) copy-start(bf16[1,256,2560]{2,1,0:T(8,128)(2,1)} %param.7) | copy-start | bytes 3932164
  3.7 31.4 %collective-permute-start.2 = (bf16[2,256,2560]{2,1,0:T(8,128)(2,1)}, bf16[2,256,2560]{2,1,0:T(8,128)(2,1)S(1)}, u32[]{:S(2)}, u32[]{:S(2)}) collective-permute-start(bf16[2,256,2560]{2,1,0:T(8,128)(2,1)} %constant_dynamic-update-slice_fusion), channel_id=1, source_target_pairs={{1,0},{2,1},{3,2},{4,3},{5,4},{6,5},{7,6},{9,8},{10,9},{11,10},{12... | collective-permute-start | bytes 7864328 | tf_op jit(solution)/shard_map/ppermute | solution.py:230
  5.7 33.3 %collective-permute-start.1 = (bf16[2,256,2560]{2,1,0:T(8,128)(2,1)}, bf16[2,256,2560]{2,1,0:T(8,128)(2,1)}, u32[]{:S(2)}, u32[]{:S(2)}) collective-permute-start(bf16[2,256,2560]{2,1,0:T(8,128)(2,1)} %constant_dynamic-update-slice_fusion), channel_id=1, source_target_pairs={{0,1},{1,2},{2,3},{3,4},{4,5},{5,6},{6,7},{8,9},{9,10},{10,11},{11... | collective-permute-start | bytes 7864328 | tf_op jit(solution)/shard_map/ppermute | solution.py:229
  10.7 20.7 %collective-permute-start = (bf16[272,1280]{1,0:T(8,128)(2,1)}, bf16[272,1280]{1,0:T(8,128)(2,1)S(1)}, u32[]{:S(2)}, u32[]{:S(2)}) collective-permute-start(bf16[272,1280]{1,0:T(8,128)(2,1)} %pad_maximum_fusion), channel_id=1, source_target_pairs={{8,0},{16,8},{24,16},{32,24},{40,32},{48,40},{56,48},{64,56},{72,6... | collective-permute-start | bytes 2088968 | tf_op jit(solution)/shard_map/ppermute | solution.py:196
  15.2 38.9 %collective-permute-start.4 = (bf16[256,1280]{1,0:T(8,128)(2,1)}, bf16[256,1280]{1,0:T(8,128)(2,1)}, u32[]{:S(2)}, u32[]{:S(2)}) collective-permute-start(bf16[256,1280]{1,0:T(8,128)(2,1)} %get-tuple-element.29), channel_id=1, source_target_pairs={{8,0},{16,8},{24,16},{32,24},{40,32},{48,40},{56,48},{64,56},{72,6... | collective-permute-start | bytes 1966088 | tf_op jit(solution)/shard_map/ppermute | solution.py:196
  31.3 7.6 %copy-start.3 = (bf16[272,1280]{1,0:T(8,128)(2,1)}, bf16[272,1280]{1,0:T(8,128)(2,1)S(1)}, u32[]{:S(2)}) copy-start(bf16[272,1280]{1,0:T(8,128)(2,1)S(1)} %collective-permute-done.q_ref) | copy-start | bytes 2088964
  35.1 3.8 %copy-start = (bf16[2,256,2560]{2,1,0:T(8,128)(2,1)}, bf16[2,256,2560]{2,1,0:T(8,128)(2,1)S(1)}, u32[]{:S(2)}) copy-start(bf16[2,256,2560]{2,1,0:T(8,128)(2,1)S(1)} %collective-permute-done.2.kr_ref.vr_ref) | copy-start | bytes 7864324
  46.5 30.0 %collective-permute-start.3 = (bf16[272,1280]{1,0:T(8,128)(2,1)}, bf16[272,1280]{1,0:T(8,128)(2,1)S(1)}, u32[]{:S(2)}, u32[]{:S(2)}) collective-permute-start(bf16[272,1280]{1,0:T(8,128)(2,1)} %copy-done.3), channel_id=1, source_target_pairs={{8,0},{16,8},{24,16},{32,24},{40,32},{48,40},{56,48},{64,56},{72,6... | collective-permute-start | bytes 2088968 | tf_op jit(solution)/shard_map/ppermute | solution.py:196
  61.6 25.2 %collective-permute-start.5 = (bf16[256,1280]{1,0:T(8,128)(2,1)}, bf16[256,1280]{1,0:T(8,128)(2,1)S(1)}, u32[]{:S(2)}, u32[]{:S(2)}) collective-permute-start(bf16[256,1280]{1,0:T(8,128)(2,1)} %collective-permute-done.4.q_ref), channel_id=1, source_target_pairs={{8,0},{16,8},{24,16},{32,24},{40,32},{48,40},{56,48},{64,56},{72,6... | collective-permute-start | bytes 1966088 | tf_op jit(solution)/shard_map/ppermute | solution.py:196
  76.5 3.3 %copy-start.4 = (bf16[272,1280]{1,0:T(8,128)(2,1)}, bf16[272,1280]{1,0:T(8,128)(2,1)S(1)}, u32[]{:S(2)}) copy-start(bf16[272,1280]{1,0:T(8,128)(2,1)S(1)} %collective-permute-done.3.q_ref) | copy-start | bytes 2088964
  83.6 23.0 %collective-permute-start.8 = (bf16[272,1280]{1,0:T(8,128)(2,1)}, bf16[272,1280]{1,0:T(8,128)(2,1)S(1)}, u32[]{:S(2)}, u32[]{:S(2)}) collective-permute-start(bf16[272,1280]{1,0:T(8,128)(2,1)} %shard_map.60), channel_id=1, source_target_pairs={{0,8},{8,16},{16,24},{24,32},{32,40},{40,48},{48,56},{56,64},{64,7... | collective-permute-start | bytes 2088968 | tf_op jit(solution)/shard_map/ppermute | solution.py:196
  86.9 0.9 copy-start.9
  91.5 30.0 %collective-permute-start.6 = (bf16[272,1280]{1,0:T(8,128)(2,1)}, bf16[272,1280]{1,0:T(8,128)(2,1)S(1)}, u32[]{:S(2)}, u32[]{:S(2)}) collective-permute-start(bf16[272,1280]{1,0:T(8,128)(2,1)} %shard_map.58), channel_id=1, source_target_pairs={{0,8},{8,16},{16,24},{24,32},{32,40},{40,48},{48,56},{56,64},{64,7... | collective-permute-start | bytes 2088968 | tf_op jit(solution)/shard_map/ppermute | solution.py:196
  106.6 0.9 copy-start.7
  110.4 26.0 %collective-permute-start.9 = (bf16[272,1280]{1,0:T(8,128)(2,1)}, bf16[272,1280]{1,0:T(8,128)(2,1)S(1)}, u32[]{:S(2)}, u32[]{:S(2)}) collective-permute-start(bf16[272,1280]{1,0:T(8,128)(2,1)} %shard_map.61), channel_id=1, source_target_pairs={{0,8},{8,16},{16,24},{24,32},{32,40},{40,48},{48,56},{56,64},{64,7... | collective-permute-start | bytes 2088968 | tf_op jit(solution)/shard_map/ppermute | solution.py:196
  121.5 0.8 copy-start.8
  125.3 24.5 %collective-permute-start.7 = (bf16[272,1280]{1,0:T(8,128)(2,1)}, bf16[272,1280]{1,0:T(8,128)(2,1)S(1)}, u32[]{:S(2)}, u32[]{:S(2)}) collective-permute-start(bf16[272,1280]{1,0:T(8,128)(2,1)} %shard_map.59), channel_id=1, source_target_pairs={{0,8},{8,16},{16,24},{24,32},{32,40},{40,48},{48,56},{56,64},{64,7... | collective-permute-start | bytes 2088968 | tf_op jit(solution)/shard_map/ppermute | solution.py:196
  136.4 0.9 copy-start.6
  149.8 0.9 copy-start.5

commit v2 on v1

--- a/solution.py
+++ b/solution.py
@@ -7,7 +7,7 @@
 
 HEAD_DIM = 128
 HG = 5
-CHUNKS = 2
+CHUNKS = 4
 NEG = -1e30
 EXTRA = 16
 

time: 155 us -> 163 us (1.052)
  waiting for transfers between devices: 58.9 us -> 18.4 us
  Pallas kernels: 46.5 us -> 72.8 us
  starting transfers between devices: 27.8 us -> 46 us
  local copies, waits for them, and re-layouts: 11.1 us -> 15.5 us
    ppermute x8 -> x16, waiting for transfers between devices: 54.6 us -> 11.9 us  [shift_tm(): return lax.ppermute(x, 'tm', pairs)]
    pallas_call x5 -> x9, Pallas kernels: 34.8 us -> 54 us  [attend(): pl.pallas_call(_attn_kernel, out_shape=jax.ShapeDtypeStruct((rows + EXTRA...]
    ppermute x8 -> x16, starting transfers between devices: 23.4 us -> 41.7 us  [shift_tm(): return lax.ppermute(x, 'tm', pairs)]
    pallas_call x4 -> x8, Pallas kernels: 11.7 us -> 18.8 us  [merge(): pl.pallas_call(kernel, out_shape=out_shape, grid_spec=pltpu.PrefetchScala...]
    unnamed x23 -> x37, local copies, waits for them, and re-layouts: 6.92 us -> 11.4 us
    ppermute x1, waiting for transfers between devices: 0.52 us -> 2.66 us  [on_device(): kv_r = lax.ppermute(kv, 'space', [(i + 1, i) for i in range(tiles - 1)])]
  transfers between devices with their start and end apart: 10 -> 18, of which waited for: 7 -> 6; matrix products, arithmetic and copies ran while one was open for 4% -> 3% of each run, Pallas kernels for 28% -> 44%
where the time goes in v2:
time: 163 us; the launch traced here: 161 us
  Pallas kernels  72.8 us (45%)
  starting transfers between devices  46 us (28%)
  waiting for transfers between devices  18.4 us (11%)
  local copies, waits for them, and re-layouts  15.5 us (10%)
  between operations  6.64 us (4%)
  other arithmetic  2.03 us (1%)
    pallas_call x9, Pallas kernels, attend(): pl.pallas_call(_attn_kernel, out_shape=jax.ShapeDtypeStruct((rows + EXTRA...  54 us
    ppermute x16, starting transfers between devices, shift_tm(): return lax.ppermute(x, 'tm', pairs)  41.7 us
    pallas_call x8, Pallas kernels, merge(): pl.pallas_call(kernel, out_shape=out_shape, grid_spec=pltpu.PrefetchScala...  18.8 us
    ppermute x16, waiting for transfers between devices, shift_tm(): return lax.ppermute(x, 'tm', pairs)  11.9 us
    unnamed x37, local copies, waits for them, and re-layouts  11.4 us
    ppermute x1, waiting for transfers between devices, on_device(): kv_l = lax.ppermute(kv, 'space', [(i, i + 1) for i in range(tiles - 1)])  3.82 us
  transfers between devices with their start and end apart: 18, of which 6 were waited for; matrix products, arithmetic and copies ran while one was open for 3% of the time, Pallas kernels for 44%

profile of v2, /device:TPU:112, one launch (start us, length us, event | category | flops | bytes accessed | tf_op | source)
XLA Modules:
  0.0 161.4 jit_solution(17489453111512005902)
XLA Ops:
  0.0 2.6 %constant_dynamic-update-slice_fusion.1 = bf16[2,256,2560]{2,1,0:T(8,128)(2,1)} fusion(bf16[1,256,2560]{2,1,0:T(8,128)(2,1)} %param.8), kind=kLoop, calls=%fused_computation.10 | loop fusion | bytes 2621440
  5.7 2.4 %collective-permute-start.1 = (bf16[2,256,2560]{2,1,0:T(8,128)(2,1)}, bf16[2,256,2560]{2,1,0:T(8,128)(2,1)}, u32[]{:S(2)}, u32[]{:S(2)}) collective-permute-start(bf16[2,256,2560]{2,1,0:T(8,128)(2,1)} %constant_dynamic-update-slice_fusion), channel_id=1, source_target_pairs={{0,1},{1,2},{2,3},{3,4},{4,5},{5,6},{6,7},{8,9},{9,10},{10,11},{11... | collective-permute-start | bytes 7864328 | tf_op jit(solution)/shard_map/ppermute | solution.py:229
  9.9 4.5 %collective-permute-start = (bf16[272,640]{1,0:T(8,128)(2,1)S(1)}, bf16[272,640]{1,0:T(8,128)(2,1)S(1)}, u32[]{:S(2)}, u32[]{:S(2)}) collective-permute-start(bf16[272,640]{1,0:T(8,128)(2,1)S(1)} %pad_maximum_fusion), channel_id=1, source_target_pairs={{8,0},{16,8},{24,16},{32,24},{40,32},{48,40},{56,48},{64,56},{72,6... | collective-permute-start | bytes 1044488 | tf_op jit(solution)/shard_map/ppermute | solution.py:196
  14.4 2.7 %collective-permute-start.12 = (bf16[256,640]{1,0:T(8,128)(2,1)}, bf16[256,640]{1,0:T(8,128)(2,1)}, u32[]{:S(2)}, u32[]{:S(2)}) collective-permute-start(bf16[256,640]{1,0:T(8,128)(2,1)} %get-tuple-element.37), channel_id=1, source_target_pairs={{8,0},{16,8},{24,16},{32,24},{40,32},{48,40},{56,48},{64,56},{72,6... | collective-permute-start | bytes 983048 | tf_op jit(solution)/shard_map/ppermute | solution.py:196
  17.1 2.4 %collective-permute-start.8 = (bf16[256,640]{1,0:T(8,128)(2,1)}, bf16[256,640]{1,0:T(8,128)(2,1)}, u32[]{:S(2)}, u32[]{:S(2)}) collective-permute-start(bf16[256,640]{1,0:T(8,128)(2,1)} %get-tuple-element.38), channel_id=1, source_target_pairs={{8,0},{16,8},{24,16},{32,24},{40,32},{48,40},{56,48},{64,56},{72,6... | collective-permute-start | bytes 983048 | tf_op jit(solution)/shard_map/ppermute | solution.py:196
  22.8 6.5 %collective-permute-start.4 = (bf16[256,640]{1,0:T(8,128)(2,1)}, bf16[256,640]{1,0:T(8,128)(2,1)S(1)}, u32[]{:S(2)}, u32[]{:S(2)}) collective-permute-start(bf16[256,640]{1,0:T(8,128)(2,1)} %get-tuple-element.39), channel_id=1, source_target_pairs={{8,0},{16,8},{24,16},{32,24},{40,32},{48,40},{56,48},{64,56},{72,6... | collective-permute-start | bytes 983048 | tf_op jit(solution)/shard_map/ppermute | solution.py:196
  32.5 2.7 %collective-permute-done.2.kr_ref.vr_ref = bf16[2,256,2560]{2,1,0:T(8,128)(2,1)S(1)} collective-permute-done((bf16[2,256,2560]{2,1,0:T(8,128)(2,1)}, bf16[2,256,2560]{2,1,0:T(8,128)(2,1)S(1)}, u32[]{:S(2)}, u32[]{:S(2)}) %collective-permute-start.2) | collective-permute-done | bytes 2621472 | tf_op jit(solution)/shard_map/ppermute | solution.py:230
  35.1 3.8 %collective-permute-done.1.kl_ref.vl_ref = bf16[2,256,2560]{2,1,0:T(8,128)(2,1)} collective-permute-done((bf16[2,256,2560]{2,1,0:T(8,128)(2,1)}, bf16[2,256,2560]{2,1,0:T(8,128)(2,1)}, u32[]{:S(2)}, u32[]{:S(2)}) %collective-permute-start.1) | collective-permute-done | bytes 2621472 | tf_op jit(solution)/shard_map/ppermute | solution.py:229
  39.0 5.2 %shard_map.55.a_ref = bf16[272,640]{1,0:T(8,128)(2,1)} custom-call(s32[3]{0:T(128)} %add_convert_fusion.flags_ref, bf16[272,640]{1,0:T(8,128)(2,1)} %copy-done.11, bf16[2,256,2560]{2,1,0:T(8,128)(2,1)} %collective-permute-done.1.kl_ref.vl_ref, bf16[256,2560]{1,0:T(8,128)(2,1)} %bitcast.24, bf16[2,256,2560]{2,1,0:T(8,128)(2,1)} %copy-done, ...), custom_call_target="tpu_custom_call" | custom-call | flops 503316480 | bytes 2621440 | tf_op jit(solution)/shard_map/pallas_call | solution.py:92
  47.0 5.2 %shard_map.63.a_ref = bf16[272,640]{1,0:T(8,128)(2,1)} custom-call(s32[3]{0:T(128)} %add_convert_fusion.flags_ref, bf16[256,640]{1,0:T(8,128)(2,1)} %collective-permute-done.12.q_ref, bf16[2,256,2560]{2,1,0:T(8,128)(2,1)} %collective-permute-done.1.kl_ref.vl_ref, bf16[256,2560]{1,0:T(8,128)(2,1)} %bitcast.25, bf16[2,256,2560]{2,1,0:T(8,128)(2,1)} %copy-done, ...), custom_call_target="tpu_custom_call" | custom-call | flops 503316480 | bytes 2621440 | tf_op jit(solution)/shard_map/pallas_call | solution.py:92
  52.3 2.7 %collective-permute-start.13 = (bf16[256,640]{1,0:T(8,128)(2,1)}, bf16[256,640]{1,0:T(8,128)(2,1)S(1)}, u32[]{:S(2)}, u32[]{:S(2)}) collective-permute-start(bf16[256,640]{1,0:T(8,128)(2,1)} %collective-permute-done.12.q_ref), channel_id=1, source_target_pairs={{8,0},{16,8},{24,16},{32,24},{40,32},{48,40},{56,48},{64,56},{72,6... | collective-permute-start | bytes 983048 | tf_op jit(solution)/shard_map/ppermute | solution.py:196
  55.0 5.2 %shard_map.60.a_ref = bf16[272,640]{1,0:T(8,128)(2,1)} custom-call(s32[3]{0:T(128)} %add_convert_fusion.flags_ref, bf16[256,640]{1,0:T(8,128)(2,1)} %collective-permute-done.8.q_ref, bf16[2,256,2560]{2,1,0:T(8,128)(2,1)} %collective-permute-done.1.kl_ref.vl_ref, bf16[256,2560]{1,0:T(8,128)(2,1)} %bitcast.26, bf16[2,256,2560]{2,1,0:T(8,128)(2,1)} %copy-done, ...), custom_call_target="tpu_custom_call" | custom-call | flops 503316480 | bytes 2621440 | tf_op jit(solution)/shard_map/pallas_call | solution.py:92
  60.2 2.4 %collective-permute-start.9 = (bf16[256,640]{1,0:T(8,128)(2,1)}, bf16[256,640]{1,0:T(8,128)(2,1)S(1)}, u32[]{:S(2)}, u32[]{:S(2)}) collective-permute-start(bf16[256,640]{1,0:T(8,128)(2,1)} %collective-permute-done.8.q_ref), channel_id=1, source_target_pairs={{8,0},{16,8},{24,16},{32,24},{40,32},{48,40},{56,48},{64,56},{72,6... | collective-permute-start | bytes 983048 | tf_op jit(solution)/shard_map/ppermute | solution.py:196
  63.4 5.2 %shard_map.57.a_ref = bf16[272,640]{1,0:T(8,128)(2,1)} custom-call(s32[3]{0:T(128)} %add_convert_fusion.flags_ref, bf16[256,640]{1,0:T(8,128)(2,1)} %copy-done.13, bf16[2,256,2560]{2,1,0:T(8,128)(2,1)} %collective-permute-done.1.kl_ref.vl_ref, bf16[256,2560]{1,0:T(8,128)(2,1)} %bitcast.27, bf16[2,256,2560]{2,1,0:T(8,128)(2,1)} %copy-done, ...), custom_call_target="tpu_custom_call" | custom-call | flops 503316480 | bytes 2621440 | tf_op jit(solution)/shard_map/pallas_call | solution.py:92
  68.6 2.6 %collective-permute-start.5 = (bf16[256,640]{1,0:T(8,128)(2,1)}, bf16[256,640]{1,0:T(8,128)(2,1)S(1)}, u32[]{:S(2)}, u32[]{:S(2)}) collective-permute-start(bf16[256,640]{1,0:T(8,128)(2,1)} %copy-done.13), channel_id=1, source_target_pairs={{8,0},{16,8},{24,16},{32,24},{40,32},{48,40},{56,48},{64,56},{72,6... | collective-permute-start | bytes 983048 | tf_op jit(solution)/shard_map/ppermute | solution.py:196
  71.2 12.1 %shard_map.56.a_ref = bf16[272,2560]{1,0:T(8,128)(2,1)} custom-call(s32[3]{0:T(128)} %add_convert_fusion.1.flags_ref, bf16[256,2560]{1,0:T(8,128)(2,1)} %bitcast.42, bf16[2,256,2560]{2,1,0:T(8,128)(2,1)} %collective-permute-done.1.kl_ref.vl_ref, bf16[256,2560]{1,0:T(8,128)(2,1)} %bitcast.28, bf16[2,256,2560]{2,1,0:T(8,128)(2,1)} %copy-done, ...), custom_call_target="tpu_custom_call" | custom-call | flops 2013265920 | bytes 10485760 | tf_op jit(solution)/shard_map/pallas_call | solution.py:92
  87.3 5.2 %shard_map.61 = bf16[272,640]{1,0:T(8,128)(2,1)} custom-call(s32[3]{0:T(128)} %add_convert_fusion.2.flags_ref, bf16[256,640]{1,0:T(8,128)(2,1)} %copy-done.16, bf16[2,256,2560]{2,1,0:T(8,128)(2,1)} %collective-permute-done.1.kl_ref.vl_ref, bf16[256,2560]{1,0:T(8,128)(2,1)} %bitcast.29, bf16[2,256,2560]{2,1,0:T(8,128)(2,1)} %copy-done, ...), custom_call_target="tpu_custom_call" | custom-call | flops 503316480 | bytes 2621440 | tf_op jit(solution)/shard_map/pallas_call | solution.py:92
  95.3 5.2 %shard_map.64 = bf16[272,640]{1,0:T(8,128)(2,1)} custom-call(s32[3]{0:T(128)} %add_convert_fusion.2.flags_ref, bf16[256,640]{1,0:T(8,128)(2,1)} %copy-done.14, bf16[2,256,2560]{2,1,0:T(8,128)(2,1)} %collective-permute-done.1.kl_ref.vl_ref, bf16[256,2560]{1,0:T(8,128)(2,1)} %bitcast.30, bf16[2,256,2560]{2,1,0:T(8,128)(2,1)} %copy-done, ...), custom_call_target="tpu_custom_call" | custom-call | flops 503316480 | bytes 2621440 | tf_op jit(solution)/shard_map/pallas_call | solution.py:92
  102.4 5.3 %shard_map.66 = bf16[272,640]{1,0:T(8,128)(2,1)} custom-call(s32[3]{0:T(128)} %add_convert_fusion.2.flags_ref, bf16[272,640]{1,0:T(8,128)(2,1)} %copy-done.12, bf16[2,256,2560]{2,1,0:T(8,128)(2,1)} %collective-permute-done.1.kl_ref.vl_ref, bf16[256,2560]{1,0:T(8,128)(2,1)} %bitcast.31, bf16[2,256,2560]{2,1,0:T(8,128)(2,1)} %copy-done, ...), custom_call_target="tpu_custom_call" | custom-call | flops 503316480 | bytes 2621440 | tf_op jit(solution)/shard_map/pallas_call | solution.py:92
  110.3 5.3 %shard_map.58 = bf16[272,640]{1,0:T(8,128)(2,1)} custom-call(s32[3]{0:T(128)} %add_convert_fusion.2.flags_ref, bf16[256,640]{1,0:T(8,128)(2,1)} %copy-done.15, bf16[2,256,2560]{2,1,0:T(8,128)(2,1)} %collective-permute-done.1.kl_ref.vl_ref, bf16[256,2560]{1,0:T(8,128)(2,1)} %bitcast.32, bf16[2,256,2560]{2,1,0:T(8,128)(2,1)} %copy-done, ...), custom_call_target="tpu_custom_call" | custom-call | flops 503316480 | bytes 2621440 | tf_op jit(solution)/shard_map/pallas_call | solution.py:92
  118.3 2.4 %shard_map.65 = bf16[272,640]{1,0:T(8,128)(2,1)} custom-call(s32[1]{0:T(128)} %bitcast.valid_ref, bf16[272,640]{1,0:T(8,128)(2,1)} %shard_map.63.a_ref, bf16[272,640]{1,0:T(8,128)(2,1)} %copy-done.8), custom_call_target="tpu_custom_call" | custom-call | flops 655360 | bytes 983040 | tf_op jit(solution)/shard_map/pallas_call | solution.py:175
  123.5 2.4 %shard_map.67 = bf16[272,640]{1,0:T(8,128)(2,1)} custom-call(s32[1]{0:T(128)} %bitcast.valid_ref, bf16[272,640]{1,0:T(8,128)(2,1)} %shard_map.55.a_ref, bf16[272,640]{1,0:T(8,128)(2,1)} %copy-done.7), custom_call_target="tpu_custom_call" | custom-call | flops 655360 | bytes 983040 | tf_op jit(solution)/shard_map/pallas_call | solution.py:175
  133.6 2.3 %shard_map.59 = bf16[272,640]{1,0:T(8,128)(2,1)} custom-call(s32[1]{0:T(128)} %bitcast.valid_ref, bf16[272,640]{1,0:T(8,128)(2,1)} %shard_map.57.a_ref, bf16[272,640]{1,0:T(8,128)(2,1)} %copy-done.5), custom_call_target="tpu_custom_call" | custom-call | flops 655360 | bytes 983040 | tf_op jit(solution)/shard_map/pallas_call | solution.py:175
  137.8 8.0 %collective-permute-done.17.b_ref = bf16[272,640]{1,0:T(8,128)(2,1)S(1)} collective-permute-done((bf16[272,640]{1,0:T(8,128)(2,1)}, bf16[272,640]{1,0:T(8,128)(2,1)S(1)}, u32[]{:S(2)}, u32[]{:S(2)}) %collective-permute-start.17) | collective-permute-done | bytes 348192 | tf_op jit(solution)/shard_map/ppermute | solution.py:196
  (80 shorter events, 50.3 us)
Async XLA Ops:
  0.0 2.6 %copy-start.1 = (bf16[1,256,2560]{2,1,0:T(8,128)(2,1)S(1)}, bf16[1,256,2560]{2,1,0:T(8,128)(2,1)}, u32[]{:S(2)}) copy-start(bf16[1,256,2560]{2,1,0:T(8,128)(2,1)} %param.9) | copy-start | bytes 3932164
  2.6 6.2 %copy-start.17 = (s32[1,1,2]{2,1,0:T(1,128)S(1)}, s32[1,1,2]{2,1,0:T(1,128)}, u32[]{:S(2)}) copy-start(s32[1,1,2]{2,1,0:T(1,128)} %param.11) | copy-start | bytes 28
  2.6 6.3 %copy-start.2 = (bf16[1,256,2560]{2,1,0:T(8,128)(2,1)S(1)}, bf16[1,256,2560]{2,1,0:T(8,128)(2,1)}, u32[]{:S(2)}) copy-start(bf16[1,256,2560]{2,1,0:T(8,128)(2,1)} %param.7) | copy-start | bytes 3932164
  3.8 31.4 %collective-permute-start.2 = (bf16[2,256,2560]{2,1,0:T(8,128)(2,1)}, bf16[2,256,2560]{2,1,0:T(8,128)(2,1)S(1)}, u32[]{:S(2)}, u32[]{:S(2)}) collective-permute-start(bf16[2,256,2560]{2,1,0:T(8,128)(2,1)} %constant_dynamic-update-slice_fusion), channel_id=1, source_target_pairs={{1,0},{2,1},{3,2},{4,3},{5,4},{6,5},{7,6},{9,8},{10,9},{11,10},{12... | collective-permute-start | bytes 7864328 | tf_op jit(solution)/shard_map/ppermute | solution.py:230
  5.7 33.3 %collective-permute-start.1 = (bf16[2,256,2560]{2,1,0:T(8,128)(2,1)}, bf16[2,256,2560]{2,1,0:T(8,128)(2,1)}, u32[]{:S(2)}, u32[]{:S(2)}) collective-permute-start(bf16[2,256,2560]{2,1,0:T(8,128)(2,1)} %constant_dynamic-update-slice_fusion), channel_id=1, source_target_pairs={{0,1},{1,2},{2,3},{3,4},{4,5},{5,6},{6,7},{8,9},{9,10},{10,11},{11... | collective-permute-start | bytes 7864328 | tf_op jit(solution)/shard_map/ppermute | solution.py:229
  9.9 12.9 %collective-permute-start = (bf16[272,640]{1,0:T(8,128)(2,1)S(1)}, bf16[272,640]{1,0:T(8,128)(2,1)S(1)}, u32[]{:S(2)}, u32[]{:S(2)}) collective-permute-start(bf16[272,640]{1,0:T(8,128)(2,1)S(1)} %pad_maximum_fusion), channel_id=1, source_target_pairs={{8,0},{16,8},{24,16},{32,24},{40,32},{48,40},{56,48},{64,56},{72,6... | collective-permute-start | bytes 1044488 | tf_op jit(solution)/shard_map/ppermute | solution.py:196
  14.4 32.7 %collective-permute-start.12 = (bf16[256,640]{1,0:T(8,128)(2,1)}, bf16[256,640]{1,0:T(8,128)(2,1)}, u32[]{:S(2)}, u32[]{:S(2)}) collective-permute-start(bf16[256,640]{1,0:T(8,128)(2,1)} %get-tuple-element.37), channel_id=1, source_target_pairs={{8,0},{16,8},{24,16},{32,24},{40,32},{48,40},{56,48},{64,56},{72,6... | collective-permute-start | bytes 983048 | tf_op jit(solution)/shard_map/ppermute | solution.py:196
  17.1 37.9 %collective-permute-start.8 = (bf16[256,640]{1,0:T(8,128)(2,1)}, bf16[256,640]{1,0:T(8,128)(2,1)}, u32[]{:S(2)}, u32[]{:S(2)}) collective-permute-start(bf16[256,640]{1,0:T(8,128)(2,1)} %get-tuple-element.38), channel_id=1, source_target_pairs={{8,0},{16,8},{24,16},{32,24},{40,32},{48,40},{56,48},{64,56},{72,6... | collective-permute-start | bytes 983048 | tf_op jit(solution)/shard_map/ppermute | solution.py:196
  22.8 16.2 %copy-start.11 = (bf16[272,640]{1,0:T(8,128)(2,1)}, bf16[272,640]{1,0:T(8,128)(2,1)S(1)}, u32[]{:S(2)}) copy-start(bf16[272,640]{1,0:T(8,128)(2,1)S(1)} %collective-permute-done.q_ref) | copy-start | bytes 1044484
  22.8 39.9 %collective-permute-start.4 = (bf16[256,640]{1,0:T(8,128)(2,1)}, bf16[256,640]{1,0:T(8,128)(2,1)S(1)}, u32[]{:S(2)}, u32[]{:S(2)}) collective-permute-start(bf16[256,640]{1,0:T(8,128)(2,1)} %get-tuple-element.39), channel_id=1, source_target_pairs={{8,0},{16,8},{24,16},{32,24},{40,32},{48,40},{56,48},{64,56},{72,6... | collective-permute-start | bytes 983048 | tf_op jit(solution)/shard_map/ppermute | solution.py:196
  35.1 3.8 %copy-start = (bf16[2,256,2560]{2,1,0:T(8,128)(2,1)}, bf16[2,256,2560]{2,1,0:T(8,128)(2,1)S(1)}, u32[]{:S(2)}) copy-start(bf16[2,256,2560]{2,1,0:T(8,128)(2,1)S(1)} %collective-permute-done.2.kr_ref.vr_ref) | copy-start | bytes 7864324
  44.2 39.2 %collective-permute-start.3 = (bf16[272,640]{1,0:T(8,128)(2,1)}, bf16[272,640]{1,0:T(8,128)(2,1)S(1)}, u32[]{:S(2)}, u32[]{:S(2)}) collective-permute-start(bf16[272,640]{1,0:T(8,128)(2,1)} %copy-done.11), channel_id=1, source_target_pairs={{8,0},{16,8},{24,16},{32,24},{40,32},{48,40},{56,48},{64,56},{72,6... | collective-permute-start | bytes 1044488 | tf_op jit(solution)/shard_map/ppermute | solution.py:196
  52.3 42.2 %collective-permute-start.13 = (bf16[256,640]{1,0:T(8,128)(2,1)}, bf16[256,640]{1,0:T(8,128)(2,1)S(1)}, u32[]{:S(2)}, u32[]{:S(2)}) collective-permute-start(bf16[256,640]{1,0:T(8,128)(2,1)} %collective-permute-done.12.q_ref), channel_id=1, source_target_pairs={{8,0},{16,8},{24,16},{32,24},{40,32},{48,40},{56,48},{64,56},{72,6... | collective-permute-start | bytes 983048 | tf_op jit(solution)/shard_map/ppermute | solution.py:196
  60.2 26.4 %collective-permute-start.9 = (bf16[256,640]{1,0:T(8,128)(2,1)}, bf16[256,640]{1,0:T(8,128)(2,1)S(1)}, u32[]{:S(2)}, u32[]{:S(2)}) collective-permute-start(bf16[256,640]{1,0:T(8,128)(2,1)} %collective-permute-done.8.q_ref), channel_id=1, source_target_pairs={{8,0},{16,8},{24,16},{32,24},{40,32},{48,40},{56,48},{64,56},{72,6... | collective-permute-start | bytes 983048 | tf_op jit(solution)/shard_map/ppermute | solution.py:196
  68.6 41.0 %collective-permute-start.5 = (bf16[256,640]{1,0:T(8,128)(2,1)}, bf16[256,640]{1,0:T(8,128)(2,1)S(1)}, u32[]{:S(2)}, u32[]{:S(2)}) collective-permute-start(bf16[256,640]{1,0:T(8,128)(2,1)} %copy-done.13), channel_id=1, source_target_pairs={{8,0},{16,8},{24,16},{32,24},{40,32},{48,40},{56,48},{64,56},{72,6... | collective-permute-start | bytes 983048 | tf_op jit(solution)/shard_map/ppermute | solution.py:196
  83.4 9.2 %copy-start.12 = (bf16[272,640]{1,0:T(8,128)(2,1)}, bf16[272,640]{1,0:T(8,128)(2,1)S(1)}, u32[]{:S(2)}) copy-start(bf16[272,640]{1,0:T(8,128)(2,1)S(1)} %collective-permute-done.3.q_ref) | copy-start | bytes 1044484
  92.6 35.2 %collective-permute-start.10 = (bf16[272,640]{1,0:T(8,128)(2,1)}, bf16[272,640]{1,0:T(8,128)(2,1)S(1)}, u32[]{:S(2)}, u32[]{:S(2)}) collective-permute-start(bf16[272,640]{1,0:T(8,128)(2,1)} %shard_map.61), channel_id=1, source_target_pairs={{0,8},{8,16},{16,24},{24,32},{32,40},{40,48},{48,56},{56,64},{64,7... | collective-permute-start | bytes 1044488 | tf_op jit(solution)/shard_map/ppermute | solution.py:196
  100.5 17.0 %collective-permute-start.14 = (bf16[272,640]{1,0:T(8,128)(2,1)}, bf16[272,640]{1,0:T(8,128)(2,1)S(1)}, u32[]{:S(2)}, u32[]{:S(2)}) collective-permute-start(bf16[272,640]{1,0:T(8,128)(2,1)} %shard_map.64), channel_id=1, source_target_pairs={{0,8},{8,16},{16,24},{24,32},{32,40},{40,48},{48,56},{56,64},{64,7... | collective-permute-start | bytes 1044488 | tf_op jit(solution)/shard_map/ppermute | solution.py:196
  107.7 15.1 %collective-permute-start.16 = (bf16[272,640]{1,0:T(8,128)(2,1)}, bf16[272,640]{1,0:T(8,128)(2,1)S(1)}, u32[]{:S(2)}, u32[]{:S(2)}) collective-permute-start(bf16[272,640]{1,0:T(8,128)(2,1)} %shard_map.66), channel_id=1, source_target_pairs={{0,8},{8,16},{16,24},{24,32},{32,40},{40,48},{48,56},{56,64},{64,7... | collective-permute-start | bytes 1044488 | tf_op jit(solution)/shard_map/ppermute | solution.py:196
  115.6 17.2 %collective-permute-start.6 = (bf16[272,640]{1,0:T(8,128)(2,1)}, bf16[272,640]{1,0:T(8,128)(2,1)S(1)}, u32[]{:S(2)}, u32[]{:S(2)}) collective-permute-start(bf16[272,640]{1,0:T(8,128)(2,1)} %shard_map.58), channel_id=1, source_target_pairs={{0,8},{8,16},{16,24},{24,32},{32,40},{40,48},{48,56},{56,64},{64,7... | collective-permute-start | bytes 1044488 | tf_op jit(solution)/shard_map/ppermute | solution.py:196
  120.6 28.3 %collective-permute-start.15 = (bf16[272,640]{1,0:T(8,128)(2,1)}, bf16[272,640]{1,0:T(8,128)(2,1)S(1)}, u32[]{:S(2)}, u32[]{:S(2)}) collective-permute-start(bf16[272,640]{1,0:T(8,128)(2,1)} %shard_map.65), channel_id=1, source_target_pairs={{0,8},{8,16},{16,24},{24,32},{32,40},{40,48},{48,56},{56,64},{64,7... | collective-permute-start | bytes 1044488 | tf_op jit(solution)/shard_map/ppermute | solution.py:196
  125.9 19.9 %collective-permute-start.17 = (bf16[272,640]{1,0:T(8,128)(2,1)}, bf16[272,640]{1,0:T(8,128)(2,1)S(1)}, u32[]{:S(2)}, u32[]{:S(2)}) collective-permute-start(bf16[272,640]{1,0:T(8,128)(2,1)} %shard_map.67), channel_id=1, source_target_pairs={{0,8},{8,16},{16,24},{24,32},{32,40},{40,48},{48,56},{56,64},{64,7... | collective-permute-start | bytes 1044488 | tf_op jit(solution)/shard_map/ppermute | solution.py:196
  130.9 22.4 %collective-permute-start.11 = (bf16[272,640]{1,0:T(8,128)(2,1)}, bf16[272,640]{1,0:T(8,128)(2,1)S(1)}, u32[]{:S(2)}, u32[]{:S(2)}) collective-permute-start(bf16[272,640]{1,0:T(8,128)(2,1)} %shard_map.62), channel_id=1, source_target_pairs={{0,8},{8,16},{16,24},{24,32},{32,40},{40,48},{48,56},{56,64},{64,7... | collective-permute-start | bytes 1044488 | tf_op jit(solution)/shard_map/ppermute | solution.py:196
  135.9 22.4 %collective-permute-start.7 = (bf16[272,640]{1,0:T(8,128)(2,1)}, bf16[272,640]{1,0:T(8,128)(2,1)S(1)}, u32[]{:S(2)}, u32[]{:S(2)}) collective-permute-start(bf16[272,640]{1,0:T(8,128)(2,1)} %shard_map.59), channel_id=1, source_target_pairs={{0,8},{8,16},{16,24},{24,32},{32,40},{40,48},{48,56},{56,64},{64,7... | collective-permute-start | bytes 1044488 | tf_op jit(solution)/shard_map/ppermute | solution.py:196
  (12 other events, 8.8 us)

commit v3 on v1

--- a/solution.py
+++ b/solution.py
@@ -150,19 +150,20 @@
     _merge_body(a_ref, b_ref, o_ref, w, o_ref.shape[1] // HEAD_DIM, rows)
 
 
-def merge(valid, a, b, base, final=False, buf=None):
+def merge(valid, a, b, base, final=False, buf=None, out_width=None):
     ext, width = b.shape
     rows = ext - EXTRA
     groups = width // HEAD_DIM // HG
     lanes = HG * HEAD_DIM
-    a_spec = pl.BlockSpec((ext, lanes), lambda g, v: (0, g + base))
+    a_base = 0 if out_width is not None else base
+    a_spec = pl.BlockSpec((ext, lanes), lambda g, v: (0, g + a_base))
     b_spec = pl.BlockSpec((ext, lanes), lambda g, v: (0, g))
     in_specs = [a_spec, b_spec]
     operands = [valid, a, b]
     aliases = {}
     if final:
         kernel = _final_kernel
-        out_shape = jax.ShapeDtypeStruct((rows, a.shape[1]), jnp.bfloat16)
+        out_shape = jax.ShapeDtypeStruct((rows, out_width or a.shape[1]), jnp.bfloat16)
         out_spec = pl.BlockSpec((rows, lanes), lambda g, v: (0, g + base))
         if buf is not None:
             in_specs.append(pl.BlockSpec(memory_space=pl.ANY))
@@ -230,7 +231,6 @@
     kv_r = lax.ppermute(kv, "space", [(i + 1, i) for i in range(tiles - 1)])
 
     f1 = flags_for(q1s[0][rows, 0:3], 1)
-    p_self = attend(flags_for(meta, 0), q, k, v, kv_l, kv_r, width, 0, 0)
     p1s, q2s = [], []
     for c in range(CHUNKS):
         p1 = attend(f1, q1s[c], k, v, kv_l, kv_r, chunk_w, c * groups_c, 0)
@@ -239,18 +239,20 @@
         q2s.append(shift_tm(relay, -1))
 
     valid = (seg >= 1).astype(jnp.int32).reshape(1)
+    f0 = flags_for(meta, 0)
     f2 = flags_for(q2s[0][rows, 0:3], 2)
     result = None
+    q_self = q
     for c in range(CHUNKS):
         base = c * groups_c
-        q2 = q2s[c]
-        if c == 0:
-            q2, p_self = lax.optimization_barrier((q2, p_self))
+        p_self = attend(f0, q_self, k, v, kv_l, kv_r, chunk_w, base, base)
+        q2, p_self = lax.optimization_barrier((q2s[c], p_self))
         p2 = attend(f2, q2, k, v, kv_l, kv_r, chunk_w, base, 0)
+        q_self, p2 = lax.optimization_barrier((q, p2))
         p2_in = shift_tm(p2, 1)
         pc = merge(valid, p1s[c], p2_in, 0)
         pc_in = shift_tm(pc, 1)
-        result = merge(valid, p_self, pc_in, base, final=True, buf=result)
+        result = merge(valid, p_self, pc_in, base, final=True, buf=result, out_width=width)
     return result.reshape(1, rows, width)
 
 

time: 155 us -> 158 us (1.019)
  Pallas kernels: 46.5 us -> 57 us
  waiting for transfers between devices: 58.9 us -> 51.7 us
    pallas_call x5 -> x6, Pallas kernels: 34.8 us -> 45.3 us  [attend(): pl.pallas_call(_attn_kernel, out_shape=jax.ShapeDtypeStruct((rows + EXTRA...]
    ppermute x8, waiting for transfers between devices: 54.6 us -> 48.7 us  [shift_tm(): return lax.ppermute(x, 'tm', pairs)]
    ppermute x1, waiting for transfers between devices: 3.82 us -> 1.14 us  [on_device(): kv_l = lax.ppermute(kv, 'space', [(i, i + 1) for i in range(tiles - 1)])]
    ppermute x1, starting transfers between devices: 1.91 us -> 3.64 us  [on_device(): kv_r = lax.ppermute(kv, 'space', [(i + 1, i) for i in range(tiles - 1)])]
  transfers between devices with their start and end apart: 10 -> 10, of which waited for: 7 -> 7; matrix products, arithmetic and copies ran while one was open for 4% -> 4% of each run, Pallas kernels for 28% -> 35%
where the time goes in v3:
time: 158 us; the launch traced here: 157 us
  Pallas kernels  57 us (36%)
  waiting for transfers between devices  51.7 us (33%)
  starting transfers between devices  27.4 us (17%)
  local copies, waits for them, and re-layouts  11.1 us (7%)
  between operations  6.47 us (4%)
  other arithmetic  2.84 us (2%)
    ppermute x8, waiting for transfers between devices, shift_tm(): return lax.ppermute(x, 'tm', pairs)  48.7 us
    pallas_call x6, Pallas kernels, attend(): pl.pallas_call(_attn_kernel, out_shape=jax.ShapeDtypeStruct((rows + EXTRA...  45.3 us
    ppermute x8, starting transfers between devices, shift_tm(): return lax.ppermute(x, 'tm', pairs)  21.9 us
    pallas_call x4, Pallas kernels, merge(): pl.pallas_call(kernel, out_shape=out_shape, grid_spec=pltpu.PrefetchScala...  11.7 us
    unnamed x23, local copies, waits for them, and re-layouts  6.99 us
    ppermute x1, starting transfers between devices, on_device(): kv_r = lax.ppermute(kv, 'space', [(i + 1, i) for i in range(tiles - 1)])  3.64 us
  transfers between devices with their start and end apart: 10, of which 7 were waited for; matrix products, arithmetic and copies ran while one was open for 4% of the time, Pallas kernels for 35%

profile of v3, /device:TPU:112, one launch (start us, length us, event | category | flops | bytes accessed | tf_op | source)
XLA Modules:
  0.0 156.6 jit_solution(711783977299592170)
XLA Ops:
  0.0 2.6 %constant_dynamic-update-slice_fusion.1 = bf16[2,256,2560]{2,1,0:T(8,128)(2,1)} fusion(bf16[1,256,2560]{2,1,0:T(8,128)(2,1)} %param.8), kind=kLoop, calls=%fused_computation.10 | loop fusion | bytes 2621440
  3.7 1.9 %collective-permute-start.2 = (bf16[2,256,2560]{2,1,0:T(8,128)(2,1)}, bf16[2,256,2560]{2,1,0:T(8,128)(2,1)S(1)}, u32[]{:S(2)}, u32[]{:S(2)}) collective-permute-start(bf16[2,256,2560]{2,1,0:T(8,128)(2,1)} %constant_dynamic-update-slice_fusion), channel_id=1, source_target_pairs={{0,1},{1,2},{2,3},{3,4},{4,5},{5,6},{6,7},{8,9},{9,10},{10,11},{11... | collective-permute-start | bytes 7864328 | tf_op jit(solution)/shard_map/ppermute | solution.py:230
  5.7 3.6 %collective-permute-start.3 = (bf16[2,256,2560]{2,1,0:T(8,128)(2,1)}, bf16[2,256,2560]{2,1,0:T(8,128)(2,1)}, u32[]{:S(2)}, u32[]{:S(2)}) collective-permute-start(bf16[2,256,2560]{2,1,0:T(8,128)(2,1)} %constant_dynamic-update-slice_fusion), channel_id=1, source_target_pairs={{1,0},{2,1},{3,2},{4,3},{5,4},{6,5},{7,6},{9,8},{10,9},{11,10},{12... | collective-permute-start | bytes 7864328 | tf_op jit(solution)/shard_map/ppermute | solution.py:231
  11.9 4.5 %collective-permute-start.1 = (bf16[272,1280]{1,0:T(8,128)(2,1)}, bf16[272,1280]{1,0:T(8,128)(2,1)S(1)}, u32[]{:S(2)}, u32[]{:S(2)}) collective-permute-start(bf16[272,1280]{1,0:T(8,128)(2,1)} %pad_maximum_fusion), channel_id=1, source_target_pairs={{8,0},{16,8},{24,16},{32,24},{40,32},{48,40},{56,48},{64,56},{72,6... | collective-permute-start | bytes 2088968 | tf_op jit(solution)/shard_map/ppermute | solution.py:197
  16.4 2.7 %collective-permute-start = (bf16[256,1280]{1,0:T(8,128)(2,1)}, bf16[256,1280]{1,0:T(8,128)(2,1)}, u32[]{:S(2)}, u32[]{:S(2)}) collective-permute-start(bf16[256,1280]{1,0:T(8,128)(2,1)} %get-tuple-element.40), channel_id=1, source_target_pairs={{8,0},{16,8},{24,16},{32,24},{40,32},{48,40},{56,48},{64,56},{72,6... | collective-permute-start | bytes 1966088 | tf_op jit(solution)/shard_map/ppermute | solution.py:197
  19.1 13.6 %collective-permute-done.1.q_ref = bf16[272,1280]{1,0:T(8,128)(2,1)S(1)} collective-permute-done((bf16[272,1280]{1,0:T(8,128)(2,1)}, bf16[272,1280]{1,0:T(8,128)(2,1)S(1)}, u32[]{:S(2)}, u32[]{:S(2)}) %collective-permute-start.1) | collective-permute-done | bytes 696352 | tf_op jit(solution)/shard_map/ppermute | solution.py:197
  38.8 7.5 %shard_map.56.a_ref = bf16[272,1280]{1,0:T(8,128)(2,1)} custom-call(s32[3]{0:T(128)} %add_convert_fusion.flags_ref, bf16[272,1280]{1,0:T(8,128)(2,1)} %copy-done.3, bf16[2,256,2560]{2,1,0:T(8,128)(2,1)} %copy-done, bf16[256,2560]{1,0:T(8,128)(2,1)} %bitcast.24, bf16[2,256,2560]{2,1,0:T(8,128)(2,1)} %collective-permute-done.3.kr_ref.vr_ref, ...), custom_call_target="tpu_custom_call" | custom-call | flops 1006632960 | bytes 5242880 | tf_op jit(solution)/shard_map/pallas_call | solution.py:92
  46.3 4.9 %collective-permute-start.5 = (bf16[272,1280]{1,0:T(8,128)(2,1)}, bf16[272,1280]{1,0:T(8,128)(2,1)S(1)}, u32[]{:S(2)}, u32[]{:S(2)}) collective-permute-start(bf16[272,1280]{1,0:T(8,128)(2,1)} %copy-done.3), channel_id=1, source_target_pairs={{8,0},{16,8},{24,16},{32,24},{40,32},{48,40},{56,48},{64,56},{72,6... | collective-permute-start | bytes 2088968 | tf_op jit(solution)/shard_map/ppermute | solution.py:197
  54.6 7.5 %shard_map.55.a_ref = bf16[272,1280]{1,0:T(8,128)(2,1)} custom-call(s32[3]{0:T(128)} %add_convert_fusion.flags_ref, bf16[256,1280]{1,0:T(8,128)(2,1)} %collective-permute-done.q_ref, bf16[2,256,2560]{2,1,0:T(8,128)(2,1)} %copy-done, bf16[256,2560]{1,0:T(8,128)(2,1)} %bitcast.25, bf16[2,256,2560]{2,1,0:T(8,128)(2,1)} %collective-permute-done.3.kr_ref.vr_ref, ...), custom_call_target="tpu_custom_call" | custom-call | flops 1006632960 | bytes 5242880 | tf_op jit(solution)/shard_map/pallas_call | solution.py:92
  62.1 1.9 %collective-permute-start.4 = (bf16[256,1280]{1,0:T(8,128)(2,1)}, bf16[256,1280]{1,0:T(8,128)(2,1)S(1)}, u32[]{:S(2)}, u32[]{:S(2)}) collective-permute-start(bf16[256,1280]{1,0:T(8,128)(2,1)} %collective-permute-done.q_ref), channel_id=1, source_target_pairs={{8,0},{16,8},{24,16},{32,24},{40,32},{48,40},{56,48},{64,56},{72,6... | collective-permute-start | bytes 1966088 | tf_op jit(solution)/shard_map/ppermute | solution.py:197
  64.0 7.6 %shard_map.57.a_ref = bf16[272,1280]{1,0:T(8,128)(2,1)} custom-call(s32[3]{0:T(128)} %add_convert_fusion.1.flags_ref, bf16[256,2560]{1,0:T(8,128)(2,1)} %bitcast.36, bf16[2,256,2560]{2,1,0:T(8,128)(2,1)} %copy-done, bf16[256,2560]{1,0:T(8,128)(2,1)} %bitcast.26, bf16[2,256,2560]{2,1,0:T(8,128)(2,1)} %collective-permute-done.3.kr_ref.vr_ref, ...), custom_call_target="tpu_custom_call" | custom-call | flops 1006632960 | bytes 5242880 | tf_op jit(solution)/shard_map/pallas_call | solution.py:92
  74.9 7.6 %shard_map.58 = bf16[272,1280]{1,0:T(8,128)(2,1)} custom-call(s32[3]{0:T(128)} %add_convert_fusion.2.flags_ref, bf16[272,1280]{1,0:T(8,128)(2,1)} %copy-done.4, bf16[2,256,2560]{2,1,0:T(8,128)(2,1)} %copy-done, bf16[256,2560]{1,0:T(8,128)(2,1)} %bitcast.27, bf16[2,256,2560]{2,1,0:T(8,128)(2,1)} %collective-permute-done.3.kr_ref.vr_ref, ...), custom_call_target="tpu_custom_call" | custom-call | flops 1006632960 | bytes 5242880 | tf_op jit(solution)/shard_map/pallas_call | solution.py:92
  82.4 2.1 %collective-permute-start.8 = (bf16[272,1280]{1,0:T(8,128)(2,1)}, bf16[272,1280]{1,0:T(8,128)(2,1)S(1)}, u32[]{:S(2)}, u32[]{:S(2)}) collective-permute-start(bf16[272,1280]{1,0:T(8,128)(2,1)} %shard_map.58), channel_id=1, source_target_pairs={{0,8},{8,16},{16,24},{24,32},{32,40},{40,48},{48,56},{56,64},{64,7... | collective-permute-start | bytes 2088968 | tf_op jit(solution)/shard_map/ppermute | solution.py:197
  84.5 7.6 %shard_map.59.a_ref = bf16[272,1280]{1,0:T(8,128)(2,1)} custom-call(s32[3]{0:T(128)} %add_convert_fusion.1.flags_ref, bf16[256,2560]{1,0:T(8,128)(2,1)} %bitcast.37, bf16[2,256,2560]{2,1,0:T(8,128)(2,1)} %copy-done, bf16[256,2560]{1,0:T(8,128)(2,1)} %bitcast.28, bf16[2,256,2560]{2,1,0:T(8,128)(2,1)} %collective-permute-done.3.kr_ref.vr_ref, ...), custom_call_target="tpu_custom_call" | custom-call | flops 1006632960 | bytes 5242880 | tf_op jit(solution)/shard_map/pallas_call | solution.py:92
  93.0 7.5 %shard_map.60 = bf16[272,1280]{1,0:T(8,128)(2,1)} custom-call(s32[3]{0:T(128)} %add_convert_fusion.2.flags_ref, bf16[256,1280]{1,0:T(8,128)(2,1)} %copy-done.9, bf16[2,256,2560]{2,1,0:T(8,128)(2,1)} %copy-done, bf16[256,2560]{1,0:T(8,128)(2,1)} %bitcast.29, bf16[2,256,2560]{2,1,0:T(8,128)(2,1)} %collective-permute-done.3.kr_ref.vr_ref, ...), custom_call_target="tpu_custom_call" | custom-call | flops 1006632960 | bytes 5242880 | tf_op jit(solution)/shard_map/pallas_call | solution.py:92
  100.5 1.9 %collective-permute-start.6 = (bf16[272,1280]{1,0:T(8,128)(2,1)}, bf16[272,1280]{1,0:T(8,128)(2,1)S(1)}, u32[]{:S(2)}, u32[]{:S(2)}) collective-permute-start(bf16[272,1280]{1,0:T(8,128)(2,1)} %shard_map.60), channel_id=1, source_target_pairs={{0,8},{8,16},{16,24},{24,32},{32,40},{40,48},{48,56},{56,64},{64,7... | collective-permute-start | bytes 2088968 | tf_op jit(solution)/shard_map/ppermute | solution.py:197
  102.4 2.5 %collective-permute-done.8.b_ref = bf16[272,1280]{1,0:T(8,128)(2,1)S(1)} collective-permute-done((bf16[272,1280]{1,0:T(8,128)(2,1)}, bf16[272,1280]{1,0:T(8,128)(2,1)S(1)}, u32[]{:S(2)}, u32[]{:S(2)}) %collective-permute-start.8) | collective-permute-done | bytes 696352 | tf_op jit(solution)/shard_map/ppermute | solution.py:197
  105.8 3.0 %shard_map.62 = bf16[272,1280]{1,0:T(8,128)(2,1)} custom-call(s32[1]{0:T(128)} %bitcast.valid_ref, bf16[272,1280]{1,0:T(8,128)(2,1)} %shard_map.56.a_ref, bf16[272,1280]{1,0:T(8,128)(2,1)} %copy-done.6), custom_call_target="tpu_custom_call" | custom-call | flops 1310720 | bytes 1966080 | tf_op jit(solution)/shard_map/pallas_call | solution.py:176
  110.7 12.3 %collective-permute-done.6.b_ref = bf16[272,1280]{1,0:T(8,128)(2,1)S(1)} collective-permute-done((bf16[272,1280]{1,0:T(8,128)(2,1)}, bf16[272,1280]{1,0:T(8,128)(2,1)S(1)}, u32[]{:S(2)}, u32[]{:S(2)}) %collective-permute-start.6) | collective-permute-done | bytes 696352 | tf_op jit(solution)/shard_map/ppermute | solution.py:197
  123.9 2.9 %shard_map.61 = bf16[272,1280]{1,0:T(8,128)(2,1)} custom-call(s32[1]{0:T(128)} %bitcast.valid_ref, bf16[272,1280]{1,0:T(8,128)(2,1)} %shard_map.55.a_ref, bf16[272,1280]{1,0:T(8,128)(2,1)} %copy-done.7), custom_call_target="tpu_custom_call" | custom-call | flops 1310720 | bytes 1966080 | tf_op jit(solution)/shard_map/pallas_call | solution.py:176
  128.8 9.2 %collective-permute-done.9.b_ref = bf16[272,1280]{1,0:T(8,128)(2,1)S(1)} collective-permute-done((bf16[272,1280]{1,0:T(8,128)(2,1)}, bf16[272,1280]{1,0:T(8,128)(2,1)S(1)}, u32[]{:S(2)}, u32[]{:S(2)}) %collective-permute-start.9) | collective-permute-done | bytes 696352 | tf_op jit(solution)/shard_map/ppermute | solution.py:197
  138.9 2.9 %shard_map.63.rest_0_ = bf16[256,2560]{1,0:T(8,128)(2,1)} custom-call(s32[1]{0:T(128)} %bitcast.valid_ref, bf16[272,1280]{1,0:T(8,128)(2,1)} %shard_map.57.a_ref, bf16[272,1280]{1,0:T(8,128)(2,1)} %copy-done.5), custom_call_target="tpu_custom_call" | custom-call | flops 1310720 | bytes 1966080 | tf_op jit(solution)/shard_map/pallas_call | solution.py:176
  141.8 11.1 %collective-permute-done.7.b_ref = bf16[272,1280]{1,0:T(8,128)(2,1)S(1)} collective-permute-done((bf16[272,1280]{1,0:T(8,128)(2,1)}, bf16[272,1280]{1,0:T(8,128)(2,1)S(1)}, u32[]{:S(2)}, u32[]{:S(2)}) %collective-permute-start.7) | collective-permute-done | bytes 696352 | tf_op jit(solution)/shard_map/ppermute | solution.py:197
  153.7 2.9 %shard_map.64 = bf16[256,2560]{1,0:T(8,128)(2,1)} custom-call(s32[1]{0:T(128)} %bitcast.valid_ref, bf16[272,1280]{1,0:T(8,128)(2,1)} %shard_map.59.a_ref, bf16[272,1280]{1,0:T(8,128)(2,1)} %copy-done.8, bf16[256,2560]{1,0:T(8,128)(2,1)} %shard_map.63.rest_0_), custom_call_target="tpu_custom_call", output_to_operand_aliasing={{}: (3, {})} | custom-call | flops 1310720 | bytes 1966080 | tf_op jit(solution)/shard_map/pallas_call | solution.py:176
  (43 shorter events, 18.2 us)
Async XLA Ops:
  0.0 2.6 %copy-start.1 = (bf16[1,256,2560]{2,1,0:T(8,128)(2,1)S(1)}, bf16[1,256,2560]{2,1,0:T(8,128)(2,1)}, u32[]{:S(2)}) copy-start(bf16[1,256,2560]{2,1,0:T(8,128)(2,1)} %param.9) | copy-start | bytes 3932164
  2.6 7.4 %copy-start.10 = (s32[1,1,2]{2,1,0:T(1,128)S(1)}, s32[1,1,2]{2,1,0:T(1,128)}, u32[]{:S(2)}) copy-start(s32[1,1,2]{2,1,0:T(1,128)} %param.11) | copy-start | bytes 28
  2.6 7.5 %copy-start.2 = (bf16[1,256,2560]{2,1,0:T(8,128)(2,1)S(1)}, bf16[1,256,2560]{2,1,0:T(8,128)(2,1)}, u32[]{:S(2)}) copy-start(bf16[1,256,2560]{2,1,0:T(8,128)(2,1)} %param.7) | copy-start | bytes 3932164
  3.7 33.2 %collective-permute-start.2 = (bf16[2,256,2560]{2,1,0:T(8,128)(2,1)}, bf16[2,256,2560]{2,1,0:T(8,128)(2,1)S(1)}, u32[]{:S(2)}, u32[]{:S(2)}) collective-permute-start(bf16[2,256,2560]{2,1,0:T(8,128)(2,1)} %constant_dynamic-update-slice_fusion), channel_id=1, source_target_pairs={{0,1},{1,2},{2,3},{3,4},{4,5},{5,6},{6,7},{8,9},{9,10},{10,11},{11... | collective-permute-start | bytes 7864328 | tf_op jit(solution)/shard_map/ppermute | solution.py:230
  5.7 33.1 %collective-permute-start.3 = (bf16[2,256,2560]{2,1,0:T(8,128)(2,1)}, bf16[2,256,2560]{2,1,0:T(8,128)(2,1)}, u32[]{:S(2)}, u32[]{:S(2)}) collective-permute-start(bf16[2,256,2560]{2,1,0:T(8,128)(2,1)} %constant_dynamic-update-slice_fusion), channel_id=1, source_target_pairs={{1,0},{2,1},{3,2},{4,3},{5,4},{6,5},{7,6},{9,8},{10,9},{11,10},{12... | collective-permute-start | bytes 7864328 | tf_op jit(solution)/shard_map/ppermute | solution.py:231
  11.9 20.8 %collective-permute-start.1 = (bf16[272,1280]{1,0:T(8,128)(2,1)}, bf16[272,1280]{1,0:T(8,128)(2,1)S(1)}, u32[]{:S(2)}, u32[]{:S(2)}) collective-permute-start(bf16[272,1280]{1,0:T(8,128)(2,1)} %pad_maximum_fusion), channel_id=1, source_target_pairs={{8,0},{16,8},{24,16},{32,24},{40,32},{48,40},{56,48},{64,56},{72,6... | collective-permute-start | bytes 2088968 | tf_op jit(solution)/shard_map/ppermute | solution.py:197
  16.4 38.2 %collective-permute-start = (bf16[256,1280]{1,0:T(8,128)(2,1)}, bf16[256,1280]{1,0:T(8,128)(2,1)}, u32[]{:S(2)}, u32[]{:S(2)}) collective-permute-start(bf16[256,1280]{1,0:T(8,128)(2,1)} %get-tuple-element.40), channel_id=1, source_target_pairs={{8,0},{16,8},{24,16},{32,24},{40,32},{48,40},{56,48},{64,56},{72,6... | collective-permute-start | bytes 1966088 | tf_op jit(solution)/shard_map/ppermute | solution.py:197
  32.7 6.1 %copy-start.3 = (bf16[272,1280]{1,0:T(8,128)(2,1)}, bf16[272,1280]{1,0:T(8,128)(2,1)S(1)}, u32[]{:S(2)}) copy-start(bf16[272,1280]{1,0:T(8,128)(2,1)S(1)} %collective-permute-done.1.q_ref) | copy-start | bytes 2088964
  36.9 1.9 %copy-start = (bf16[2,256,2560]{2,1,0:T(8,128)(2,1)}, bf16[2,256,2560]{2,1,0:T(8,128)(2,1)S(1)}, u32[]{:S(2)}) copy-start(bf16[2,256,2560]{2,1,0:T(8,128)(2,1)S(1)} %collective-permute-done.2.kl_ref.vl_ref) | copy-start | bytes 7864324
  46.3 25.3 %collective-permute-start.5 = (bf16[272,1280]{1,0:T(8,128)(2,1)}, bf16[272,1280]{1,0:T(8,128)(2,1)S(1)}, u32[]{:S(2)}, u32[]{:S(2)}) collective-permute-start(bf16[272,1280]{1,0:T(8,128)(2,1)} %copy-done.3), channel_id=1, source_target_pairs={{8,0},{16,8},{24,16},{32,24},{40,32},{48,40},{56,48},{64,56},{72,6... | collective-permute-start | bytes 2088968 | tf_op jit(solution)/shard_map/ppermute | solution.py:197
  62.1 30.0 %collective-permute-start.4 = (bf16[256,1280]{1,0:T(8,128)(2,1)}, bf16[256,1280]{1,0:T(8,128)(2,1)S(1)}, u32[]{:S(2)}, u32[]{:S(2)}) collective-permute-start(bf16[256,1280]{1,0:T(8,128)(2,1)} %collective-permute-done.q_ref), channel_id=1, source_target_pairs={{8,0},{16,8},{24,16},{32,24},{40,32},{48,40},{56,48},{64,56},{72,6... | collective-permute-start | bytes 1966088 | tf_op jit(solution)/shard_map/ppermute | solution.py:197
  71.6 3.3 %copy-start.4 = (bf16[272,1280]{1,0:T(8,128)(2,1)}, bf16[272,1280]{1,0:T(8,128)(2,1)S(1)}, u32[]{:S(2)}) copy-start(bf16[272,1280]{1,0:T(8,128)(2,1)S(1)} %collective-permute-done.5.q_ref) | copy-start | bytes 2088964
  82.4 22.5 %collective-permute-start.8 = (bf16[272,1280]{1,0:T(8,128)(2,1)}, bf16[272,1280]{1,0:T(8,128)(2,1)S(1)}, u32[]{:S(2)}, u32[]{:S(2)}) collective-permute-start(bf16[272,1280]{1,0:T(8,128)(2,1)} %shard_map.58), channel_id=1, source_target_pairs={{0,8},{8,16},{16,24},{24,32},{32,40},{40,48},{48,56},{56,64},{64,7... | collective-permute-start | bytes 2088968 | tf_op jit(solution)/shard_map/ppermute | solution.py:197
  92.1 0.9 copy-start.9
  100.5 22.5 %collective-permute-start.6 = (bf16[272,1280]{1,0:T(8,128)(2,1)}, bf16[272,1280]{1,0:T(8,128)(2,1)S(1)}, u32[]{:S(2)}, u32[]{:S(2)}) collective-permute-start(bf16[272,1280]{1,0:T(8,128)(2,1)} %shard_map.60), channel_id=1, source_target_pairs={{0,8},{8,16},{16,24},{24,32},{32,40},{40,48},{48,56},{56,64},{64,7... | collective-permute-start | bytes 2088968 | tf_op jit(solution)/shard_map/ppermute | solution.py:197
  105.0 0.9 copy-start.6
  108.8 29.2 %collective-permute-start.9 = (bf16[272,1280]{1,0:T(8,128)(2,1)}, bf16[272,1280]{1,0:T(8,128)(2,1)S(1)}, u32[]{:S(2)}, u32[]{:S(2)}) collective-permute-start(bf16[272,1280]{1,0:T(8,128)(2,1)} %shard_map.62), channel_id=1, source_target_pairs={{0,8},{8,16},{16,24},{24,32},{32,40},{40,48},{48,56},{56,64},{64,7... | collective-permute-start | bytes 2088968 | tf_op jit(solution)/shard_map/ppermute | solution.py:197
  123.0 0.9 copy-start.7
  126.9 26.0 %collective-permute-start.7 = (bf16[272,1280]{1,0:T(8,128)(2,1)}, bf16[272,1280]{1,0:T(8,128)(2,1)S(1)}, u32[]{:S(2)}, u32[]{:S(2)}) collective-permute-start(bf16[272,1280]{1,0:T(8,128)(2,1)} %shard_map.61), channel_id=1, source_target_pairs={{0,8},{8,16},{16,24},{24,32},{32,40},{40,48},{48,56},{56,64},{64,7... | collective-permute-start | bytes 2088968 | tf_op jit(solution)/shard_map/ppermute | solution.py:197
  138.0 0.9 copy-start.5
  152.9 0.9 copy-start.8

commit v4 on v3

--- a/solution.py
+++ b/solution.py
@@ -191,6 +191,33 @@
     )(*operands)
 
 
+def _split_kernel(meta_ref, q_ref, *out_refs):
+    rows = q_ref.shape[0]
+    chunk_w = out_refs[0].shape[1]
+    for c, o_ref in enumerate(out_refs):
+        o_ref[0:rows, :] = q_ref[:, c * chunk_w : (c + 1) * chunk_w]
+    row = lax.broadcasted_iota(jnp.int32, (EXTRA, chunk_w), 0)
+    lane = lax.broadcasted_iota(jnp.int32, (EXTRA, chunk_w), 1)
+    extra = jnp.zeros((EXTRA, chunk_w), jnp.float32)
+    for i in range(3):
+        extra = jnp.where((row == 0) & (lane == i), meta_ref[i].astype(jnp.float32), extra)
+    out_refs[0][rows : rows + EXTRA, :] = extra.astype(out_refs[0].dtype)
+
+
+def split_queries(meta, q, chunks):
+    rows, width = q.shape
+    chunk_w = width // chunks
+    shapes = [jax.ShapeDtypeStruct((rows + EXTRA, chunk_w), q.dtype)]
+    shapes += [jax.ShapeDtypeStruct((rows, chunk_w), q.dtype)] * (chunks - 1)
+    vmem = pltpu.MemorySpace.VMEM
+    return pl.pallas_call(
+        _split_kernel,
+        out_shape=shapes,
+        in_specs=[pl.BlockSpec(memory_space=pltpu.SMEM), pl.BlockSpec(memory_space=vmem)],
+        out_specs=[pl.BlockSpec(memory_space=vmem)] * chunks,
+    )(meta, q)
+
+
 def shift_tm(x, by):
     size = lax.axis_size("tm")
     pairs = [(i, i + by) for i in range(size) if 0 <= i + by < size]
@@ -218,12 +245,10 @@
             ]
         )
 
-    meta = jnp.concatenate([history.reshape(1), neighbours.reshape(2)]).astype(jnp.bfloat16)
+    meta = jnp.concatenate([history.reshape(1), neighbours.reshape(2)]).astype(jnp.int32)
     chunk_w = width // CHUNKS
     groups_c = chunk_w // HEAD_DIM // HG
-    meta_rows = jnp.zeros((EXTRA, chunk_w), jnp.bfloat16).at[0, 0:3].set(meta)
-    sends = [jnp.concatenate([q[:, :chunk_w], meta_rows], axis=0)]
-    sends += [q[:, c * chunk_w : (c + 1) * chunk_w] for c in range(1, CHUNKS)]
+    sends = split_queries(meta, q, CHUNKS)
     q1s = [shift_tm(x, -1) for x in sends]
 
     kv = jnp.stack([k, v])

time: 158 us -> 156 us (0.987)
  the two profiles are of different devices: /device:TPU:112 before, /device:TPU:41 now
where the time goes in v4:
time: 156 us; the launch traced here: 157 us
  waiting for transfers between devices  52.8 us (34%)
  Pallas kernels  51.9 us (33%)
  starting transfers between devices  33.8 us (22%)
  local copies, waits for them, and re-layouts  10.2 us (7%)
  between operations  5.87 us (4%)
  other arithmetic  2.43 us (2%)
    ppermute x8, waiting for transfers between devices, shift_tm(): return lax.ppermute(x, 'tm', pairs)  46.7 us
    pallas_call x6, Pallas kernels, attend(): pl.pallas_call(_attn_kernel, out_shape=jax.ShapeDtypeStruct((rows + EXTRA...  37.7 us
    ppermute x8, starting transfers between devices, shift_tm(): return lax.ppermute(x, 'tm', pairs)  28.1 us
    pallas_call x4, Pallas kernels, merge(): pl.pallas_call(kernel, out_shape=out_shape, grid_spec=pltpu.PrefetchScala...  11.7 us
    unnamed x21, local copies, waits for them, and re-layouts  6.97 us
    ppermute x1, waiting for transfers between devices, on_device(): kv_r = lax.ppermute(kv, 'space', [(i + 1, i) for i in range(tiles - 1)])  4.69 us
    ppermute x1, starting transfers between devices, on_device(): kv_l = lax.ppermute(kv, 'space', [(i, i + 1) for i in range(tiles - 1)])  3.75 us
  transfers between devices with their start and end apart: 10, of which 7 were waited for; matrix products, arithmetic and copies ran while one was open for 3% of the time, Pallas kernels for 31%

profile of v4, /device:TPU:41, one launch (start us, length us, event | category | flops | bytes accessed | tf_op | source)
XLA Modules:
  0.0 157.0 jit_solution(1525716188265095802)
XLA Ops:
  0.0 2.6 %constant_dynamic-update-slice_fusion.1 = bf16[2,256,2560]{2,1,0:T(8,128)(2,1)} fusion(bf16[1,256,2560]{2,1,0:T(8,128)(2,1)} %param.6), kind=kLoop, calls=%fused_computation.1 | loop fusion | bytes 2621440
  3.8 3.8 %collective-permute-start.2 = (bf16[2,256,2560]{2,1,0:T(8,128)(2,1)}, bf16[2,256,2560]{2,1,0:T(8,128)(2,1)S(1)}, u32[]{:S(2)}, u32[]{:S(2)}) collective-permute-start(bf16[2,256,2560]{2,1,0:T(8,128)(2,1)} %constant_dynamic-update-slice_fusion), channel_id=1, source_target_pairs={{0,1},{1,2},{2,3},{3,4},{4,5},{5,6},{6,7},{8,9},{9,10},{10,11},{11... | collective-permute-start | bytes 7864328 | tf_op jit(solution)/shard_map/ppermute | solution.py:255
  7.5 1.9 %collective-permute-start.3 = (bf16[2,256,2560]{2,1,0:T(8,128)(2,1)}, bf16[2,256,2560]{2,1,0:T(8,128)(2,1)}, u32[]{:S(2)}, u32[]{:S(2)}) collective-permute-start(bf16[2,256,2560]{2,1,0:T(8,128)(2,1)} %constant_dynamic-update-slice_fusion), channel_id=1, source_target_pairs={{1,0},{2,1},{3,2},{4,3},{5,4},{6,5},{7,6},{9,8},{10,9},{11,10},{12... | collective-permute-start | bytes 7864328 | tf_op jit(solution)/shard_map/ppermute | solution.py:256
  10.7 2.4 %shard_map.55 = (bf16[272,1280]{1,0:T(8,128)(2,1)}, bf16[256,1280]{1,0:T(8,128)(2,1)}) custom-call(s32[3]{0:T(128)} %pad_add_fusion.meta_ref, bf16[256,2560]{1,0:T(8,128)(2,1)} %bitcast.32), custom_call_target="tpu_custom_call" | custom-call | tf_op jit(solution)/shard_map/pallas_call | solution.py:213
  13.1 3.9 %collective-permute-start.1 = (bf16[272,1280]{1,0:T(8,128)(2,1)}, bf16[272,1280]{1,0:T(8,128)(2,1)S(1)}, u32[]{:S(2)}, u32[]{:S(2)}) collective-permute-start(bf16[272,1280]{1,0:T(8,128)(2,1)} %get-tuple-element.19), channel_id=1, source_target_pairs={{8,0},{16,8},{24,16},{32,24},{40,32},{48,40},{56,48},{64,56},{72,6... | collective-permute-start | bytes 2088968 | tf_op jit(solution)/shard_map/ppermute | solution.py:224
  17.0 2.5 %collective-permute-start = (bf16[256,1280]{1,0:T(8,128)(2,1)}, bf16[256,1280]{1,0:T(8,128)(2,1)}, u32[]{:S(2)}, u32[]{:S(2)}) collective-permute-start(bf16[256,1280]{1,0:T(8,128)(2,1)} %get-tuple-element.18), channel_id=1, source_target_pairs={{8,0},{16,8},{24,16},{32,24},{40,32},{48,40},{56,48},{64,56},{72,6... | collective-permute-start | bytes 1966088 | tf_op jit(solution)/shard_map/ppermute | solution.py:224
  19.5 12.3 %collective-permute-done.1.q_ref = bf16[272,1280]{1,0:T(8,128)(2,1)S(1)} collective-permute-done((bf16[272,1280]{1,0:T(8,128)(2,1)}, bf16[272,1280]{1,0:T(8,128)(2,1)S(1)}, u32[]{:S(2)}, u32[]{:S(2)}) %collective-permute-start.1) | collective-permute-done | bytes 696352 | tf_op jit(solution)/shard_map/ppermute | solution.py:224
  36.4 4.7 %collective-permute-done.3.kr_ref.vr_ref = bf16[2,256,2560]{2,1,0:T(8,128)(2,1)} collective-permute-done((bf16[2,256,2560]{2,1,0:T(8,128)(2,1)}, bf16[2,256,2560]{2,1,0:T(8,128)(2,1)}, u32[]{:S(2)}, u32[]{:S(2)}) %collective-permute-start.3) | collective-permute-done | bytes 2621472 | tf_op jit(solution)/shard_map/ppermute | solution.py:256
  41.1 3.8 %shard_map.57.a_ref = bf16[272,1280]{1,0:T(8,128)(2,1)} custom-call(s32[3]{0:T(128)} %add_convert_fusion.flags_ref, bf16[272,1280]{1,0:T(8,128)(2,1)} %copy-done.2, bf16[2,256,2560]{2,1,0:T(8,128)(2,1)} %copy-done, bf16[256,2560]{1,0:T(8,128)(2,1)} %bitcast.20, bf16[2,256,2560]{2,1,0:T(8,128)(2,1)} %collective-permute-done.3.kr_ref.vr_ref, ...), custom_call_target="tpu_custom_call" | custom-call | flops 1006632960 | bytes 5242880 | tf_op jit(solution)/shard_map/pallas_call | solution.py:92
  44.9 7.7 %collective-permute-start.5 = (bf16[272,1280]{1,0:T(8,128)(2,1)}, bf16[272,1280]{1,0:T(8,128)(2,1)S(1)}, u32[]{:S(2)}, u32[]{:S(2)}) collective-permute-start(bf16[272,1280]{1,0:T(8,128)(2,1)} %copy-done.2), channel_id=1, source_target_pairs={{8,0},{16,8},{24,16},{32,24},{40,32},{48,40},{56,48},{64,56},{72,6... | collective-permute-start | bytes 2088968 | tf_op jit(solution)/shard_map/ppermute | solution.py:224
  55.3 3.8 %shard_map.56.a_ref = bf16[272,1280]{1,0:T(8,128)(2,1)} custom-call(s32[3]{0:T(128)} %add_convert_fusion.flags_ref, bf16[256,1280]{1,0:T(8,128)(2,1)} %collective-permute-done.q_ref, bf16[2,256,2560]{2,1,0:T(8,128)(2,1)} %copy-done, bf16[256,2560]{1,0:T(8,128)(2,1)} %bitcast.21, bf16[2,256,2560]{2,1,0:T(8,128)(2,1)} %collective-permute-done.3.kr_ref.vr_ref, ...), custom_call_target="tpu_custom_call" | custom-call | flops 1006632960 | bytes 5242880 | tf_op jit(solution)/shard_map/pallas_call | solution.py:92
  59.0 6.2 %collective-permute-start.4 = (bf16[256,1280]{1,0:T(8,128)(2,1)}, bf16[256,1280]{1,0:T(8,128)(2,1)S(1)}, u32[]{:S(2)}, u32[]{:S(2)}) collective-permute-start(bf16[256,1280]{1,0:T(8,128)(2,1)} %collective-permute-done.q_ref), channel_id=1, source_target_pairs={{8,0},{16,8},{24,16},{32,24},{40,32},{48,40},{56,48},{64,56},{72,6... | collective-permute-start | bytes 1966088 | tf_op jit(solution)/shard_map/ppermute | solution.py:224
  65.2 7.5 %shard_map.58.a_ref = bf16[272,1280]{1,0:T(8,128)(2,1)} custom-call(s32[3]{0:T(128)} %add_convert_fusion.1.flags_ref, bf16[256,2560]{1,0:T(8,128)(2,1)} %bitcast.33, bf16[2,256,2560]{2,1,0:T(8,128)(2,1)} %copy-done, bf16[256,2560]{1,0:T(8,128)(2,1)} %bitcast.22, bf16[2,256,2560]{2,1,0:T(8,128)(2,1)} %collective-permute-done.3.kr_ref.vr_ref, ...), custom_call_target="tpu_custom_call" | custom-call | flops 1006632960 | bytes 5242880 | tf_op jit(solution)/shard_map/pallas_call | solution.py:92
  76.0 7.6 %shard_map.59 = bf16[272,1280]{1,0:T(8,128)(2,1)} custom-call(s32[3]{0:T(128)} %add_convert_fusion.2.flags_ref, bf16[272,1280]{1,0:T(8,128)(2,1)} %copy-done.3, bf16[2,256,2560]{2,1,0:T(8,128)(2,1)} %copy-done, bf16[256,2560]{1,0:T(8,128)(2,1)} %bitcast.23, bf16[2,256,2560]{2,1,0:T(8,128)(2,1)} %collective-permute-done.3.kr_ref.vr_ref, ...), custom_call_target="tpu_custom_call" | custom-call | flops 1006632960 | bytes 5242880 | tf_op jit(solution)/shard_map/pallas_call | solution.py:92
  83.6 2.1 %collective-permute-start.8 = (bf16[272,1280]{1,0:T(8,128)(2,1)}, bf16[272,1280]{1,0:T(8,128)(2,1)S(1)}, u32[]{:S(2)}, u32[]{:S(2)}) collective-permute-start(bf16[272,1280]{1,0:T(8,128)(2,1)} %shard_map.59), channel_id=1, source_target_pairs={{0,8},{8,16},{16,24},{24,32},{32,40},{40,48},{48,56},{56,64},{64,7... | collective-permute-start | bytes 2088968 | tf_op jit(solution)/shard_map/ppermute | solution.py:224
  85.7 7.6 %shard_map.60.a_ref = bf16[272,1280]{1,0:T(8,128)(2,1)} custom-call(s32[3]{0:T(128)} %add_convert_fusion.1.flags_ref, bf16[256,2560]{1,0:T(8,128)(2,1)} %bitcast.34, bf16[2,256,2560]{2,1,0:T(8,128)(2,1)} %copy-done, bf16[256,2560]{1,0:T(8,128)(2,1)} %bitcast.24, bf16[2,256,2560]{2,1,0:T(8,128)(2,1)} %collective-permute-done.3.kr_ref.vr_ref, ...), custom_call_target="tpu_custom_call" | custom-call | flops 1006632960 | bytes 5242880 | tf_op jit(solution)/shard_map/pallas_call | solution.py:92
  94.1 7.6 %shard_map.61 = bf16[272,1280]{1,0:T(8,128)(2,1)} custom-call(s32[3]{0:T(128)} %add_convert_fusion.2.flags_ref, bf16[256,1280]{1,0:T(8,128)(2,1)} %copy-done.8, bf16[2,256,2560]{2,1,0:T(8,128)(2,1)} %copy-done, bf16[256,2560]{1,0:T(8,128)(2,1)} %bitcast.25, bf16[2,256,2560]{2,1,0:T(8,128)(2,1)} %collective-permute-done.3.kr_ref.vr_ref, ...), custom_call_target="tpu_custom_call" | custom-call | flops 1006632960 | bytes 5242880 | tf_op jit(solution)/shard_map/pallas_call | solution.py:92
  106.1 3.0 %shard_map.63 = bf16[272,1280]{1,0:T(8,128)(2,1)} custom-call(s32[1]{0:T(128)} %bitcast.valid_ref, bf16[272,1280]{1,0:T(8,128)(2,1)} %shard_map.57.a_ref, bf16[272,1280]{1,0:T(8,128)(2,1)} %copy-done.5), custom_call_target="tpu_custom_call" | custom-call | flops 1310720 | bytes 1966080 | tf_op jit(solution)/shard_map/pallas_call | solution.py:176
  111.0 12.4 %collective-permute-done.6.b_ref = bf16[272,1280]{1,0:T(8,128)(2,1)S(1)} collective-permute-done((bf16[272,1280]{1,0:T(8,128)(2,1)}, bf16[272,1280]{1,0:T(8,128)(2,1)S(1)}, u32[]{:S(2)}, u32[]{:S(2)}) %collective-permute-start.6) | collective-permute-done | bytes 696352 | tf_op jit(solution)/shard_map/ppermute | solution.py:224
  124.2 2.9 %shard_map.62 = bf16[272,1280]{1,0:T(8,128)(2,1)} custom-call(s32[1]{0:T(128)} %bitcast.valid_ref, bf16[272,1280]{1,0:T(8,128)(2,1)} %shard_map.56.a_ref, bf16[272,1280]{1,0:T(8,128)(2,1)} %copy-done.6), custom_call_target="tpu_custom_call" | custom-call | flops 1310720 | bytes 1966080 | tf_op jit(solution)/shard_map/pallas_call | solution.py:176
  129.1 9.2 %collective-permute-done.9.b_ref = bf16[272,1280]{1,0:T(8,128)(2,1)S(1)} collective-permute-done((bf16[272,1280]{1,0:T(8,128)(2,1)}, bf16[272,1280]{1,0:T(8,128)(2,1)S(1)}, u32[]{:S(2)}, u32[]{:S(2)}) %collective-permute-start.9) | collective-permute-done | bytes 696352 | tf_op jit(solution)/shard_map/ppermute | solution.py:224
  139.2 2.9 %shard_map.64.rest_0_ = bf16[256,2560]{1,0:T(8,128)(2,1)} custom-call(s32[1]{0:T(128)} %bitcast.valid_ref, bf16[272,1280]{1,0:T(8,128)(2,1)} %shard_map.58.a_ref, bf16[272,1280]{1,0:T(8,128)(2,1)} %copy-done.4), custom_call_target="tpu_custom_call" | custom-call | flops 1310720 | bytes 1966080 | tf_op jit(solution)/shard_map/pallas_call | solution.py:176
  142.0 11.1 %collective-permute-done.7.b_ref = bf16[272,1280]{1,0:T(8,128)(2,1)S(1)} collective-permute-done((bf16[272,1280]{1,0:T(8,128)(2,1)}, bf16[272,1280]{1,0:T(8,128)(2,1)S(1)}, u32[]{:S(2)}, u32[]{:S(2)}) %collective-permute-start.7) | collective-permute-done | bytes 696352 | tf_op jit(solution)/shard_map/ppermute | solution.py:224
  154.1 2.9 %shard_map.65 = bf16[256,2560]{1,0:T(8,128)(2,1)} custom-call(s32[1]{0:T(128)} %bitcast.valid_ref, bf16[272,1280]{1,0:T(8,128)(2,1)} %shard_map.60.a_ref, bf16[272,1280]{1,0:T(8,128)(2,1)} %copy-done.7, bf16[256,2560]{1,0:T(8,128)(2,1)} %shard_map.64.rest_0_), custom_call_target="tpu_custom_call", output_to_operand_aliasing={{}: (3, {})} | custom-call | flops 1310720 | bytes 1966080 | tf_op jit(solution)/shard_map/pallas_call | solution.py:176
  (38 shorter events, 18.9 us)
Async XLA Ops:
  0.0 2.6 %copy-start.1 = (bf16[1,256,2560]{2,1,0:T(8,128)(2,1)S(1)}, bf16[1,256,2560]{2,1,0:T(8,128)(2,1)}, u32[]{:S(2)}) copy-start(bf16[1,256,2560]{2,1,0:T(8,128)(2,1)} %param.7) | copy-start | bytes 3932164
  0.0 10.1 %copy-start.9 = (s32[1,1,2]{2,1,0:T(1,128)S(1)}, s32[1,1,2]{2,1,0:T(1,128)}, u32[]{:S(2)}) copy-start(s32[1,1,2]{2,1,0:T(1,128)} %param.9) | copy-start | bytes 28
  3.8 32.7 %collective-permute-start.2 = (bf16[2,256,2560]{2,1,0:T(8,128)(2,1)}, bf16[2,256,2560]{2,1,0:T(8,128)(2,1)S(1)}, u32[]{:S(2)}, u32[]{:S(2)}) collective-permute-start(bf16[2,256,2560]{2,1,0:T(8,128)(2,1)} %constant_dynamic-update-slice_fusion), channel_id=1, source_target_pairs={{0,1},{1,2},{2,3},{3,4},{4,5},{5,6},{6,7},{8,9},{9,10},{10,11},{11... | collective-permute-start | bytes 7864328 | tf_op jit(solution)/shard_map/ppermute | solution.py:255
  7.5 33.6 %collective-permute-start.3 = (bf16[2,256,2560]{2,1,0:T(8,128)(2,1)}, bf16[2,256,2560]{2,1,0:T(8,128)(2,1)}, u32[]{:S(2)}, u32[]{:S(2)}) collective-permute-start(bf16[2,256,2560]{2,1,0:T(8,128)(2,1)} %constant_dynamic-update-slice_fusion), channel_id=1, source_target_pairs={{1,0},{2,1},{3,2},{4,3},{5,4},{6,5},{7,6},{9,8},{10,9},{11,10},{12... | collective-permute-start | bytes 7864328 | tf_op jit(solution)/shard_map/ppermute | solution.py:256
  13.1 18.7 %collective-permute-start.1 = (bf16[272,1280]{1,0:T(8,128)(2,1)}, bf16[272,1280]{1,0:T(8,128)(2,1)S(1)}, u32[]{:S(2)}, u32[]{:S(2)}) collective-permute-start(bf16[272,1280]{1,0:T(8,128)(2,1)} %get-tuple-element.19), channel_id=1, source_target_pairs={{8,0},{16,8},{24,16},{32,24},{40,32},{48,40},{56,48},{64,56},{72,6... | collective-permute-start | bytes 2088968 | tf_op jit(solution)/shard_map/ppermute | solution.py:224
  17.0 38.2 %collective-permute-start = (bf16[256,1280]{1,0:T(8,128)(2,1)}, bf16[256,1280]{1,0:T(8,128)(2,1)}, u32[]{:S(2)}, u32[]{:S(2)}) collective-permute-start(bf16[256,1280]{1,0:T(8,128)(2,1)} %get-tuple-element.18), channel_id=1, source_target_pairs={{8,0},{16,8},{24,16},{32,24},{40,32},{48,40},{56,48},{64,56},{72,6... | collective-permute-start | bytes 1966088 | tf_op jit(solution)/shard_map/ppermute | solution.py:224
  31.8 9.3 %copy-start.2 = (bf16[272,1280]{1,0:T(8,128)(2,1)}, bf16[272,1280]{1,0:T(8,128)(2,1)S(1)}, u32[]{:S(2)}) copy-start(bf16[272,1280]{1,0:T(8,128)(2,1)S(1)} %collective-permute-done.1.q_ref) | copy-start | bytes 2088964
  36.4 4.7 %copy-start = (bf16[2,256,2560]{2,1,0:T(8,128)(2,1)}, bf16[2,256,2560]{2,1,0:T(8,128)(2,1)S(1)}, u32[]{:S(2)}) copy-start(bf16[2,256,2560]{2,1,0:T(8,128)(2,1)S(1)} %collective-permute-done.2.kl_ref.vl_ref) | copy-start | bytes 7864324
  44.9 27.9 %collective-permute-start.5 = (bf16[272,1280]{1,0:T(8,128)(2,1)}, bf16[272,1280]{1,0:T(8,128)(2,1)S(1)}, u32[]{:S(2)}, u32[]{:S(2)}) collective-permute-start(bf16[272,1280]{1,0:T(8,128)(2,1)} %copy-done.2), channel_id=1, source_target_pairs={{8,0},{16,8},{24,16},{32,24},{40,32},{48,40},{56,48},{64,56},{72,6... | collective-permute-start | bytes 2088968 | tf_op jit(solution)/shard_map/ppermute | solution.py:224
  59.0 34.2 %collective-permute-start.4 = (bf16[256,1280]{1,0:T(8,128)(2,1)}, bf16[256,1280]{1,0:T(8,128)(2,1)S(1)}, u32[]{:S(2)}, u32[]{:S(2)}) collective-permute-start(bf16[256,1280]{1,0:T(8,128)(2,1)} %collective-permute-done.q_ref), channel_id=1, source_target_pairs={{8,0},{16,8},{24,16},{32,24},{40,32},{48,40},{56,48},{64,56},{72,6... | collective-permute-start | bytes 1966088 | tf_op jit(solution)/shard_map/ppermute | solution.py:224
  72.8 3.2 %copy-start.3 = (bf16[272,1280]{1,0:T(8,128)(2,1)}, bf16[272,1280]{1,0:T(8,128)(2,1)S(1)}, u32[]{:S(2)}) copy-start(bf16[272,1280]{1,0:T(8,128)(2,1)S(1)} %collective-permute-done.5.q_ref) | copy-start | bytes 2088964
  83.6 21.7 %collective-permute-start.8 = (bf16[272,1280]{1,0:T(8,128)(2,1)}, bf16[272,1280]{1,0:T(8,128)(2,1)S(1)}, u32[]{:S(2)}, u32[]{:S(2)}) collective-permute-start(bf16[272,1280]{1,0:T(8,128)(2,1)} %shard_map.59), channel_id=1, source_target_pairs={{0,8},{8,16},{16,24},{24,32},{32,40},{40,48},{48,56},{56,64},{64,7... | collective-permute-start | bytes 2088968 | tf_op jit(solution)/shard_map/ppermute | solution.py:224
  93.2 0.9 copy-start.8
  101.7 21.7 %collective-permute-start.6 = (bf16[272,1280]{1,0:T(8,128)(2,1)}, bf16[272,1280]{1,0:T(8,128)(2,1)S(1)}, u32[]{:S(2)}, u32[]{:S(2)}) collective-permute-start(bf16[272,1280]{1,0:T(8,128)(2,1)} %shard_map.61), channel_id=1, source_target_pairs={{0,8},{8,16},{16,24},{24,32},{32,40},{40,48},{48,56},{56,64},{64,7... | collective-permute-start | bytes 2088968 | tf_op jit(solution)/shard_map/ppermute | solution.py:224
  105.3 0.9 copy-start.5
  109.1 29.2 %collective-permute-start.9 = (bf16[272,1280]{1,0:T(8,128)(2,1)}, bf16[272,1280]{1,0:T(8,128)(2,1)S(1)}, u32[]{:S(2)}, u32[]{:S(2)}) collective-permute-start(bf16[272,1280]{1,0:T(8,128)(2,1)} %shard_map.63), channel_id=1, source_target_pairs={{0,8},{8,16},{16,24},{24,32},{32,40},{40,48},{48,56},{56,64},{64,7... | collective-permute-start | bytes 2088968 | tf_op jit(solution)/shard_map/ppermute | solution.py:224
  123.4 0.9 copy-start.6
  127.2 26.0 %collective-permute-start.7 = (bf16[272,1280]{1,0:T(8,128)(2,1)}, bf16[272,1280]{1,0:T(8,128)(2,1)S(1)}, u32[]{:S(2)}, u32[]{:S(2)}) collective-permute-start(bf16[272,1280]{1,0:T(8,128)(2,1)} %shard_map.62), channel_id=1, source_target_pairs={{0,8},{8,16},{16,24},{24,32},{32,40},{40,48},{48,56},{56,64},{64,7... | collective-permute-start | bytes 2088968 | tf_op jit(solution)/shard_map/ppermute | solution.py:224
  138.3 0.9 copy-start.4
  153.2 0.9 copy-start.7

commit v5 on v3

--- a/solution.py
+++ b/solution.py
@@ -233,9 +233,10 @@
     f1 = flags_for(q1s[0][rows, 0:3], 1)
     p1s, q2s = [], []
     for c in range(CHUNKS):
-        p1 = attend(f1, q1s[c], k, v, kv_l, kv_r, chunk_w, c * groups_c, 0)
-        relay, p1 = lax.optimization_barrier((q1s[c], p1))
-        p1s.append(p1)
+        p1s.append(attend(f1, q1s[c], k, v, kv_l, kv_r, chunk_w, c * groups_c, 0))
+        relay = q1s[c]
+        if c > 0:
+            relay, p1s[0], p1s[c] = lax.optimization_barrier((relay, p1s[0], p1s[c]))
         q2s.append(shift_tm(relay, -1))
 
     valid = (seg >= 1).astype(jnp.int32).reshape(1)

time: 158 us -> 154 us (0.975)
  the two profiles are of different devices: /device:TPU:112 before, /device:TPU:56 now
where the time goes in v5:
time: 154 us; the launch traced here: 153 us
  Pallas kernels  49.3 us (32%)
  waiting for transfers between devices  46.6 us (30%)
  starting transfers between devices  34 us (22%)
  local copies, waits for them, and re-layouts  12.5 us (8%)
  between operations  6.6 us (4%)
  other arithmetic  3.6 us (2%)
    ppermute x8, waiting for transfers between devices, shift_tm(): return lax.ppermute(x, 'tm', pairs)  46.6 us
    pallas_call x6, Pallas kernels, attend(): pl.pallas_call(_attn_kernel, out_shape=jax.ShapeDtypeStruct((rows + EXTRA...  37.7 us
    ppermute x8, starting transfers between devices, shift_tm(): return lax.ppermute(x, 'tm', pairs)  28.5 us
    pallas_call x4, Pallas kernels, merge(): pl.pallas_call(kernel, out_shape=out_shape, grid_spec=pltpu.PrefetchScala...  11.7 us
    unnamed x21, local copies, waits for them, and re-layouts  8.42 us
    ppermute x1, starting transfers between devices, on_device(): kv_r = lax.ppermute(kv, 'space', [(i + 1, i) for i in range(tiles - 1)])  3.64 us
  transfers between devices with their start and end apart: 10, of which 6 were waited for; matrix products, arithmetic and copies ran while one was open for 4% of the time, Pallas kernels for 30%

profile of v5, /device:TPU:56, one launch (start us, length us, event | category | flops | bytes accessed | tf_op | source)
XLA Modules:
  0.0 152.7 jit_solution(7575109946962890359)
XLA Ops:
  0.0 2.6 %constant_dynamic-update-slice_fusion.1 = bf16[2,256,2560]{2,1,0:T(8,128)(2,1)} fusion(bf16[1,256,2560]{2,1,0:T(8,128)(2,1)} %param.8), kind=kLoop, calls=%fused_computation.10 | loop fusion | bytes 2621440
  5.7 3.6 %collective-permute-start.3 = (bf16[2,256,2560]{2,1,0:T(8,128)(2,1)}, bf16[2,256,2560]{2,1,0:T(8,128)(2,1)}, u32[]{:S(2)}, u32[]{:S(2)}) collective-permute-start(bf16[2,256,2560]{2,1,0:T(8,128)(2,1)} %constant_dynamic-update-slice_fusion), channel_id=1, source_target_pairs={{1,0},{2,1},{3,2},{4,3},{5,4},{6,5},{7,6},{9,8},{10,9},{11,10},{12... | collective-permute-start | bytes 7864328 | tf_op jit(solution)/shard_map/ppermute | solution.py:231
  11.9 4.2 %collective-permute-start.1 = (bf16[272,1280]{1,0:T(8,128)(2,1)}, bf16[272,1280]{1,0:T(8,128)(2,1)S(1)}, u32[]{:S(2)}, u32[]{:S(2)}) collective-permute-start(bf16[272,1280]{1,0:T(8,128)(2,1)} %pad_maximum_fusion), channel_id=1, source_target_pairs={{8,0},{16,8},{24,16},{32,24},{40,32},{48,40},{56,48},{64,56},{72,6... | collective-permute-start | bytes 2088968 | tf_op jit(solution)/shard_map/ppermute | solution.py:197
  16.1 2.7 %collective-permute-start = (bf16[256,1280]{1,0:T(8,128)(2,1)}, bf16[256,1280]{1,0:T(8,128)(2,1)}, u32[]{:S(2)}, u32[]{:S(2)}) collective-permute-start(bf16[256,1280]{1,0:T(8,128)(2,1)} %get-tuple-element.38), channel_id=1, source_target_pairs={{8,0},{16,8},{24,16},{32,24},{40,32},{48,40},{56,48},{64,56},{72,6... | collective-permute-start | bytes 1966088 | tf_op jit(solution)/shard_map/ppermute | solution.py:197
  21.6 10.9 %collective-permute-done.1.q_ref = bf16[272,1280]{1,0:T(8,128)(2,1)S(1)} collective-permute-done((bf16[272,1280]{1,0:T(8,128)(2,1)}, bf16[272,1280]{1,0:T(8,128)(2,1)S(1)}, u32[]{:S(2)}, u32[]{:S(2)}) %collective-permute-start.1) | collective-permute-done | bytes 696352 | tf_op jit(solution)/shard_map/ppermute | solution.py:197
  32.5 6.3 %collective-permute-start.5 = (bf16[272,1280]{1,0:T(8,128)(2,1)S(1)}, bf16[272,1280]{1,0:T(8,128)(2,1)}, u32[]{:S(2)}, u32[]{:S(2)}) collective-permute-start(bf16[272,1280]{1,0:T(8,128)(2,1)S(1)} %collective-permute-done.1.q_ref), channel_id=1, source_target_pairs={{8,0},{16,8},{24,16},{32,24},{40,32},{48,40},{56,48},{64,56},{72,6... | collective-permute-start | bytes 2088968 | tf_op jit(solution)/shard_map/ppermute | solution.py:197
  44.1 3.8 %shard_map.55.a_ref = bf16[272,1280]{1,0:T(8,128)(2,1)} custom-call(s32[3]{0:T(128)} %add_convert_fusion.flags_ref, bf16[272,1280]{1,0:T(8,128)(2,1)} %copy-done.3, bf16[2,256,2560]{2,1,0:T(8,128)(2,1)} %copy-done, bf16[256,2560]{1,0:T(8,128)(2,1)} %bitcast.24, bf16[2,256,2560]{2,1,0:T(8,128)(2,1)} %collective-permute-done.3.kr_ref.vr_ref, ...), custom_call_target="tpu_custom_call" | custom-call | flops 1006632960 | bytes 5242880 | tf_op jit(solution)/shard_map/pallas_call | solution.py:92
  47.9 3.7 %shard_map.56.a_ref = bf16[272,1280]{1,0:T(8,128)(2,1)} custom-call(s32[3]{0:T(128)} %add_convert_fusion.flags_ref, bf16[256,1280]{1,0:T(8,128)(2,1)} %collective-permute-done.q_ref, bf16[2,256,2560]{2,1,0:T(8,128)(2,1)} %copy-done, bf16[256,2560]{1,0:T(8,128)(2,1)} %bitcast.25, bf16[2,256,2560]{2,1,0:T(8,128)(2,1)} %collective-permute-done.3.kr_ref.vr_ref, ...), custom_call_target="tpu_custom_call" | custom-call | flops 1006632960 | bytes 5242880 | tf_op jit(solution)/shard_map/pallas_call | solution.py:92
  51.6 5.0 %collective-permute-start.4 = (bf16[256,1280]{1,0:T(8,128)(2,1)}, bf16[256,1280]{1,0:T(8,128)(2,1)S(1)}, u32[]{:S(2)}, u32[]{:S(2)}) collective-permute-start(bf16[256,1280]{1,0:T(8,128)(2,1)} %collective-permute-done.q_ref), channel_id=1, source_target_pairs={{8,0},{16,8},{24,16},{32,24},{40,32},{48,40},{56,48},{64,56},{72,6... | collective-permute-start | bytes 1966088 | tf_op jit(solution)/shard_map/ppermute | solution.py:197
  56.6 4.9 %collective-permute-done.5.q_ref = bf16[272,1280]{1,0:T(8,128)(2,1)} collective-permute-done((bf16[272,1280]{1,0:T(8,128)(2,1)S(1)}, bf16[272,1280]{1,0:T(8,128)(2,1)}, u32[]{:S(2)}, u32[]{:S(2)}) %collective-permute-start.5) | collective-permute-done | bytes 696352 | tf_op jit(solution)/shard_map/ppermute | solution.py:197
  65.4 7.5 %shard_map.57.a_ref = bf16[272,1280]{1,0:T(8,128)(2,1)} custom-call(s32[3]{0:T(128)} %add_convert_fusion.1.flags_ref, bf16[256,2560]{1,0:T(8,128)(2,1)} %bitcast.36, bf16[2,256,2560]{2,1,0:T(8,128)(2,1)} %copy-done, bf16[256,2560]{1,0:T(8,128)(2,1)} %bitcast.26, bf16[2,256,2560]{2,1,0:T(8,128)(2,1)} %collective-permute-done.3.kr_ref.vr_ref, ...), custom_call_target="tpu_custom_call" | custom-call | flops 1006632960 | bytes 5242880 | tf_op jit(solution)/shard_map/pallas_call | solution.py:92
  72.9 7.5 %shard_map.58 = bf16[272,1280]{1,0:T(8,128)(2,1)} custom-call(s32[3]{0:T(128)} %add_convert_fusion.2.flags_ref, bf16[272,1280]{1,0:T(8,128)(2,1)} %collective-permute-done.5.q_ref, bf16[2,256,2560]{2,1,0:T(8,128)(2,1)} %copy-done, bf16[256,2560]{1,0:T(8,128)(2,1)} %bitcast.27, bf16[2,256,2560]{2,1,0:T(8,128)(2,1)} %collective-permute-done.3.kr_ref.vr_ref, ...), custom_call_target="tpu_custom_call" | custom-call | flops 1006632960 | bytes 5242880 | tf_op jit(solution)/shard_map/pallas_call | solution.py:92
  80.5 2.1 %collective-permute-start.8 = (bf16[272,1280]{1,0:T(8,128)(2,1)}, bf16[272,1280]{1,0:T(8,128)(2,1)S(1)}, u32[]{:S(2)}, u32[]{:S(2)}) collective-permute-start(bf16[272,1280]{1,0:T(8,128)(2,1)} %shard_map.58), channel_id=1, source_target_pairs={{0,8},{8,16},{16,24},{24,32},{32,40},{40,48},{48,56},{56,64},{64,7... | collective-permute-start | bytes 2088968 | tf_op jit(solution)/shard_map/ppermute | solution.py:197
  82.6 7.5 %shard_map.59.a_ref = bf16[272,1280]{1,0:T(8,128)(2,1)} custom-call(s32[3]{0:T(128)} %add_convert_fusion.1.flags_ref, bf16[256,2560]{1,0:T(8,128)(2,1)} %bitcast.37, bf16[2,256,2560]{2,1,0:T(8,128)(2,1)} %copy-done, bf16[256,2560]{1,0:T(8,128)(2,1)} %bitcast.28, bf16[2,256,2560]{2,1,0:T(8,128)(2,1)} %collective-permute-done.3.kr_ref.vr_ref, ...), custom_call_target="tpu_custom_call" | custom-call | flops 1006632960 | bytes 5242880 | tf_op jit(solution)/shard_map/pallas_call | solution.py:92
  90.9 7.6 %shard_map.60 = bf16[272,1280]{1,0:T(8,128)(2,1)} custom-call(s32[3]{0:T(128)} %add_convert_fusion.2.flags_ref, bf16[256,1280]{1,0:T(8,128)(2,1)} %copy-done.8, bf16[2,256,2560]{2,1,0:T(8,128)(2,1)} %copy-done, bf16[256,2560]{1,0:T(8,128)(2,1)} %bitcast.29, bf16[2,256,2560]{2,1,0:T(8,128)(2,1)} %collective-permute-done.3.kr_ref.vr_ref, ...), custom_call_target="tpu_custom_call" | custom-call | flops 1006632960 | bytes 5242880 | tf_op jit(solution)/shard_map/pallas_call | solution.py:92
  98.5 1.9 %collective-permute-start.6 = (bf16[272,1280]{1,0:T(8,128)(2,1)}, bf16[272,1280]{1,0:T(8,128)(2,1)S(1)}, u32[]{:S(2)}, u32[]{:S(2)}) collective-permute-start(bf16[272,1280]{1,0:T(8,128)(2,1)} %shard_map.60), channel_id=1, source_target_pairs={{0,8},{8,16},{16,24},{24,32},{32,40},{40,48},{48,56},{56,64},{64,7... | collective-permute-start | bytes 2088968 | tf_op jit(solution)/shard_map/ppermute | solution.py:197
  101.9 2.9 %shard_map.62 = bf16[272,1280]{1,0:T(8,128)(2,1)} custom-call(s32[1]{0:T(128)} %bitcast.valid_ref, bf16[272,1280]{1,0:T(8,128)(2,1)} %shard_map.55.a_ref, bf16[272,1280]{1,0:T(8,128)(2,1)} %copy-done.5), custom_call_target="tpu_custom_call" | custom-call | flops 1310720 | bytes 1966080 | tf_op jit(solution)/shard_map/pallas_call | solution.py:176
  104.8 4.3 %collective-permute-start.9 = (bf16[272,1280]{1,0:T(8,128)(2,1)}, bf16[272,1280]{1,0:T(8,128)(2,1)S(1)}, u32[]{:S(2)}, u32[]{:S(2)}) collective-permute-start(bf16[272,1280]{1,0:T(8,128)(2,1)} %shard_map.62), channel_id=1, source_target_pairs={{0,8},{8,16},{16,24},{24,32},{32,40},{40,48},{48,56},{56,64},{64,7... | collective-permute-start | bytes 2088968 | tf_op jit(solution)/shard_map/ppermute | solution.py:197
  109.1 12.1 %collective-permute-done.6.b_ref = bf16[272,1280]{1,0:T(8,128)(2,1)S(1)} collective-permute-done((bf16[272,1280]{1,0:T(8,128)(2,1)}, bf16[272,1280]{1,0:T(8,128)(2,1)S(1)}, u32[]{:S(2)}, u32[]{:S(2)}) %collective-permute-start.6) | collective-permute-done | bytes 696352 | tf_op jit(solution)/shard_map/ppermute | solution.py:197
  122.1 2.9 %shard_map.61 = bf16[272,1280]{1,0:T(8,128)(2,1)} custom-call(s32[1]{0:T(128)} %bitcast.valid_ref, bf16[272,1280]{1,0:T(8,128)(2,1)} %shard_map.56.a_ref, bf16[272,1280]{1,0:T(8,128)(2,1)} %copy-done.6), custom_call_target="tpu_custom_call" | custom-call | flops 1310720 | bytes 1966080 | tf_op jit(solution)/shard_map/pallas_call | solution.py:176
  127.0 9.2 %collective-permute-done.9.b_ref = bf16[272,1280]{1,0:T(8,128)(2,1)S(1)} collective-permute-done((bf16[272,1280]{1,0:T(8,128)(2,1)}, bf16[272,1280]{1,0:T(8,128)(2,1)S(1)}, u32[]{:S(2)}, u32[]{:S(2)}) %collective-permute-start.9) | collective-permute-done | bytes 696352 | tf_op jit(solution)/shard_map/ppermute | solution.py:197
  137.1 2.9 %shard_map.63.rest_0_ = bf16[256,2560]{1,0:T(8,128)(2,1)} custom-call(s32[1]{0:T(128)} %bitcast.valid_ref, bf16[272,1280]{1,0:T(8,128)(2,1)} %shard_map.57.a_ref, bf16[272,1280]{1,0:T(8,128)(2,1)} %copy-done.4), custom_call_target="tpu_custom_call" | custom-call | flops 1310720 | bytes 1966080 | tf_op jit(solution)/shard_map/pallas_call | solution.py:176
  140.0 9.0 %collective-permute-done.7.b_ref = bf16[272,1280]{1,0:T(8,128)(2,1)S(1)} collective-permute-done((bf16[272,1280]{1,0:T(8,128)(2,1)}, bf16[272,1280]{1,0:T(8,128)(2,1)S(1)}, u32[]{:S(2)}, u32[]{:S(2)}) %collective-permute-start.7) | collective-permute-done | bytes 696352 | tf_op jit(solution)/shard_map/ppermute | solution.py:197
  149.8 2.9 %shard_map.64 = bf16[256,2560]{1,0:T(8,128)(2,1)} custom-call(s32[1]{0:T(128)} %bitcast.valid_ref, bf16[272,1280]{1,0:T(8,128)(2,1)} %shard_map.59.a_ref, bf16[272,1280]{1,0:T(8,128)(2,1)} %copy-done.7, bf16[256,2560]{1,0:T(8,128)(2,1)} %shard_map.63.rest_0_), custom_call_target="tpu_custom_call", output_to_operand_aliasing={{}: (3, {})} | custom-call | flops 1310720 | bytes 1966080 | tf_op jit(solution)/shard_map/pallas_call | solution.py:176
  (41 shorter events, 17.9 us)
Async XLA Ops:
  0.0 2.6 %copy-start.1 = (bf16[1,256,2560]{2,1,0:T(8,128)(2,1)S(1)}, bf16[1,256,2560]{2,1,0:T(8,128)(2,1)}, u32[]{:S(2)}) copy-start(bf16[1,256,2560]{2,1,0:T(8,128)(2,1)} %param.9) | copy-start | bytes 3932164
  2.6 7.4 %copy-start.9 = (s32[1,1,2]{2,1,0:T(1,128)S(1)}, s32[1,1,2]{2,1,0:T(1,128)}, u32[]{:S(2)}) copy-start(s32[1,1,2]{2,1,0:T(1,128)} %param.11) | copy-start | bytes 28
  2.6 7.5 %copy-start.2 = (bf16[1,256,2560]{2,1,0:T(8,128)(2,1)S(1)}, bf16[1,256,2560]{2,1,0:T(8,128)(2,1)}, u32[]{:S(2)}) copy-start(bf16[1,256,2560]{2,1,0:T(8,128)(2,1)} %param.7) | copy-start | bytes 3932164
  3.8 38.8 %collective-permute-start.2 = (bf16[2,256,2560]{2,1,0:T(8,128)(2,1)}, bf16[2,256,2560]{2,1,0:T(8,128)(2,1)S(1)}, u32[]{:S(2)}, u32[]{:S(2)}) collective-permute-start(bf16[2,256,2560]{2,1,0:T(8,128)(2,1)} %constant_dynamic-update-slice_fusion), channel_id=1, source_target_pairs={{0,1},{1,2},{2,3},{3,4},{4,5},{5,6},{6,7},{8,9},{9,10},{10,11},{11... | collective-permute-start | bytes 7864328 | tf_op jit(solution)/shard_map/ppermute | solution.py:230
  5.7 36.9 %collective-permute-start.3 = (bf16[2,256,2560]{2,1,0:T(8,128)(2,1)}, bf16[2,256,2560]{2,1,0:T(8,128)(2,1)}, u32[]{:S(2)}, u32[]{:S(2)}) collective-permute-start(bf16[2,256,2560]{2,1,0:T(8,128)(2,1)} %constant_dynamic-update-slice_fusion), channel_id=1, source_target_pairs={{1,0},{2,1},{3,2},{4,3},{5,4},{6,5},{7,6},{9,8},{10,9},{11,10},{12... | collective-permute-start | bytes 7864328 | tf_op jit(solution)/shard_map/ppermute | solution.py:231
  11.9 20.5 %collective-permute-start.1 = (bf16[272,1280]{1,0:T(8,128)(2,1)}, bf16[272,1280]{1,0:T(8,128)(2,1)S(1)}, u32[]{:S(2)}, u32[]{:S(2)}) collective-permute-start(bf16[272,1280]{1,0:T(8,128)(2,1)} %pad_maximum_fusion), channel_id=1, source_target_pairs={{8,0},{16,8},{24,16},{32,24},{40,32},{48,40},{56,48},{64,56},{72,6... | collective-permute-start | bytes 2088968 | tf_op jit(solution)/shard_map/ppermute | solution.py:197
  16.1 31.8 %collective-permute-start = (bf16[256,1280]{1,0:T(8,128)(2,1)}, bf16[256,1280]{1,0:T(8,128)(2,1)}, u32[]{:S(2)}, u32[]{:S(2)}) collective-permute-start(bf16[256,1280]{1,0:T(8,128)(2,1)} %get-tuple-element.38), channel_id=1, source_target_pairs={{8,0},{16,8},{24,16},{32,24},{40,32},{48,40},{56,48},{64,56},{72,6... | collective-permute-start | bytes 1966088 | tf_op jit(solution)/shard_map/ppermute | solution.py:197
  32.4 10.1 %copy-start.3 = (bf16[272,1280]{1,0:T(8,128)(2,1)}, bf16[272,1280]{1,0:T(8,128)(2,1)S(1)}, u32[]{:S(2)}) copy-start(bf16[272,1280]{1,0:T(8,128)(2,1)S(1)} %collective-permute-done.1.q_ref) | copy-start | bytes 2088964
  32.5 29.1 %collective-permute-start.5 = (bf16[272,1280]{1,0:T(8,128)(2,1)S(1)}, bf16[272,1280]{1,0:T(8,128)(2,1)}, u32[]{:S(2)}, u32[]{:S(2)}) collective-permute-start(bf16[272,1280]{1,0:T(8,128)(2,1)S(1)} %collective-permute-done.1.q_ref), channel_id=1, source_target_pairs={{8,0},{16,8},{24,16},{32,24},{40,32},{48,40},{56,48},{64,56},{72,6... | collective-permute-start | bytes 2088968 | tf_op jit(solution)/shard_map/ppermute | solution.py:197
  42.6 1.6 %copy-start = (bf16[2,256,2560]{2,1,0:T(8,128)(2,1)}, bf16[2,256,2560]{2,1,0:T(8,128)(2,1)S(1)}, u32[]{:S(2)}) copy-start(bf16[2,256,2560]{2,1,0:T(8,128)(2,1)S(1)} %collective-permute-done.2.kl_ref.vl_ref) | copy-start | bytes 7864324
  51.6 38.5 %collective-permute-start.4 = (bf16[256,1280]{1,0:T(8,128)(2,1)}, bf16[256,1280]{1,0:T(8,128)(2,1)S(1)}, u32[]{:S(2)}, u32[]{:S(2)}) collective-permute-start(bf16[256,1280]{1,0:T(8,128)(2,1)} %collective-permute-done.q_ref), channel_id=1, source_target_pairs={{8,0},{16,8},{24,16},{32,24},{40,32},{48,40},{56,48},{64,56},{72,6... | collective-permute-start | bytes 1966088 | tf_op jit(solution)/shard_map/ppermute | solution.py:197
  80.5 20.6 %collective-permute-start.8 = (bf16[272,1280]{1,0:T(8,128)(2,1)}, bf16[272,1280]{1,0:T(8,128)(2,1)S(1)}, u32[]{:S(2)}, u32[]{:S(2)}) collective-permute-start(bf16[272,1280]{1,0:T(8,128)(2,1)} %shard_map.58), channel_id=1, source_target_pairs={{0,8},{8,16},{16,24},{24,32},{32,40},{40,48},{48,56},{56,64},{64,7... | collective-permute-start | bytes 2088968 | tf_op jit(solution)/shard_map/ppermute | solution.py:197
  90.1 0.8 copy-start.8
  98.5 22.8 %collective-permute-start.6 = (bf16[272,1280]{1,0:T(8,128)(2,1)}, bf16[272,1280]{1,0:T(8,128)(2,1)S(1)}, u32[]{:S(2)}, u32[]{:S(2)}) collective-permute-start(bf16[272,1280]{1,0:T(8,128)(2,1)} %shard_map.60), channel_id=1, source_target_pairs={{0,8},{8,16},{16,24},{24,32},{32,40},{40,48},{48,56},{56,64},{64,7... | collective-permute-start | bytes 2088968 | tf_op jit(solution)/shard_map/ppermute | solution.py:197
  101.0 0.9 copy-start.5
  104.8 31.4 %collective-permute-start.9 = (bf16[272,1280]{1,0:T(8,128)(2,1)}, bf16[272,1280]{1,0:T(8,128)(2,1)S(1)}, u32[]{:S(2)}, u32[]{:S(2)}) collective-permute-start(bf16[272,1280]{1,0:T(8,128)(2,1)} %shard_map.62), channel_id=1, source_target_pairs={{0,8},{8,16},{16,24},{24,32},{32,40},{40,48},{48,56},{56,64},{64,7... | collective-permute-start | bytes 2088968 | tf_op jit(solution)/shard_map/ppermute | solution.py:197
  121.3 0.9 copy-start.6
  125.1 23.8 %collective-permute-start.7 = (bf16[272,1280]{1,0:T(8,128)(2,1)}, bf16[272,1280]{1,0:T(8,128)(2,1)S(1)}, u32[]{:S(2)}, u32[]{:S(2)}) collective-permute-start(bf16[272,1280]{1,0:T(8,128)(2,1)} %shard_map.61), channel_id=1, source_target_pairs={{0,8},{8,16},{16,24},{24,32},{32,40},{40,48},{48,56},{56,64},{64,7... | collective-permute-start | bytes 2088968 | tf_op jit(solution)/shard_map/ppermute | solution.py:197
  136.2 0.9 copy-start.4
  148.9 0.9 copy-start.7

commit v6 on v3

--- a/solution.py
+++ b/solution.py
@@ -224,33 +224,39 @@
     meta_rows = jnp.zeros((EXTRA, chunk_w), jnp.bfloat16).at[0, 0:3].set(meta)
     sends = [jnp.concatenate([q[:, :chunk_w], meta_rows], axis=0)]
     sends += [q[:, c * chunk_w : (c + 1) * chunk_w] for c in range(1, CHUNKS)]
-    q1s = [shift_tm(x, -1) for x in sends]
+    q1s = [shift_tm(sends[0], -1)]
 
     kv = jnp.stack([k, v])
     kv_l = lax.ppermute(kv, "space", [(i, i + 1) for i in range(tiles - 1)])
     kv_r = lax.ppermute(kv, "space", [(i + 1, i) for i in range(tiles - 1)])
 
     f1 = flags_for(q1s[0][rows, 0:3], 1)
-    p1s, q2s = [], []
-    for c in range(CHUNKS):
-        p1 = attend(f1, q1s[c], k, v, kv_l, kv_r, chunk_w, c * groups_c, 0)
-        relay, p1 = lax.optimization_barrier((q1s[c], p1))
-        p1s.append(p1)
-        q2s.append(shift_tm(relay, -1))
-
+    f0 = flags_for(meta, 0)
     valid = (seg >= 1).astype(jnp.int32).reshape(1)
-    f0 = flags_for(meta, 0)
-    f2 = flags_for(q2s[0][rows, 0:3], 2)
     result = None
-    q_self = q
+    q_pa, q_self = q1s[0], q
+    q2_prev = shift_tm(q1s[0], -1)
+    f2 = flags_for(q2_prev[rows, 0:3], 2)
     for c in range(CHUNKS):
         base = c * groups_c
+        if c == 0:
+            q2 = q2_prev
+        else:
+            held, _ = lax.optimization_barrier((sends[c], q2_prev))
+            q1 = shift_tm(held, -1)
+            q_pa, _ = lax.optimization_barrier((q1, p2))
+            q_relay = q1
+        p1 = attend(f1, q_pa, k, v, kv_l, kv_r, chunk_w, base, 0)
+        if c > 0:
+            q_relay, p1 = lax.optimization_barrier((q_relay, p1))
+            q2 = shift_tm(q_relay, -1)
         p_self = attend(f0, q_self, k, v, kv_l, kv_r, chunk_w, base, base)
-        q2, p_self = lax.optimization_barrier((q2s[c], p_self))
+        q2, p_self, p1 = lax.optimization_barrier((q2, p_self, p1))
         p2 = attend(f2, q2, k, v, kv_l, kv_r, chunk_w, base, 0)
         q_self, p2 = lax.optimization_barrier((q, p2))
+        q2_prev = q2
         p2_in = shift_tm(p2, 1)
-        pc = merge(valid, p1s[c], p2_in, 0)
+        pc = merge(valid, p1, p2_in, 0)
         pc_in = shift_tm(pc, 1)
         result = merge(valid, p_self, pc_in, base, final=True, buf=result, out_width=width)
     return result.reshape(1, rows, width)

time: 158 us -> 167 us (1.057)
  waiting for transfers between devices: 51.7 us -> 55.3 us
  local copies, waits for them, and re-layouts: 11.1 us -> 13.5 us
  starting transfers between devices: 27.4 us -> 29.3 us
    ppermute x8, waiting for transfers between devices: 48.7 us -> 55.3 us  [shift_tm(): return lax.ppermute(x, 'tm', pairs)]
    ppermute x8, starting transfers between devices: 21.9 us -> 24.9 us  [shift_tm(): return lax.ppermute(x, 'tm', pairs)]
    unnamed x23 -> x27, local copies, waits for them, and re-layouts: 6.99 us -> 9.41 us
    ppermute x1, waiting for transfers between devices: 1.86 us -> 0.01 us  [on_device(): kv_r = lax.ppermute(kv, 'space', [(i + 1, i) for i in range(tiles - 1)])]
    ppermute x1, starting transfers between devices: 3.64 us -> 1.91 us  [on_device(): kv_r = lax.ppermute(kv, 'space', [(i + 1, i) for i in range(tiles - 1)])]
  transfers between devices with their start and end apart: 10 -> 10, of which waited for: 7 -> 6; matrix products, arithmetic and copies ran while one was open for 4% -> 4% of each run, Pallas kernels for 35% -> 28%
where the time goes in v6:
time: 167 us; the launch traced here: 166 us
  Pallas kernels  57.1 us (34%)
  waiting for transfers between devices  55.3 us (33%)
  starting transfers between devices  29.3 us (18%)
  local copies, waits for them, and re-layouts  13.5 us (8%)
  between operations  6.84 us (4%)
  other arithmetic  3.61 us (2%)
    ppermute x8, waiting for transfers between devices, shift_tm(): return lax.ppermute(x, 'tm', pairs)  55.3 us
    pallas_call x6, Pallas kernels, attend(): pl.pallas_call(_attn_kernel, out_shape=jax.ShapeDtypeStruct((rows + EXTRA...  45.4 us
    ppermute x8, starting transfers between devices, shift_tm(): return lax.ppermute(x, 'tm', pairs)  24.9 us
    pallas_call x4, Pallas kernels, merge(): pl.pallas_call(kernel, out_shape=out_shape, grid_spec=pltpu.PrefetchScala...  11.7 us
    unnamed x27, local copies, waits for them, and re-layouts  9.41 us
  transfers between devices with their start and end apart: 10, of which 6 were waited for; matrix products, arithmetic and copies ran while one was open for 4% of the time, Pallas kernels for 28%

profile of v6, /device:TPU:112, one launch (start us, length us, event | category | flops | bytes accessed | tf_op | source)
XLA Modules:
  0.0 165.6 jit_solution(1744415330445659809)
XLA Ops:
  0.0 2.6 %constant_dynamic-update-slice_fusion.1 = bf16[2,256,2560]{2,1,0:T(8,128)(2,1)} fusion(bf16[1,256,2560]{2,1,0:T(8,128)(2,1)} %param.8), kind=kLoop, calls=%fused_computation.10 | loop fusion | bytes 2621440
  3.8 1.9 %collective-permute-start.3 = (bf16[2,256,2560]{2,1,0:T(8,128)(2,1)}, bf16[2,256,2560]{2,1,0:T(8,128)(2,1)S(1)}, u32[]{:S(2)}, u32[]{:S(2)}) collective-permute-start(bf16[2,256,2560]{2,1,0:T(8,128)(2,1)} %constant_dynamic-update-slice_fusion), channel_id=1, source_target_pairs={{1,0},{2,1},{3,2},{4,3},{5,4},{6,5},{7,6},{9,8},{10,9},{11,10},{12... | collective-permute-start | bytes 7864328 | tf_op jit(solution)/shard_map/ppermute | solution.py:231
  5.7 2.4 %collective-permute-start.2 = (bf16[2,256,2560]{2,1,0:T(8,128)(2,1)}, bf16[2,256,2560]{2,1,0:T(8,128)(2,1)}, u32[]{:S(2)}, u32[]{:S(2)}) collective-permute-start(bf16[2,256,2560]{2,1,0:T(8,128)(2,1)} %constant_dynamic-update-slice_fusion), channel_id=1, source_target_pairs={{0,1},{1,2},{2,3},{3,4},{4,5},{5,6},{6,7},{8,9},{9,10},{10,11},{11... | collective-permute-start | bytes 7864328 | tf_op jit(solution)/shard_map/ppermute | solution.py:230
  10.7 4.5 %collective-permute-start = (bf16[272,1280]{1,0:T(8,128)(2,1)}, bf16[272,1280]{1,0:T(8,128)(2,1)S(1)}, u32[]{:S(2)}, u32[]{:S(2)}) collective-permute-start(bf16[272,1280]{1,0:T(8,128)(2,1)} %pad_maximum_fusion), channel_id=1, source_target_pairs={{8,0},{16,8},{24,16},{32,24},{40,32},{48,40},{56,48},{64,56},{72,6... | collective-permute-start | bytes 2088968 | tf_op jit(solution)/shard_map/ppermute | solution.py:197
  17.9 13.5 %collective-permute-done.q_ref = bf16[272,1280]{1,0:T(8,128)(2,1)S(1)} collective-permute-done((bf16[272,1280]{1,0:T(8,128)(2,1)}, bf16[272,1280]{1,0:T(8,128)(2,1)S(1)}, u32[]{:S(2)}, u32[]{:S(2)}) %collective-permute-start) | collective-permute-done | bytes 696352 | tf_op jit(solution)/shard_map/ppermute | solution.py:197
  31.4 6.4 %collective-permute-start.1 = (bf16[272,1280]{1,0:T(8,128)(2,1)S(1)}, bf16[272,1280]{1,0:T(8,128)(2,1)}, u32[]{:S(2)}, u32[]{:S(2)}) collective-permute-start(bf16[272,1280]{1,0:T(8,128)(2,1)S(1)} %collective-permute-done.q_ref), channel_id=1, source_target_pairs={{8,0},{16,8},{24,16},{32,24},{40,32},{48,40},{56,48},{64,56},{72,6... | collective-permute-start | bytes 2088968 | tf_op jit(solution)/shard_map/ppermute | solution.py:197
  43.4 7.5 %shard_map.56.a_ref = bf16[272,1280]{1,0:T(8,128)(2,1)} custom-call(s32[3]{0:T(128)} %add_convert_fusion.1.flags_ref, bf16[272,1280]{1,0:T(8,128)(2,1)} %copy-done.3, bf16[2,256,2560]{2,1,0:T(8,128)(2,1)} %collective-permute-done.2.kl_ref.vl_ref, bf16[256,2560]{1,0:T(8,128)(2,1)} %bitcast.24, bf16[2,256,2560]{2,1,0:T(8,128)(2,1)} %copy-done, ...), custom_call_target="tpu_custom_call" | custom-call | flops 1006632960 | bytes 5242880 | tf_op jit(solution)/shard_map/pallas_call | solution.py:92
  50.9 7.7 %shard_map.55.a_ref = bf16[272,1280]{1,0:T(8,128)(2,1)} custom-call(s32[3]{0:T(128)} %add_convert_fusion.flags_ref, bf16[256,2560]{1,0:T(8,128)(2,1)} %bitcast.36, bf16[2,256,2560]{2,1,0:T(8,128)(2,1)} %collective-permute-done.2.kl_ref.vl_ref, bf16[256,2560]{1,0:T(8,128)(2,1)} %bitcast.25, bf16[2,256,2560]{2,1,0:T(8,128)(2,1)} %copy-done, ...), custom_call_target="tpu_custom_call" | custom-call | flops 1006632960 | bytes 5242880 | tf_op jit(solution)/shard_map/pallas_call | solution.py:92
  58.6 1.9 %collective-permute-start.4 = (bf16[256,1280]{1,0:T(8,128)(2,1)S(1)}, bf16[256,1280]{1,0:T(8,128)(2,1)S(1)}, u32[]{:S(2)}, u32[]{:S(2)}) collective-permute-start(bf16[256,1280]{1,0:T(8,128)(2,1)S(1)} %copy-done.9), channel_id=1, source_target_pairs={{8,0},{16,8},{24,16},{32,24},{40,32},{48,40},{56,48},{64,56},{72,6... | collective-permute-start | bytes 1966088 | tf_op jit(solution)/shard_map/ppermute | solution.py:197
  64.5 7.5 %shard_map.57 = bf16[272,1280]{1,0:T(8,128)(2,1)} custom-call(s32[3]{0:T(128)} %add_convert_fusion.2.flags_ref, bf16[272,1280]{1,0:T(8,128)(2,1)} %collective-permute-done.1.q_ref, bf16[2,256,2560]{2,1,0:T(8,128)(2,1)} %collective-permute-done.2.kl_ref.vl_ref, bf16[256,2560]{1,0:T(8,128)(2,1)} %bitcast.26, bf16[2,256,2560]{2,1,0:T(8,128)(2,1)} %copy-done, ...), custom_call_target="tpu_custom_call" | custom-call | flops 1006632960 | bytes 5242880 | tf_op jit(solution)/shard_map/pallas_call | solution.py:92
  72.0 5.0 %collective-permute-done.4.q_ref = bf16[256,1280]{1,0:T(8,128)(2,1)S(1)} collective-permute-done((bf16[256,1280]{1,0:T(8,128)(2,1)S(1)}, bf16[256,1280]{1,0:T(8,128)(2,1)S(1)}, u32[]{:S(2)}, u32[]{:S(2)}) %collective-permute-start.4) | collective-permute-done | bytes 655392 | tf_op jit(solution)/shard_map/ppermute | solution.py:197
  77.9 7.5 %shard_map.58.a_ref = bf16[272,1280]{1,0:T(8,128)(2,1)} custom-call(s32[3]{0:T(128)} %add_convert_fusion.1.flags_ref, bf16[256,1280]{1,0:T(8,128)(2,1)} %copy-done.10, bf16[2,256,2560]{2,1,0:T(8,128)(2,1)} %collective-permute-done.2.kl_ref.vl_ref, bf16[256,2560]{1,0:T(8,128)(2,1)} %bitcast.27, bf16[2,256,2560]{2,1,0:T(8,128)(2,1)} %copy-done, ...), custom_call_target="tpu_custom_call" | custom-call | flops 1006632960 | bytes 5242880 | tf_op jit(solution)/shard_map/pallas_call | solution.py:92
  85.4 4.3 %collective-permute-start.5 = (bf16[256,1280]{1,0:T(8,128)(2,1)}, bf16[256,1280]{1,0:T(8,128)(2,1)S(1)}, u32[]{:S(2)}, u32[]{:S(2)}) collective-permute-start(bf16[256,1280]{1,0:T(8,128)(2,1)} %copy-done.10), channel_id=1, source_target_pairs={{8,0},{16,8},{24,16},{32,24},{40,32},{48,40},{56,48},{64,56},{72,6... | collective-permute-start | bytes 1966088 | tf_op jit(solution)/shard_map/ppermute | solution.py:197
  89.7 2.1 %collective-permute-start.8 = (bf16[272,1280]{1,0:T(8,128)(2,1)S(1)}, bf16[272,1280]{1,0:T(8,128)(2,1)S(1)}, u32[]{:S(2)}, u32[]{:S(2)}) collective-permute-start(bf16[272,1280]{1,0:T(8,128)(2,1)S(1)} %copy-done.4), channel_id=1, source_target_pairs={{0,8},{8,16},{16,24},{24,32},{32,40},{40,48},{48,56},{56,64},{64,7... | collective-permute-start | bytes 2088968 | tf_op jit(solution)/shard_map/ppermute | solution.py:197
  91.8 7.5 %shard_map.59.a_ref = bf16[272,1280]{1,0:T(8,128)(2,1)} custom-call(s32[3]{0:T(128)} %add_convert_fusion.flags_ref, bf16[256,2560]{1,0:T(8,128)(2,1)} %bitcast.37, bf16[2,256,2560]{2,1,0:T(8,128)(2,1)} %collective-permute-done.2.kl_ref.vl_ref, bf16[256,2560]{1,0:T(8,128)(2,1)} %bitcast.28, bf16[2,256,2560]{2,1,0:T(8,128)(2,1)} %copy-done, ...), custom_call_target="tpu_custom_call" | custom-call | flops 1006632960 | bytes 5242880 | tf_op jit(solution)/shard_map/pallas_call | solution.py:92
  99.4 4.1 %collective-permute-done.5.q_ref = bf16[256,1280]{1,0:T(8,128)(2,1)S(1)} collective-permute-done((bf16[256,1280]{1,0:T(8,128)(2,1)}, bf16[256,1280]{1,0:T(8,128)(2,1)S(1)}, u32[]{:S(2)}, u32[]{:S(2)}) %collective-permute-start.5) | collective-permute-done | bytes 655392 | tf_op jit(solution)/shard_map/ppermute | solution.py:197
  104.3 7.6 %shard_map.60 = bf16[272,1280]{1,0:T(8,128)(2,1)} custom-call(s32[3]{0:T(128)} %add_convert_fusion.2.flags_ref, bf16[256,1280]{1,0:T(8,128)(2,1)} %copy-done.11, bf16[2,256,2560]{2,1,0:T(8,128)(2,1)} %collective-permute-done.2.kl_ref.vl_ref, bf16[256,2560]{1,0:T(8,128)(2,1)} %bitcast.29, bf16[2,256,2560]{2,1,0:T(8,128)(2,1)} %copy-done, ...), custom_call_target="tpu_custom_call" | custom-call | flops 1006632960 | bytes 5242880 | tf_op jit(solution)/shard_map/pallas_call | solution.py:92
  114.7 2.9 %shard_map.62 = bf16[272,1280]{1,0:T(8,128)(2,1)} custom-call(s32[1]{0:T(128)} %bitcast.valid_ref, bf16[272,1280]{1,0:T(8,128)(2,1)} %shard_map.56.a_ref, bf16[272,1280]{1,0:T(8,128)(2,1)} %copy-done.6), custom_call_target="tpu_custom_call" | custom-call | flops 1310720 | bytes 1966080 | tf_op jit(solution)/shard_map/pallas_call | solution.py:176
  119.6 15.1 %collective-permute-done.6.b_ref = bf16[272,1280]{1,0:T(8,128)(2,1)S(1)} collective-permute-done((bf16[272,1280]{1,0:T(8,128)(2,1)}, bf16[272,1280]{1,0:T(8,128)(2,1)S(1)}, u32[]{:S(2)}, u32[]{:S(2)}) %collective-permute-start.6) | collective-permute-done | bytes 696352 | tf_op jit(solution)/shard_map/ppermute | solution.py:197
  135.5 2.9 %shard_map.61 = bf16[272,1280]{1,0:T(8,128)(2,1)} custom-call(s32[1]{0:T(128)} %bitcast.valid_ref, bf16[272,1280]{1,0:T(8,128)(2,1)} %shard_map.58.a_ref, bf16[272,1280]{1,0:T(8,128)(2,1)} %copy-done.7), custom_call_target="tpu_custom_call" | custom-call | flops 1310720 | bytes 1966080 | tf_op jit(solution)/shard_map/pallas_call | solution.py:176
  140.4 9.2 %collective-permute-done.9.b_ref = bf16[272,1280]{1,0:T(8,128)(2,1)S(1)} collective-permute-done((bf16[272,1280]{1,0:T(8,128)(2,1)}, bf16[272,1280]{1,0:T(8,128)(2,1)S(1)}, u32[]{:S(2)}, u32[]{:S(2)}) %collective-permute-start.9) | collective-permute-done | bytes 696352 | tf_op jit(solution)/shard_map/ppermute | solution.py:197
  150.4 2.9 %shard_map.63.rest_0_ = bf16[256,2560]{1,0:T(8,128)(2,1)} custom-call(s32[1]{0:T(128)} %bitcast.valid_ref, bf16[272,1280]{1,0:T(8,128)(2,1)} %shard_map.55.a_ref, bf16[272,1280]{1,0:T(8,128)(2,1)} %copy-done.5), custom_call_target="tpu_custom_call" | custom-call | flops 1310720 | bytes 1966080 | tf_op jit(solution)/shard_map/pallas_call | solution.py:176
  153.3 8.5 %collective-permute-done.7.b_ref = bf16[272,1280]{1,0:T(8,128)(2,1)S(1)} collective-permute-done((bf16[272,1280]{1,0:T(8,128)(2,1)}, bf16[272,1280]{1,0:T(8,128)(2,1)S(1)}, u32[]{:S(2)}, u32[]{:S(2)}) %collective-permute-start.7) | collective-permute-done | bytes 696352 | tf_op jit(solution)/shard_map/ppermute | solution.py:197
  162.7 2.9 %shard_map.64 = bf16[256,2560]{1,0:T(8,128)(2,1)} custom-call(s32[1]{0:T(128)} %bitcast.valid_ref, bf16[272,1280]{1,0:T(8,128)(2,1)} %shard_map.59.a_ref, bf16[272,1280]{1,0:T(8,128)(2,1)} %copy-done.8, bf16[256,2560]{1,0:T(8,128)(2,1)} %shard_map.63.rest_0_), custom_call_target="tpu_custom_call", output_to_operand_aliasing={{}: (3, {})} | custom-call | flops 1310720 | bytes 1966080 | tf_op jit(solution)/shard_map/pallas_call | solution.py:176
  (47 shorter events, 20.3 us)
Async XLA Ops:
  0.0 2.6 %copy-start.1 = (bf16[1,256,2560]{2,1,0:T(8,128)(2,1)S(1)}, bf16[1,256,2560]{2,1,0:T(8,128)(2,1)}, u32[]{:S(2)}) copy-start(bf16[1,256,2560]{2,1,0:T(8,128)(2,1)} %param.9) | copy-start | bytes 3932164
  2.6 6.1 %copy-start.12 = (s32[1,1,2]{2,1,0:T(1,128)S(1)}, s32[1,1,2]{2,1,0:T(1,128)}, u32[]{:S(2)}) copy-start(s32[1,1,2]{2,1,0:T(1,128)} %param.11) | copy-start | bytes 28
  2.6 6.2 %copy-start.2 = (bf16[1,256,2560]{2,1,0:T(8,128)(2,1)S(1)}, bf16[1,256,2560]{2,1,0:T(8,128)(2,1)}, u32[]{:S(2)}) copy-start(bf16[1,256,2560]{2,1,0:T(8,128)(2,1)} %param.7) | copy-start | bytes 3932164
  3.8 38.1 %collective-permute-start.3 = (bf16[2,256,2560]{2,1,0:T(8,128)(2,1)}, bf16[2,256,2560]{2,1,0:T(8,128)(2,1)S(1)}, u32[]{:S(2)}, u32[]{:S(2)}) collective-permute-start(bf16[2,256,2560]{2,1,0:T(8,128)(2,1)} %constant_dynamic-update-slice_fusion), channel_id=1, source_target_pairs={{1,0},{2,1},{3,2},{4,3},{5,4},{6,5},{7,6},{9,8},{10,9},{11,10},{12... | collective-permute-start | bytes 7864328 | tf_op jit(solution)/shard_map/ppermute | solution.py:231
  5.7 36.2 %collective-permute-start.2 = (bf16[2,256,2560]{2,1,0:T(8,128)(2,1)}, bf16[2,256,2560]{2,1,0:T(8,128)(2,1)}, u32[]{:S(2)}, u32[]{:S(2)}) collective-permute-start(bf16[2,256,2560]{2,1,0:T(8,128)(2,1)} %constant_dynamic-update-slice_fusion), channel_id=1, source_target_pairs={{0,1},{1,2},{2,3},{3,4},{4,5},{5,6},{6,7},{8,9},{9,10},{10,11},{11... | collective-permute-start | bytes 7864328 | tf_op jit(solution)/shard_map/ppermute | solution.py:230
  10.7 20.7 %collective-permute-start = (bf16[272,1280]{1,0:T(8,128)(2,1)}, bf16[272,1280]{1,0:T(8,128)(2,1)S(1)}, u32[]{:S(2)}, u32[]{:S(2)}) collective-permute-start(bf16[272,1280]{1,0:T(8,128)(2,1)} %pad_maximum_fusion), channel_id=1, source_target_pairs={{8,0},{16,8},{24,16},{32,24},{40,32},{48,40},{56,48},{64,56},{72,6... | collective-permute-start | bytes 2088968 | tf_op jit(solution)/shard_map/ppermute | solution.py:197
  31.4 10.4 %copy-start.3 = (bf16[272,1280]{1,0:T(8,128)(2,1)}, bf16[272,1280]{1,0:T(8,128)(2,1)S(1)}, u32[]{:S(2)}) copy-start(bf16[272,1280]{1,0:T(8,128)(2,1)S(1)} %collective-permute-done.q_ref) | copy-start | bytes 2088964
  31.4 27.2 %collective-permute-start.1 = (bf16[272,1280]{1,0:T(8,128)(2,1)S(1)}, bf16[272,1280]{1,0:T(8,128)(2,1)}, u32[]{:S(2)}, u32[]{:S(2)}) collective-permute-start(bf16[272,1280]{1,0:T(8,128)(2,1)S(1)} %collective-permute-done.q_ref), channel_id=1, source_target_pairs={{8,0},{16,8},{24,16},{32,24},{40,32},{48,40},{56,48},{64,56},{72,6... | collective-permute-start | bytes 2088968 | tf_op jit(solution)/shard_map/ppermute | solution.py:197
  41.8 1.6 copy-start
  50.9 7.7 %copy-start.9 = (bf16[256,1280]{1,0:T(8,128)(2,1)S(1)}, bf16[256,1280]{1,0:T(8,128)(2,1)}, u32[]{:S(2)}) copy-start(bf16[256,1280]{1,0:T(8,128)(2,1)} %get-tuple-element.31) | copy-start | bytes 1966084
  58.6 18.4 %collective-permute-start.4 = (bf16[256,1280]{1,0:T(8,128)(2,1)S(1)}, bf16[256,1280]{1,0:T(8,128)(2,1)S(1)}, u32[]{:S(2)}, u32[]{:S(2)}) collective-permute-start(bf16[256,1280]{1,0:T(8,128)(2,1)S(1)} %copy-done.9), channel_id=1, source_target_pairs={{8,0},{16,8},{24,16},{32,24},{40,32},{48,40},{56,48},{64,56},{72,6... | collective-permute-start | bytes 1966088 | tf_op jit(solution)/shard_map/ppermute | solution.py:197
  72.0 17.7 %copy-start.4 = (bf16[272,1280]{1,0:T(8,128)(2,1)S(1)}, bf16[272,1280]{1,0:T(8,128)(2,1)}, u32[]{:S(2)}) copy-start(bf16[272,1280]{1,0:T(8,128)(2,1)} %shard_map.57) | copy-start | bytes 2088964
  77.0 0.9 copy-start.10
  85.4 18.0 %collective-permute-start.5 = (bf16[256,1280]{1,0:T(8,128)(2,1)}, bf16[256,1280]{1,0:T(8,128)(2,1)S(1)}, u32[]{:S(2)}, u32[]{:S(2)}) collective-permute-start(bf16[256,1280]{1,0:T(8,128)(2,1)} %copy-done.10), channel_id=1, source_target_pairs={{8,0},{16,8},{24,16},{32,24},{40,32},{48,40},{56,48},{64,56},{72,6... | collective-permute-start | bytes 1966088 | tf_op jit(solution)/shard_map/ppermute | solution.py:197
  89.7 24.1 %collective-permute-start.8 = (bf16[272,1280]{1,0:T(8,128)(2,1)S(1)}, bf16[272,1280]{1,0:T(8,128)(2,1)S(1)}, u32[]{:S(2)}, u32[]{:S(2)}) collective-permute-start(bf16[272,1280]{1,0:T(8,128)(2,1)S(1)} %copy-done.4), channel_id=1, source_target_pairs={{0,8},{8,16},{16,24},{24,32},{32,40},{40,48},{48,56},{56,64},{64,7... | collective-permute-start | bytes 2088968 | tf_op jit(solution)/shard_map/ppermute | solution.py:197
  103.4 0.9 copy-start.11
  111.9 22.8 %collective-permute-start.6 = (bf16[272,1280]{1,0:T(8,128)(2,1)}, bf16[272,1280]{1,0:T(8,128)(2,1)S(1)}, u32[]{:S(2)}, u32[]{:S(2)}) collective-permute-start(bf16[272,1280]{1,0:T(8,128)(2,1)} %shard_map.60), channel_id=1, source_target_pairs={{0,8},{8,16},{16,24},{24,32},{32,40},{40,48},{48,56},{56,64},{64,7... | collective-permute-start | bytes 2088968 | tf_op jit(solution)/shard_map/ppermute | solution.py:197
  113.8 0.9 copy-start.6
  117.7 31.9 %collective-permute-start.9 = (bf16[272,1280]{1,0:T(8,128)(2,1)}, bf16[272,1280]{1,0:T(8,128)(2,1)S(1)}, u32[]{:S(2)}, u32[]{:S(2)}) collective-permute-start(bf16[272,1280]{1,0:T(8,128)(2,1)} %shard_map.62), channel_id=1, source_target_pairs={{0,8},{8,16},{16,24},{24,32},{32,40},{40,48},{48,56},{56,64},{64,7... | collective-permute-start | bytes 2088968 | tf_op jit(solution)/shard_map/ppermute | solution.py:197
  134.6 0.9 copy-start.7
  138.5 23.3 %collective-permute-start.7 = (bf16[272,1280]{1,0:T(8,128)(2,1)}, bf16[272,1280]{1,0:T(8,128)(2,1)S(1)}, u32[]{:S(2)}, u32[]{:S(2)}) collective-permute-start(bf16[272,1280]{1,0:T(8,128)(2,1)} %shard_map.61), channel_id=1, source_target_pairs={{0,8},{8,16},{16,24},{24,32},{32,40},{40,48},{48,56},{56,64},{64,7... | collective-permute-start | bytes 2088968 | tf_op jit(solution)/shard_map/ppermute | solution.py:197
  149.6 0.9 copy-start.5
  161.8 0.9 copy-start.8

commit v7 on v5

--- a/solution.py
+++ b/solution.py
@@ -13,17 +13,25 @@
 
 
 def _store_stats(o_ref, st_ref, t, hg, rows):
-    hi = t[0 : 2 * hg].astype(jnp.bfloat16).astype(jnp.float32)
+    top, den = t[0:hg], t[hg : 2 * hg]
+    top_hi = top.astype(jnp.bfloat16).astype(jnp.float32)
+    rest = top - top_hi
+    top_mid = rest.astype(jnp.bfloat16).astype(jnp.float32)
+    den_hi = den.astype(jnp.bfloat16).astype(jnp.float32)
     st_ref[...] = jnp.zeros_like(st_ref)
-    st_ref[0 : 2 * hg, 0:rows] = hi
-    st_ref[0 : 2 * hg, rows : 2 * rows] = t[0 : 2 * hg] - hi
+    st_ref[0:hg, 0:rows] = top_hi
+    st_ref[0:hg, rows : 2 * rows] = top_mid
+    st_ref[2 * hg : 3 * hg, 0:rows] = rest - top_mid
+    st_ref[hg : 2 * hg, 0:rows] = den_hi
+    st_ref[hg : 2 * hg, rows : 2 * rows] = den - den_hi
     o_ref[rows : rows + EXTRA, :] = st_ref[...].astype(o_ref.dtype)
 
 
 def _load_stats(ref, hg, rows):
     block = ref[rows : rows + EXTRA, :].astype(jnp.float32)
-    full = block[0 : 2 * hg, 0:rows] + block[0 : 2 * hg, rows : 2 * rows]
-    return full[0:hg], full[hg : 2 * hg]
+    top = block[0:hg, 0:rows] + block[0:hg, rows : 2 * rows] + block[2 * hg : 3 * hg, 0:rows]
+    den = block[hg : 2 * hg, 0:rows] + block[hg : 2 * hg, rows : 2 * rows]
+    return top, den
 
 
 def _attn_kernel(flags_ref, q_ref, kl_ref, kc_ref, kr_ref, vl_ref, vc_ref, vr_ref, o_ref, col_ref, st_ref):

time: 154 us -> 154 us (level)
  the two profiles are of different devices: /device:TPU:56 before, /device:TPU:112 now
where the time goes in v7:
time: 154 us; the launch traced here: 153 us
  Pallas kernels  57.1 us (37%)
  waiting for transfers between devices  43.8 us (28%)
  starting transfers between devices  28.9 us (19%)
  local copies, waits for them, and re-layouts  12.5 us (8%)
  between operations  6.61 us (4%)
  other arithmetic  3.6 us (2%)
    pallas_call x6, Pallas kernels, attend(): pl.pallas_call(_attn_kernel, out_shape=jax.ShapeDtypeStruct((rows + EXTRA...  45.5 us
    ppermute x8, waiting for transfers between devices, shift_tm(): return lax.ppermute(x, 'tm', pairs)  43.8 us
    ppermute x8, starting transfers between devices, shift_tm(): return lax.ppermute(x, 'tm', pairs)  23.3 us
    pallas_call x4, Pallas kernels, merge(): pl.pallas_call(kernel, out_shape=out_shape, grid_spec=pltpu.PrefetchScala...  11.7 us
    unnamed x21, local copies, waits for them, and re-layouts  8.42 us
    ppermute x1, starting transfers between devices, on_device(): kv_r = lax.ppermute(kv, 'space', [(i + 1, i) for i in range(tiles - 1)])  3.64 us
  transfers between devices with their start and end apart: 10, of which 5 were waited for; matrix products, arithmetic and copies ran while one was open for 4% of the time, Pallas kernels for 36%

profile of v7, /device:TPU:112, one launch (start us, length us, event | category | flops | bytes accessed | tf_op | source)
XLA Modules:
  0.0 152.5 jit_solution(6761418165638662060)
XLA Ops:
  0.0 2.6 %constant_dynamic-update-slice_fusion.1 = bf16[2,256,2560]{2,1,0:T(8,128)(2,1)} fusion(bf16[1,256,2560]{2,1,0:T(8,128)(2,1)} %param.8), kind=kLoop, calls=%fused_computation.10 | loop fusion | bytes 2621440
  3.8 1.9 %collective-permute-start.2 = (bf16[2,256,2560]{2,1,0:T(8,128)(2,1)}, bf16[2,256,2560]{2,1,0:T(8,128)(2,1)S(1)}, u32[]{:S(2)}, u32[]{:S(2)}) collective-permute-start(bf16[2,256,2560]{2,1,0:T(8,128)(2,1)} %constant_dynamic-update-slice_fusion), channel_id=1, source_target_pairs={{0,1},{1,2},{2,3},{3,4},{4,5},{5,6},{6,7},{8,9},{9,10},{10,11},{11... | collective-permute-start | bytes 7864328 | tf_op jit(solution)/shard_map/ppermute | solution.py:238
  5.7 3.6 %collective-permute-start.3 = (bf16[2,256,2560]{2,1,0:T(8,128)(2,1)}, bf16[2,256,2560]{2,1,0:T(8,128)(2,1)}, u32[]{:S(2)}, u32[]{:S(2)}) collective-permute-start(bf16[2,256,2560]{2,1,0:T(8,128)(2,1)} %constant_dynamic-update-slice_fusion), channel_id=1, source_target_pairs={{1,0},{2,1},{3,2},{4,3},{5,4},{6,5},{7,6},{9,8},{10,9},{11,10},{12... | collective-permute-start | bytes 7864328 | tf_op jit(solution)/shard_map/ppermute | solution.py:239
  11.9 4.5 %collective-permute-start.1 = (bf16[272,1280]{1,0:T(8,128)(2,1)}, bf16[272,1280]{1,0:T(8,128)(2,1)S(1)}, u32[]{:S(2)}, u32[]{:S(2)}) collective-permute-start(bf16[272,1280]{1,0:T(8,128)(2,1)} %pad_maximum_fusion), channel_id=1, source_target_pairs={{8,0},{16,8},{24,16},{32,24},{40,32},{48,40},{56,48},{64,56},{72,6... | collective-permute-start | bytes 2088968 | tf_op jit(solution)/shard_map/ppermute | solution.py:205
  16.4 2.7 %collective-permute-start = (bf16[256,1280]{1,0:T(8,128)(2,1)}, bf16[256,1280]{1,0:T(8,128)(2,1)}, u32[]{:S(2)}, u32[]{:S(2)}) collective-permute-start(bf16[256,1280]{1,0:T(8,128)(2,1)} %get-tuple-element.38), channel_id=1, source_target_pairs={{8,0},{16,8},{24,16},{32,24},{40,32},{48,40},{56,48},{64,56},{72,6... | collective-permute-start | bytes 1966088 | tf_op jit(solution)/shard_map/ppermute | solution.py:205
  21.9 10.9 %collective-permute-done.1.q_ref = bf16[272,1280]{1,0:T(8,128)(2,1)S(1)} collective-permute-done((bf16[272,1280]{1,0:T(8,128)(2,1)}, bf16[272,1280]{1,0:T(8,128)(2,1)S(1)}, u32[]{:S(2)}, u32[]{:S(2)}) %collective-permute-start.1) | collective-permute-done | bytes 696352 | tf_op jit(solution)/shard_map/ppermute | solution.py:205
  32.8 6.4 %collective-permute-start.5 = (bf16[272,1280]{1,0:T(8,128)(2,1)S(1)}, bf16[272,1280]{1,0:T(8,128)(2,1)}, u32[]{:S(2)}, u32[]{:S(2)}) collective-permute-start(bf16[272,1280]{1,0:T(8,128)(2,1)S(1)} %collective-permute-done.1.q_ref), channel_id=1, source_target_pairs={{8,0},{16,8},{24,16},{32,24},{40,32},{48,40},{56,48},{64,56},{72,6... | collective-permute-start | bytes 2088968 | tf_op jit(solution)/shard_map/ppermute | solution.py:205
  44.5 7.6 %shard_map.55.a_ref = bf16[272,1280]{1,0:T(8,128)(2,1)} custom-call(s32[3]{0:T(128)} %add_convert_fusion.flags_ref, bf16[272,1280]{1,0:T(8,128)(2,1)} %copy-done.3, bf16[2,256,2560]{2,1,0:T(8,128)(2,1)} %copy-done, bf16[256,2560]{1,0:T(8,128)(2,1)} %bitcast.24, bf16[2,256,2560]{2,1,0:T(8,128)(2,1)} %collective-permute-done.3.kr_ref.vr_ref, ...), custom_call_target="tpu_custom_call" | custom-call | flops 1006632960 | bytes 5242880 | tf_op jit(solution)/shard_map/pallas_call | solution.py:100
  52.1 7.6 %shard_map.56.a_ref = bf16[272,1280]{1,0:T(8,128)(2,1)} custom-call(s32[3]{0:T(128)} %add_convert_fusion.flags_ref, bf16[256,1280]{1,0:T(8,128)(2,1)} %collective-permute-done.q_ref, bf16[2,256,2560]{2,1,0:T(8,128)(2,1)} %copy-done, bf16[256,2560]{1,0:T(8,128)(2,1)} %bitcast.25, bf16[2,256,2560]{2,1,0:T(8,128)(2,1)} %collective-permute-done.3.kr_ref.vr_ref, ...), custom_call_target="tpu_custom_call" | custom-call | flops 1006632960 | bytes 5242880 | tf_op jit(solution)/shard_map/pallas_call | solution.py:100
  59.7 1.9 %collective-permute-start.4 = (bf16[256,1280]{1,0:T(8,128)(2,1)}, bf16[256,1280]{1,0:T(8,128)(2,1)S(1)}, u32[]{:S(2)}, u32[]{:S(2)}) collective-permute-start(bf16[256,1280]{1,0:T(8,128)(2,1)} %collective-permute-done.q_ref), channel_id=1, source_target_pairs={{8,0},{16,8},{24,16},{32,24},{40,32},{48,40},{56,48},{64,56},{72,6... | collective-permute-start | bytes 1966088 | tf_op jit(solution)/shard_map/ppermute | solution.py:205
  65.5 7.6 %shard_map.57.a_ref = bf16[272,1280]{1,0:T(8,128)(2,1)} custom-call(s32[3]{0:T(128)} %add_convert_fusion.1.flags_ref, bf16[256,2560]{1,0:T(8,128)(2,1)} %bitcast.36, bf16[2,256,2560]{2,1,0:T(8,128)(2,1)} %copy-done, bf16[256,2560]{1,0:T(8,128)(2,1)} %bitcast.26, bf16[2,256,2560]{2,1,0:T(8,128)(2,1)} %collective-permute-done.3.kr_ref.vr_ref, ...), custom_call_target="tpu_custom_call" | custom-call | flops 1006632960 | bytes 5242880 | tf_op jit(solution)/shard_map/pallas_call | solution.py:100
  73.1 7.6 %shard_map.58 = bf16[272,1280]{1,0:T(8,128)(2,1)} custom-call(s32[3]{0:T(128)} %add_convert_fusion.2.flags_ref, bf16[272,1280]{1,0:T(8,128)(2,1)} %collective-permute-done.5.q_ref, bf16[2,256,2560]{2,1,0:T(8,128)(2,1)} %copy-done, bf16[256,2560]{1,0:T(8,128)(2,1)} %bitcast.27, bf16[2,256,2560]{2,1,0:T(8,128)(2,1)} %collective-permute-done.3.kr_ref.vr_ref, ...), custom_call_target="tpu_custom_call" | custom-call | flops 1006632960 | bytes 5242880 | tf_op jit(solution)/shard_map/pallas_call | solution.py:100
  80.6 2.1 %collective-permute-start.8 = (bf16[272,1280]{1,0:T(8,128)(2,1)}, bf16[272,1280]{1,0:T(8,128)(2,1)S(1)}, u32[]{:S(2)}, u32[]{:S(2)}) collective-permute-start(bf16[272,1280]{1,0:T(8,128)(2,1)} %shard_map.58), channel_id=1, source_target_pairs={{0,8},{8,16},{16,24},{24,32},{32,40},{40,48},{48,56},{56,64},{64,7... | collective-permute-start | bytes 2088968 | tf_op jit(solution)/shard_map/ppermute | solution.py:205
  82.7 7.6 %shard_map.59.a_ref = bf16[272,1280]{1,0:T(8,128)(2,1)} custom-call(s32[3]{0:T(128)} %add_convert_fusion.1.flags_ref, bf16[256,2560]{1,0:T(8,128)(2,1)} %bitcast.37, bf16[2,256,2560]{2,1,0:T(8,128)(2,1)} %copy-done, bf16[256,2560]{1,0:T(8,128)(2,1)} %bitcast.28, bf16[2,256,2560]{2,1,0:T(8,128)(2,1)} %collective-permute-done.3.kr_ref.vr_ref, ...), custom_call_target="tpu_custom_call" | custom-call | flops 1006632960 | bytes 5242880 | tf_op jit(solution)/shard_map/pallas_call | solution.py:100
  91.1 7.6 %shard_map.60 = bf16[272,1280]{1,0:T(8,128)(2,1)} custom-call(s32[3]{0:T(128)} %add_convert_fusion.2.flags_ref, bf16[256,1280]{1,0:T(8,128)(2,1)} %copy-done.8, bf16[2,256,2560]{2,1,0:T(8,128)(2,1)} %copy-done, bf16[256,2560]{1,0:T(8,128)(2,1)} %bitcast.29, bf16[2,256,2560]{2,1,0:T(8,128)(2,1)} %collective-permute-done.3.kr_ref.vr_ref, ...), custom_call_target="tpu_custom_call" | custom-call | flops 1006632960 | bytes 5242880 | tf_op jit(solution)/shard_map/pallas_call | solution.py:100
  98.7 1.9 %collective-permute-start.6 = (bf16[272,1280]{1,0:T(8,128)(2,1)}, bf16[272,1280]{1,0:T(8,128)(2,1)S(1)}, u32[]{:S(2)}, u32[]{:S(2)}) collective-permute-start(bf16[272,1280]{1,0:T(8,128)(2,1)} %shard_map.60), channel_id=1, source_target_pairs={{0,8},{8,16},{16,24},{24,32},{32,40},{40,48},{48,56},{56,64},{64,7... | collective-permute-start | bytes 2088968 | tf_op jit(solution)/shard_map/ppermute | solution.py:205
  101.6 2.9 %shard_map.62 = bf16[272,1280]{1,0:T(8,128)(2,1)} custom-call(s32[1]{0:T(128)} %bitcast.valid_ref, bf16[272,1280]{1,0:T(8,128)(2,1)} %shard_map.55.a_ref, bf16[272,1280]{1,0:T(8,128)(2,1)} %copy-done.5), custom_call_target="tpu_custom_call" | custom-call | flops 1310720 | bytes 1966080 | tf_op jit(solution)/shard_map/pallas_call | solution.py:184
  104.6 1.9 %collective-permute-start.9 = (bf16[272,1280]{1,0:T(8,128)(2,1)}, bf16[272,1280]{1,0:T(8,128)(2,1)S(1)}, u32[]{:S(2)}, u32[]{:S(2)}) collective-permute-start(bf16[272,1280]{1,0:T(8,128)(2,1)} %shard_map.62), channel_id=1, source_target_pairs={{0,8},{8,16},{16,24},{24,32},{32,40},{40,48},{48,56},{56,64},{64,7... | collective-permute-start | bytes 2088968 | tf_op jit(solution)/shard_map/ppermute | solution.py:205
  106.5 15.0 %collective-permute-done.6.b_ref = bf16[272,1280]{1,0:T(8,128)(2,1)S(1)} collective-permute-done((bf16[272,1280]{1,0:T(8,128)(2,1)}, bf16[272,1280]{1,0:T(8,128)(2,1)S(1)}, u32[]{:S(2)}, u32[]{:S(2)}) %collective-permute-start.6) | collective-permute-done | bytes 696352 | tf_op jit(solution)/shard_map/ppermute | solution.py:205
  122.4 2.9 %shard_map.61 = bf16[272,1280]{1,0:T(8,128)(2,1)} custom-call(s32[1]{0:T(128)} %bitcast.valid_ref, bf16[272,1280]{1,0:T(8,128)(2,1)} %shard_map.56.a_ref, bf16[272,1280]{1,0:T(8,128)(2,1)} %copy-done.6), custom_call_target="tpu_custom_call" | custom-call | flops 1310720 | bytes 1966080 | tf_op jit(solution)/shard_map/pallas_call | solution.py:184
  127.2 9.2 %collective-permute-done.9.b_ref = bf16[272,1280]{1,0:T(8,128)(2,1)S(1)} collective-permute-done((bf16[272,1280]{1,0:T(8,128)(2,1)}, bf16[272,1280]{1,0:T(8,128)(2,1)S(1)}, u32[]{:S(2)}, u32[]{:S(2)}) %collective-permute-start.9) | collective-permute-done | bytes 696352 | tf_op jit(solution)/shard_map/ppermute | solution.py:205
  137.3 2.9 %shard_map.63.rest_0_ = bf16[256,2560]{1,0:T(8,128)(2,1)} custom-call(s32[1]{0:T(128)} %bitcast.valid_ref, bf16[272,1280]{1,0:T(8,128)(2,1)} %shard_map.57.a_ref, bf16[272,1280]{1,0:T(8,128)(2,1)} %copy-done.4), custom_call_target="tpu_custom_call" | custom-call | flops 1310720 | bytes 1966080 | tf_op jit(solution)/shard_map/pallas_call | solution.py:184
  140.2 8.6 %collective-permute-done.7.b_ref = bf16[272,1280]{1,0:T(8,128)(2,1)S(1)} collective-permute-done((bf16[272,1280]{1,0:T(8,128)(2,1)}, bf16[272,1280]{1,0:T(8,128)(2,1)S(1)}, u32[]{:S(2)}, u32[]{:S(2)}) %collective-permute-start.7) | collective-permute-done | bytes 696352 | tf_op jit(solution)/shard_map/ppermute | solution.py:205
  149.6 2.9 %shard_map.64 = bf16[256,2560]{1,0:T(8,128)(2,1)} custom-call(s32[1]{0:T(128)} %bitcast.valid_ref, bf16[272,1280]{1,0:T(8,128)(2,1)} %shard_map.59.a_ref, bf16[272,1280]{1,0:T(8,128)(2,1)} %copy-done.7, bf16[256,2560]{1,0:T(8,128)(2,1)} %shard_map.63.rest_0_), custom_call_target="tpu_custom_call", output_to_operand_aliasing={{}: (3, {})} | custom-call | flops 1310720 | bytes 1966080 | tf_op jit(solution)/shard_map/pallas_call | solution.py:184
  (41 shorter events, 15.5 us)
Async XLA Ops:
  0.0 2.6 %copy-start.1 = (bf16[1,256,2560]{2,1,0:T(8,128)(2,1)S(1)}, bf16[1,256,2560]{2,1,0:T(8,128)(2,1)}, u32[]{:S(2)}) copy-start(bf16[1,256,2560]{2,1,0:T(8,128)(2,1)} %param.9) | copy-start | bytes 3932164
  2.6 7.4 %copy-start.9 = (s32[1,1,2]{2,1,0:T(1,128)S(1)}, s32[1,1,2]{2,1,0:T(1,128)}, u32[]{:S(2)}) copy-start(s32[1,1,2]{2,1,0:T(1,128)} %param.11) | copy-start | bytes 28
  2.6 7.5 %copy-start.2 = (bf16[1,256,2560]{2,1,0:T(8,128)(2,1)S(1)}, bf16[1,256,2560]{2,1,0:T(8,128)(2,1)}, u32[]{:S(2)}) copy-start(bf16[1,256,2560]{2,1,0:T(8,128)(2,1)} %param.7) | copy-start | bytes 3932164
  3.8 39.2 %collective-permute-start.2 = (bf16[2,256,2560]{2,1,0:T(8,128)(2,1)}, bf16[2,256,2560]{2,1,0:T(8,128)(2,1)S(1)}, u32[]{:S(2)}, u32[]{:S(2)}) collective-permute-start(bf16[2,256,2560]{2,1,0:T(8,128)(2,1)} %constant_dynamic-update-slice_fusion), channel_id=1, source_target_pairs={{0,1},{1,2},{2,3},{3,4},{4,5},{5,6},{6,7},{8,9},{9,10},{10,11},{11... | collective-permute-start | bytes 7864328 | tf_op jit(solution)/shard_map/ppermute | solution.py:238
  5.7 37.3 %collective-permute-start.3 = (bf16[2,256,2560]{2,1,0:T(8,128)(2,1)}, bf16[2,256,2560]{2,1,0:T(8,128)(2,1)}, u32[]{:S(2)}, u32[]{:S(2)}) collective-permute-start(bf16[2,256,2560]{2,1,0:T(8,128)(2,1)} %constant_dynamic-update-slice_fusion), channel_id=1, source_target_pairs={{1,0},{2,1},{3,2},{4,3},{5,4},{6,5},{7,6},{9,8},{10,9},{11,10},{12... | collective-permute-start | bytes 7864328 | tf_op jit(solution)/shard_map/ppermute | solution.py:239
  11.9 20.8 %collective-permute-start.1 = (bf16[272,1280]{1,0:T(8,128)(2,1)}, bf16[272,1280]{1,0:T(8,128)(2,1)S(1)}, u32[]{:S(2)}, u32[]{:S(2)}) collective-permute-start(bf16[272,1280]{1,0:T(8,128)(2,1)} %pad_maximum_fusion), channel_id=1, source_target_pairs={{8,0},{16,8},{24,16},{32,24},{40,32},{48,40},{56,48},{64,56},{72,6... | collective-permute-start | bytes 2088968 | tf_op jit(solution)/shard_map/ppermute | solution.py:205
  16.4 35.7 %collective-permute-start = (bf16[256,1280]{1,0:T(8,128)(2,1)}, bf16[256,1280]{1,0:T(8,128)(2,1)}, u32[]{:S(2)}, u32[]{:S(2)}) collective-permute-start(bf16[256,1280]{1,0:T(8,128)(2,1)} %get-tuple-element.38), channel_id=1, source_target_pairs={{8,0},{16,8},{24,16},{32,24},{40,32},{48,40},{56,48},{64,56},{72,6... | collective-permute-start | bytes 1966088 | tf_op jit(solution)/shard_map/ppermute | solution.py:205
  32.8 10.2 %copy-start.3 = (bf16[272,1280]{1,0:T(8,128)(2,1)}, bf16[272,1280]{1,0:T(8,128)(2,1)S(1)}, u32[]{:S(2)}) copy-start(bf16[272,1280]{1,0:T(8,128)(2,1)S(1)} %collective-permute-done.1.q_ref) | copy-start | bytes 2088964
  32.8 28.8 %collective-permute-start.5 = (bf16[272,1280]{1,0:T(8,128)(2,1)S(1)}, bf16[272,1280]{1,0:T(8,128)(2,1)}, u32[]{:S(2)}, u32[]{:S(2)}) collective-permute-start(bf16[272,1280]{1,0:T(8,128)(2,1)S(1)} %collective-permute-done.1.q_ref), channel_id=1, source_target_pairs={{8,0},{16,8},{24,16},{32,24},{40,32},{48,40},{56,48},{64,56},{72,6... | collective-permute-start | bytes 2088968 | tf_op jit(solution)/shard_map/ppermute | solution.py:205
  43.0 1.6 %copy-start = (bf16[2,256,2560]{2,1,0:T(8,128)(2,1)}, bf16[2,256,2560]{2,1,0:T(8,128)(2,1)S(1)}, u32[]{:S(2)}) copy-start(bf16[2,256,2560]{2,1,0:T(8,128)(2,1)S(1)} %collective-permute-done.2.kl_ref.vl_ref) | copy-start | bytes 7864324
  59.7 30.6 %collective-permute-start.4 = (bf16[256,1280]{1,0:T(8,128)(2,1)}, bf16[256,1280]{1,0:T(8,128)(2,1)S(1)}, u32[]{:S(2)}, u32[]{:S(2)}) collective-permute-start(bf16[256,1280]{1,0:T(8,128)(2,1)} %collective-permute-done.q_ref), channel_id=1, source_target_pairs={{8,0},{16,8},{24,16},{32,24},{40,32},{48,40},{56,48},{64,56},{72,6... | collective-permute-start | bytes 1966088 | tf_op jit(solution)/shard_map/ppermute | solution.py:205
  80.6 20.2 %collective-permute-start.8 = (bf16[272,1280]{1,0:T(8,128)(2,1)}, bf16[272,1280]{1,0:T(8,128)(2,1)S(1)}, u32[]{:S(2)}, u32[]{:S(2)}) collective-permute-start(bf16[272,1280]{1,0:T(8,128)(2,1)} %shard_map.58), channel_id=1, source_target_pairs={{0,8},{8,16},{16,24},{24,32},{32,40},{40,48},{48,56},{56,64},{64,7... | collective-permute-start | bytes 2088968 | tf_op jit(solution)/shard_map/ppermute | solution.py:205
  90.3 0.8 copy-start.8
  98.7 22.7 %collective-permute-start.6 = (bf16[272,1280]{1,0:T(8,128)(2,1)}, bf16[272,1280]{1,0:T(8,128)(2,1)S(1)}, u32[]{:S(2)}, u32[]{:S(2)}) collective-permute-start(bf16[272,1280]{1,0:T(8,128)(2,1)} %shard_map.60), channel_id=1, source_target_pairs={{0,8},{8,16},{16,24},{24,32},{32,40},{40,48},{48,56},{56,64},{64,7... | collective-permute-start | bytes 2088968 | tf_op jit(solution)/shard_map/ppermute | solution.py:205
  100.8 0.9 copy-start.5
  104.6 31.8 %collective-permute-start.9 = (bf16[272,1280]{1,0:T(8,128)(2,1)}, bf16[272,1280]{1,0:T(8,128)(2,1)S(1)}, u32[]{:S(2)}, u32[]{:S(2)}) collective-permute-start(bf16[272,1280]{1,0:T(8,128)(2,1)} %shard_map.62), channel_id=1, source_target_pairs={{0,8},{8,16},{16,24},{24,32},{32,40},{40,48},{48,56},{56,64},{64,7... | collective-permute-start | bytes 2088968 | tf_op jit(solution)/shard_map/ppermute | solution.py:205
  121.5 0.9 copy-start.6
  125.3 23.5 %collective-permute-start.7 = (bf16[272,1280]{1,0:T(8,128)(2,1)}, bf16[272,1280]{1,0:T(8,128)(2,1)S(1)}, u32[]{:S(2)}, u32[]{:S(2)}) collective-permute-start(bf16[272,1280]{1,0:T(8,128)(2,1)} %shard_map.61), channel_id=1, source_target_pairs={{0,8},{8,16},{16,24},{24,32},{32,40},{40,48},{48,56},{56,64},{64,7... | collective-permute-start | bytes 2088968 | tf_op jit(solution)/shard_map/ppermute | solution.py:205
  136.4 0.9 copy-start.4
  148.8 0.9 copy-start.7

commit v8 on v7

--- a/solution.py
+++ b/solution.py
@@ -199,6 +199,25 @@
     )(*operands)
 
 
+def _stack_kernel(k_ref, v_ref, o_ref):
+    o_ref[0] = k_ref[...]
+    o_ref[1] = v_ref[...]
+
+
+def stack_kv(k, v):
+    rows, width = k.shape
+    lanes = width // 2
+    spec = pl.BlockSpec((rows, lanes), lambda g: (0, g))
+    return pl.pallas_call(
+        _stack_kernel,
+        out_shape=jax.ShapeDtypeStruct((2, rows, width), k.dtype),
+        grid=(2,),
+        in_specs=[spec, spec],
+        out_specs=pl.BlockSpec((2, rows, lanes), lambda g: (0, 0, g)),
+        cost_estimate=pl.CostEstimate(flops=0, transcendentals=0, bytes_accessed=4 * rows * width * 2),
+    )(k, v)
+
+
 def shift_tm(x, by):
     size = lax.axis_size("tm")
     pairs = [(i, i + by) for i in range(size) if 0 <= i + by < size]
@@ -234,7 +253,7 @@
     sends += [q[:, c * chunk_w : (c + 1) * chunk_w] for c in range(1, CHUNKS)]
     q1s = [shift_tm(x, -1) for x in sends]
 
-    kv = jnp.stack([k, v])
+    kv = stack_kv(k, v)
     kv_l = lax.ppermute(kv, "space", [(i, i + 1) for i in range(tiles - 1)])
     kv_r = lax.ppermute(kv, "space", [(i + 1, i) for i in range(tiles - 1)])
 

time: 154 us -> 155 us (level)
  Pallas kernels: 57.1 us -> 60.1 us
  local copies, waits for them, and re-layouts: 12.5 us -> 9.99 us
    pallas_call x0 -> x1, Pallas kernels: none -> 2.92 us  [stack_kv(): pl.pallas_call(_stack_kernel, out_shape=jax.ShapeDtypeStruct((2, rows, wi...]
    unnamed x21 -> x16, local copies, waits for them, and re-layouts: 8.42 us -> 5.84 us
  transfers between devices with their start and end apart: 10 -> 10, of which waited for: 5 -> 4; matrix products, arithmetic and copies ran while one was open for 4% -> 5% of each run, Pallas kernels for 36% -> 36%
where the time goes in v8:
time: 155 us; the launch traced here: 153 us
  Pallas kernels  60.1 us (39%)
  waiting for transfers between devices  43.5 us (28%)
  starting transfers between devices  28.9 us (19%)
  local copies, waits for them, and re-layouts  9.99 us (6%)
  between operations  6.57 us (4%)
  other arithmetic  3.66 us (2%)
    pallas_call x6, Pallas kernels, attend(): pl.pallas_call(_attn_kernel, out_shape=jax.ShapeDtypeStruct((rows + EXTRA...  45.5 us
    ppermute x8, waiting for transfers between devices, shift_tm(): return lax.ppermute(x, 'tm', pairs)  43.5 us
    ppermute x8, starting transfers between devices, shift_tm(): return lax.ppermute(x, 'tm', pairs)  23.3 us
    pallas_call x4, Pallas kernels, merge(): pl.pallas_call(kernel, out_shape=out_shape, grid_spec=pltpu.PrefetchScala...  11.7 us
    unnamed x16, local copies, waits for them, and re-layouts  5.84 us
    ppermute x1, starting transfers between devices, on_device(): kv_r = lax.ppermute(kv, 'space', [(i + 1, i) for i in range(tiles - 1)])  3.64 us
  transfers between devices with their start and end apart: 10, of which 4 were waited for; matrix products, arithmetic and copies ran while one was open for 5% of the time, Pallas kernels for 36%

profile of v8, /device:TPU:112, one launch (start us, length us, event | category | flops | bytes accessed | tf_op | source)
XLA Modules:
  0.0 152.8 jit_solution(1823189456660115085)
XLA Ops:
  0.0 2.9 %shard_map.55 = bf16[2,256,2560]{2,1,0:T(8,128)(2,1)} custom-call(bf16[256,2560]{1,0:T(8,128)(2,1)} %bitcast.24, bf16[256,2560]{1,0:T(8,128)(2,1)} %bitcast.31), custom_call_target="tpu_custom_call" | custom-call | bytes 5242880 | tf_op jit(solution)/shard_map/pallas_call | solution.py:211
  2.9 1.9 %collective-permute-start.2 = (bf16[2,256,2560]{2,1,0:T(8,128)(2,1)}, bf16[2,256,2560]{2,1,0:T(8,128)(2,1)S(1)}, u32[]{:S(2)}, u32[]{:S(2)}) collective-permute-start(bf16[2,256,2560]{2,1,0:T(8,128)(2,1)} %shard_map.55), channel_id=1, source_target_pairs={{0,1},{1,2},{2,3},{3,4},{4,5},{5,6},{6,7},{8,9},{9,10},{10,11},{11... | collective-permute-start | bytes 7864328 | tf_op jit(solution)/shard_map/ppermute | solution.py:257
  4.8 3.6 %collective-permute-start.3 = (bf16[2,256,2560]{2,1,0:T(8,128)(2,1)}, bf16[2,256,2560]{2,1,0:T(8,128)(2,1)}, u32[]{:S(2)}, u32[]{:S(2)}) collective-permute-start(bf16[2,256,2560]{2,1,0:T(8,128)(2,1)} %shard_map.55), channel_id=1, source_target_pairs={{1,0},{2,1},{3,2},{4,3},{5,4},{6,5},{7,6},{9,8},{10,9},{11,10},{12... | collective-permute-start | bytes 7864328 | tf_op jit(solution)/shard_map/ppermute | solution.py:258
  9.2 2.2 %fusion.6 = (bf16[256,1280]{1,0:T(8,128)(2,1)S(1)}, bf16[256,1280]{1,0:T(8,128)(2,1)}) fusion(bf16[256,2560]{1,0:T(8,128)(2,1)} %bitcast.38), kind=kLoop, calls=%fused_computation.17 | loop fusion | bytes 2621440 | tf_op jit(solution)/shard_map/slice | solution.py:252
  12.3 4.5 %collective-permute-start.1 = (bf16[272,1280]{1,0:T(8,128)(2,1)}, bf16[272,1280]{1,0:T(8,128)(2,1)S(1)}, u32[]{:S(2)}, u32[]{:S(2)}) collective-permute-start(bf16[272,1280]{1,0:T(8,128)(2,1)} %pad_maximum_fusion), channel_id=1, source_target_pairs={{8,0},{16,8},{24,16},{32,24},{40,32},{48,40},{56,48},{64,56},{72,6... | collective-permute-start | bytes 2088968 | tf_op jit(solution)/shard_map/ppermute | solution.py:224
  16.8 2.7 %collective-permute-start = (bf16[256,1280]{1,0:T(8,128)(2,1)}, bf16[256,1280]{1,0:T(8,128)(2,1)}, u32[]{:S(2)}, u32[]{:S(2)}) collective-permute-start(bf16[256,1280]{1,0:T(8,128)(2,1)} %get-tuple-element.38), channel_id=1, source_target_pairs={{8,0},{16,8},{24,16},{32,24},{40,32},{48,40},{56,48},{64,56},{72,6... | collective-permute-start | bytes 1966088 | tf_op jit(solution)/shard_map/ppermute | solution.py:224
  22.3 10.9 %collective-permute-done.1.q_ref = bf16[272,1280]{1,0:T(8,128)(2,1)S(1)} collective-permute-done((bf16[272,1280]{1,0:T(8,128)(2,1)}, bf16[272,1280]{1,0:T(8,128)(2,1)S(1)}, u32[]{:S(2)}, u32[]{:S(2)}) %collective-permute-start.1) | collective-permute-done | bytes 696352 | tf_op jit(solution)/shard_map/ppermute | solution.py:224
  33.2 6.4 %collective-permute-start.5 = (bf16[272,1280]{1,0:T(8,128)(2,1)S(1)}, bf16[272,1280]{1,0:T(8,128)(2,1)}, u32[]{:S(2)}, u32[]{:S(2)}) collective-permute-start(bf16[272,1280]{1,0:T(8,128)(2,1)S(1)} %collective-permute-done.1.q_ref), channel_id=1, source_target_pairs={{8,0},{16,8},{24,16},{32,24},{40,32},{48,40},{56,48},{64,56},{72,6... | collective-permute-start | bytes 2088968 | tf_op jit(solution)/shard_map/ppermute | solution.py:224
  45.0 7.6 %shard_map.56.a_ref = bf16[272,1280]{1,0:T(8,128)(2,1)} custom-call(s32[3]{0:T(128)} %add_convert_fusion.flags_ref, bf16[272,1280]{1,0:T(8,128)(2,1)} %copy-done.1, bf16[2,256,2560]{2,1,0:T(8,128)(2,1)} %copy-done, bf16[256,2560]{1,0:T(8,128)(2,1)} %bitcast.25, bf16[2,256,2560]{2,1,0:T(8,128)(2,1)} %collective-permute-done.3.kr_ref.vr_ref, ...), custom_call_target="tpu_custom_call" | custom-call | flops 1006632960 | bytes 5242880 | tf_op jit(solution)/shard_map/pallas_call | solution.py:100
  52.6 7.6 %shard_map.57.a_ref = bf16[272,1280]{1,0:T(8,128)(2,1)} custom-call(s32[3]{0:T(128)} %add_convert_fusion.flags_ref, bf16[256,1280]{1,0:T(8,128)(2,1)} %collective-permute-done.q_ref, bf16[2,256,2560]{2,1,0:T(8,128)(2,1)} %copy-done, bf16[256,2560]{1,0:T(8,128)(2,1)} %bitcast.26, bf16[2,256,2560]{2,1,0:T(8,128)(2,1)} %collective-permute-done.3.kr_ref.vr_ref, ...), custom_call_target="tpu_custom_call" | custom-call | flops 1006632960 | bytes 5242880 | tf_op jit(solution)/shard_map/pallas_call | solution.py:100
  60.1 1.9 %collective-permute-start.4 = (bf16[256,1280]{1,0:T(8,128)(2,1)}, bf16[256,1280]{1,0:T(8,128)(2,1)S(1)}, u32[]{:S(2)}, u32[]{:S(2)}) collective-permute-start(bf16[256,1280]{1,0:T(8,128)(2,1)} %collective-permute-done.q_ref), channel_id=1, source_target_pairs={{8,0},{16,8},{24,16},{32,24},{40,32},{48,40},{56,48},{64,56},{72,6... | collective-permute-start | bytes 1966088 | tf_op jit(solution)/shard_map/ppermute | solution.py:224
  65.9 7.6 %shard_map.58.a_ref = bf16[272,1280]{1,0:T(8,128)(2,1)} custom-call(s32[3]{0:T(128)} %add_convert_fusion.1.flags_ref, bf16[256,2560]{1,0:T(8,128)(2,1)} %bitcast.39, bf16[2,256,2560]{2,1,0:T(8,128)(2,1)} %copy-done, bf16[256,2560]{1,0:T(8,128)(2,1)} %bitcast.27, bf16[2,256,2560]{2,1,0:T(8,128)(2,1)} %collective-permute-done.3.kr_ref.vr_ref, ...), custom_call_target="tpu_custom_call" | custom-call | flops 1006632960 | bytes 5242880 | tf_op jit(solution)/shard_map/pallas_call | solution.py:100
  73.5 7.6 %shard_map.59 = bf16[272,1280]{1,0:T(8,128)(2,1)} custom-call(s32[3]{0:T(128)} %add_convert_fusion.2.flags_ref, bf16[272,1280]{1,0:T(8,128)(2,1)} %collective-permute-done.5.q_ref, bf16[2,256,2560]{2,1,0:T(8,128)(2,1)} %copy-done, bf16[256,2560]{1,0:T(8,128)(2,1)} %bitcast.28, bf16[2,256,2560]{2,1,0:T(8,128)(2,1)} %collective-permute-done.3.kr_ref.vr_ref, ...), custom_call_target="tpu_custom_call" | custom-call | flops 1006632960 | bytes 5242880 | tf_op jit(solution)/shard_map/pallas_call | solution.py:100
  81.0 2.1 %collective-permute-start.8 = (bf16[272,1280]{1,0:T(8,128)(2,1)}, bf16[272,1280]{1,0:T(8,128)(2,1)S(1)}, u32[]{:S(2)}, u32[]{:S(2)}) collective-permute-start(bf16[272,1280]{1,0:T(8,128)(2,1)} %shard_map.59), channel_id=1, source_target_pairs={{0,8},{8,16},{16,24},{24,32},{32,40},{40,48},{48,56},{56,64},{64,7... | collective-permute-start | bytes 2088968 | tf_op jit(solution)/shard_map/ppermute | solution.py:224
  83.1 7.6 %shard_map.60.a_ref = bf16[272,1280]{1,0:T(8,128)(2,1)} custom-call(s32[3]{0:T(128)} %add_convert_fusion.1.flags_ref, bf16[256,2560]{1,0:T(8,128)(2,1)} %bitcast.40, bf16[2,256,2560]{2,1,0:T(8,128)(2,1)} %copy-done, bf16[256,2560]{1,0:T(8,128)(2,1)} %bitcast.29, bf16[2,256,2560]{2,1,0:T(8,128)(2,1)} %collective-permute-done.3.kr_ref.vr_ref, ...), custom_call_target="tpu_custom_call" | custom-call | flops 1006632960 | bytes 5242880 | tf_op jit(solution)/shard_map/pallas_call | solution.py:100
  91.6 7.6 %shard_map.61 = bf16[272,1280]{1,0:T(8,128)(2,1)} custom-call(s32[3]{0:T(128)} %add_convert_fusion.2.flags_ref, bf16[256,1280]{1,0:T(8,128)(2,1)} %copy-done.6, bf16[2,256,2560]{2,1,0:T(8,128)(2,1)} %copy-done, bf16[256,2560]{1,0:T(8,128)(2,1)} %bitcast.30, bf16[2,256,2560]{2,1,0:T(8,128)(2,1)} %collective-permute-done.3.kr_ref.vr_ref, ...), custom_call_target="tpu_custom_call" | custom-call | flops 1006632960 | bytes 5242880 | tf_op jit(solution)/shard_map/pallas_call | solution.py:100
  99.2 1.9 %collective-permute-start.6 = (bf16[272,1280]{1,0:T(8,128)(2,1)}, bf16[272,1280]{1,0:T(8,128)(2,1)S(1)}, u32[]{:S(2)}, u32[]{:S(2)}) collective-permute-start(bf16[272,1280]{1,0:T(8,128)(2,1)} %shard_map.61), channel_id=1, source_target_pairs={{0,8},{8,16},{16,24},{24,32},{32,40},{40,48},{48,56},{56,64},{64,7... | collective-permute-start | bytes 2088968 | tf_op jit(solution)/shard_map/ppermute | solution.py:224
  102.0 3.0 %shard_map.63 = bf16[272,1280]{1,0:T(8,128)(2,1)} custom-call(s32[1]{0:T(128)} %bitcast.valid_ref, bf16[272,1280]{1,0:T(8,128)(2,1)} %shard_map.56.a_ref, bf16[272,1280]{1,0:T(8,128)(2,1)} %copy-done.3), custom_call_target="tpu_custom_call" | custom-call | flops 1310720 | bytes 1966080 | tf_op jit(solution)/shard_map/pallas_call | solution.py:184
  106.8 15.1 %collective-permute-done.6.b_ref = bf16[272,1280]{1,0:T(8,128)(2,1)S(1)} collective-permute-done((bf16[272,1280]{1,0:T(8,128)(2,1)}, bf16[272,1280]{1,0:T(8,128)(2,1)S(1)}, u32[]{:S(2)}, u32[]{:S(2)}) %collective-permute-start.6) | collective-permute-done | bytes 696352 | tf_op jit(solution)/shard_map/ppermute | solution.py:224
  122.9 2.9 %shard_map.62 = bf16[272,1280]{1,0:T(8,128)(2,1)} custom-call(s32[1]{0:T(128)} %bitcast.valid_ref, bf16[272,1280]{1,0:T(8,128)(2,1)} %shard_map.57.a_ref, bf16[272,1280]{1,0:T(8,128)(2,1)} %copy-done.4), custom_call_target="tpu_custom_call" | custom-call | flops 1310720 | bytes 1966080 | tf_op jit(solution)/shard_map/pallas_call | solution.py:184
  127.7 9.2 %collective-permute-done.9.b_ref = bf16[272,1280]{1,0:T(8,128)(2,1)S(1)} collective-permute-done((bf16[272,1280]{1,0:T(8,128)(2,1)}, bf16[272,1280]{1,0:T(8,128)(2,1)S(1)}, u32[]{:S(2)}, u32[]{:S(2)}) %collective-permute-start.9) | collective-permute-done | bytes 696352 | tf_op jit(solution)/shard_map/ppermute | solution.py:224
  137.8 2.9 %shard_map.64.rest_0_ = bf16[256,2560]{1,0:T(8,128)(2,1)} custom-call(s32[1]{0:T(128)} %bitcast.valid_ref, bf16[272,1280]{1,0:T(8,128)(2,1)} %shard_map.58.a_ref, bf16[272,1280]{1,0:T(8,128)(2,1)} %copy-done.2), custom_call_target="tpu_custom_call" | custom-call | flops 1310720 | bytes 1966080 | tf_op jit(solution)/shard_map/pallas_call | solution.py:184
  140.7 8.3 %collective-permute-done.7.b_ref = bf16[272,1280]{1,0:T(8,128)(2,1)S(1)} collective-permute-done((bf16[272,1280]{1,0:T(8,128)(2,1)}, bf16[272,1280]{1,0:T(8,128)(2,1)S(1)}, u32[]{:S(2)}, u32[]{:S(2)}) %collective-permute-start.7) | collective-permute-done | bytes 696352 | tf_op jit(solution)/shard_map/ppermute | solution.py:224
  149.9 2.9 %shard_map.65 = bf16[256,2560]{1,0:T(8,128)(2,1)} custom-call(s32[1]{0:T(128)} %bitcast.valid_ref, bf16[272,1280]{1,0:T(8,128)(2,1)} %shard_map.60.a_ref, bf16[272,1280]{1,0:T(8,128)(2,1)} %copy-done.5, bf16[256,2560]{1,0:T(8,128)(2,1)} %shard_map.64.rest_0_), custom_call_target="tpu_custom_call", output_to_operand_aliasing={{}: (3, {})} | custom-call | flops 1310720 | bytes 1966080 | tf_op jit(solution)/shard_map/pallas_call | solution.py:184
  (36 shorter events, 15.3 us)
Async XLA Ops:
  0.0 9.1 %copy-start.7 = (s32[1,1,2]{2,1,0:T(1,128)S(1)}, s32[1,1,2]{2,1,0:T(1,128)}, u32[]{:S(2)}) copy-start(s32[1,1,2]{2,1,0:T(1,128)} %param.11) | copy-start | bytes 28
  2.9 40.5 %collective-permute-start.2 = (bf16[2,256,2560]{2,1,0:T(8,128)(2,1)}, bf16[2,256,2560]{2,1,0:T(8,128)(2,1)S(1)}, u32[]{:S(2)}, u32[]{:S(2)}) collective-permute-start(bf16[2,256,2560]{2,1,0:T(8,128)(2,1)} %shard_map.55), channel_id=1, source_target_pairs={{0,1},{1,2},{2,3},{3,4},{4,5},{5,6},{6,7},{8,9},{9,10},{10,11},{11... | collective-permute-start | bytes 7864328 | tf_op jit(solution)/shard_map/ppermute | solution.py:257
  4.8 38.6 %collective-permute-start.3 = (bf16[2,256,2560]{2,1,0:T(8,128)(2,1)}, bf16[2,256,2560]{2,1,0:T(8,128)(2,1)}, u32[]{:S(2)}, u32[]{:S(2)}) collective-permute-start(bf16[2,256,2560]{2,1,0:T(8,128)(2,1)} %shard_map.55), channel_id=1, source_target_pairs={{1,0},{2,1},{3,2},{4,3},{5,4},{6,5},{7,6},{9,8},{10,9},{11,10},{12... | collective-permute-start | bytes 7864328 | tf_op jit(solution)/shard_map/ppermute | solution.py:258
  12.3 20.8 %collective-permute-start.1 = (bf16[272,1280]{1,0:T(8,128)(2,1)}, bf16[272,1280]{1,0:T(8,128)(2,1)S(1)}, u32[]{:S(2)}, u32[]{:S(2)}) collective-permute-start(bf16[272,1280]{1,0:T(8,128)(2,1)} %pad_maximum_fusion), channel_id=1, source_target_pairs={{8,0},{16,8},{24,16},{32,24},{40,32},{48,40},{56,48},{64,56},{72,6... | collective-permute-start | bytes 2088968 | tf_op jit(solution)/shard_map/ppermute | solution.py:224
  16.8 35.7 %collective-permute-start = (bf16[256,1280]{1,0:T(8,128)(2,1)}, bf16[256,1280]{1,0:T(8,128)(2,1)}, u32[]{:S(2)}, u32[]{:S(2)}) collective-permute-start(bf16[256,1280]{1,0:T(8,128)(2,1)} %get-tuple-element.38), channel_id=1, source_target_pairs={{8,0},{16,8},{24,16},{32,24},{40,32},{48,40},{56,48},{64,56},{72,6... | collective-permute-start | bytes 1966088 | tf_op jit(solution)/shard_map/ppermute | solution.py:224
  33.2 10.3 %copy-start.1 = (bf16[272,1280]{1,0:T(8,128)(2,1)}, bf16[272,1280]{1,0:T(8,128)(2,1)S(1)}, u32[]{:S(2)}) copy-start(bf16[272,1280]{1,0:T(8,128)(2,1)S(1)} %collective-permute-done.1.q_ref) | copy-start | bytes 2088964
  33.2 28.9 %collective-permute-start.5 = (bf16[272,1280]{1,0:T(8,128)(2,1)S(1)}, bf16[272,1280]{1,0:T(8,128)(2,1)}, u32[]{:S(2)}, u32[]{:S(2)}) collective-permute-start(bf16[272,1280]{1,0:T(8,128)(2,1)S(1)} %collective-permute-done.1.q_ref), channel_id=1, source_target_pairs={{8,0},{16,8},{24,16},{32,24},{40,32},{48,40},{56,48},{64,56},{72,6... | collective-permute-start | bytes 2088968 | tf_op jit(solution)/shard_map/ppermute | solution.py:224
  43.4 1.6 %copy-start = (bf16[2,256,2560]{2,1,0:T(8,128)(2,1)}, bf16[2,256,2560]{2,1,0:T(8,128)(2,1)S(1)}, u32[]{:S(2)}) copy-start(bf16[2,256,2560]{2,1,0:T(8,128)(2,1)S(1)} %collective-permute-done.2.kl_ref.vl_ref) | copy-start | bytes 7864324
  60.1 30.6 %collective-permute-start.4 = (bf16[256,1280]{1,0:T(8,128)(2,1)}, bf16[256,1280]{1,0:T(8,128)(2,1)S(1)}, u32[]{:S(2)}, u32[]{:S(2)}) collective-permute-start(bf16[256,1280]{1,0:T(8,128)(2,1)} %collective-permute-done.q_ref), channel_id=1, source_target_pairs={{8,0},{16,8},{24,16},{32,24},{40,32},{48,40},{56,48},{64,56},{72,6... | collective-permute-start | bytes 1966088 | tf_op jit(solution)/shard_map/ppermute | solution.py:224
  81.0 20.0 %collective-permute-start.8 = (bf16[272,1280]{1,0:T(8,128)(2,1)}, bf16[272,1280]{1,0:T(8,128)(2,1)S(1)}, u32[]{:S(2)}, u32[]{:S(2)}) collective-permute-start(bf16[272,1280]{1,0:T(8,128)(2,1)} %shard_map.59), channel_id=1, source_target_pairs={{0,8},{8,16},{16,24},{24,32},{32,40},{40,48},{48,56},{56,64},{64,7... | collective-permute-start | bytes 2088968 | tf_op jit(solution)/shard_map/ppermute | solution.py:224
  90.7 0.8 copy-start.6
  99.2 22.8 %collective-permute-start.6 = (bf16[272,1280]{1,0:T(8,128)(2,1)}, bf16[272,1280]{1,0:T(8,128)(2,1)S(1)}, u32[]{:S(2)}, u32[]{:S(2)}) collective-permute-start(bf16[272,1280]{1,0:T(8,128)(2,1)} %shard_map.61), channel_id=1, source_target_pairs={{0,8},{8,16},{16,24},{24,32},{32,40},{40,48},{48,56},{56,64},{64,7... | collective-permute-start | bytes 2088968 | tf_op jit(solution)/shard_map/ppermute | solution.py:224
  101.1 0.9 copy-start.3
  104.9 32.0 %collective-permute-start.9 = (bf16[272,1280]{1,0:T(8,128)(2,1)}, bf16[272,1280]{1,0:T(8,128)(2,1)S(1)}, u32[]{:S(2)}, u32[]{:S(2)}) collective-permute-start(bf16[272,1280]{1,0:T(8,128)(2,1)} %shard_map.63), channel_id=1, source_target_pairs={{0,8},{8,16},{16,24},{24,32},{32,40},{40,48},{48,56},{56,64},{64,7... | collective-permute-start | bytes 2088968 | tf_op jit(solution)/shard_map/ppermute | solution.py:224
  122.0 0.9 copy-start.4
  125.8 23.2 %collective-permute-start.7 = (bf16[272,1280]{1,0:T(8,128)(2,1)}, bf16[272,1280]{1,0:T(8,128)(2,1)S(1)}, u32[]{:S(2)}, u32[]{:S(2)}) collective-permute-start(bf16[272,1280]{1,0:T(8,128)(2,1)} %shard_map.62), channel_id=1, source_target_pairs={{0,8},{8,16},{16,24},{24,32},{32,40},{40,48},{48,56},{56,64},{64,7... | collective-permute-start | bytes 2088968 | tf_op jit(solution)/shard_map/ppermute | solution.py:224
  136.9 0.9 copy-start.2
  149.0 0.9 copy-start.5

commit v9 on v7

--- a/solution.py
+++ b/solution.py
@@ -250,16 +250,17 @@
     valid = (seg >= 1).astype(jnp.int32).reshape(1)
     f0 = flags_for(meta, 0)
     f2 = flags_for(q2s[0][rows, 0:3], 2)
+    p2s = [attend(f2, q2s[c], k, v, kv_l, kv_r, chunk_w, c * groups_c, 0) for c in range(CHUNKS)]
+    p2_ins = [shift_tm(p2, 1) for p2 in p2s]
+    after = p2s[-1]
     result = None
-    q_self = q
     for c in range(CHUNKS):
         base = c * groups_c
+        q_self, _ = lax.optimization_barrier((q, after))
         p_self = attend(f0, q_self, k, v, kv_l, kv_r, chunk_w, base, base)
-        q2, p_self = lax.optimization_barrier((q2s[c], p_self))
-        p2 = attend(f2, q2, k, v, kv_l, kv_r, chunk_w, base, 0)
-        q_self, p2 = lax.optimization_barrier((q, p2))
-        p2_in = shift_tm(p2, 1)
+        p2_in, p_self = lax.optimization_barrier((p2_ins[c], p_self))
         pc = merge(valid, p1s[c], p2_in, 0)
+        after = pc
         pc_in = shift_tm(pc, 1)
         result = merge(valid, p_self, pc_in, base, final=True, buf=result, out_width=width)
     return result.reshape(1, rows, width)

time: 154 us -> 142 us (0.922)
  Pallas kernels: 57.1 us -> 49.5 us
  waiting for transfers between devices: 43.8 us -> 39.8 us
    pallas_call x6, Pallas kernels: 45.5 us -> 37.8 us  [attend(): pl.pallas_call(_attn_kernel, out_shape=jax.ShapeDtypeStruct((rows + EXTRA...]
    ppermute x8, waiting for transfers between devices: 43.8 us -> 39.8 us  [shift_tm(): return lax.ppermute(x, 'tm', pairs)]
    ppermute x8, starting transfers between devices: 23.3 us -> 25.6 us  [shift_tm(): return lax.ppermute(x, 'tm', pairs)]
    ppermute x1, starting transfers between devices: 3.64 us -> 1.91 us  [on_device(): kv_r = lax.ppermute(kv, 'space', [(i + 1, i) for i in range(tiles - 1)])]
  transfers between devices with their start and end apart: 10 -> 10, of which waited for: 5 -> 6; matrix products, arithmetic and copies ran while one was open for 4% -> 4% of each run, Pallas kernels for 36% -> 33%
where the time goes in v9:
time: 142 us; the launch traced here: 141 us
  Pallas kernels  49.5 us (35%)
  waiting for transfers between devices  39.8 us (28%)
  starting transfers between devices  29.9 us (21%)
  local copies, waits for them, and re-layouts  12.7 us (9%)
  between operations  6.54 us (5%)
  other arithmetic  2.7 us (2%)
    ppermute x8, waiting for transfers between devices, shift_tm(): return lax.ppermute(x, 'tm', pairs)  39.8 us
    pallas_call x6, Pallas kernels, attend(): pl.pallas_call(_attn_kernel, out_shape=jax.ShapeDtypeStruct((rows + EXTRA...  37.8 us
    ppermute x8, starting transfers between devices, shift_tm(): return lax.ppermute(x, 'tm', pairs)  25.6 us
    pallas_call x4, Pallas kernels, merge(): pl.pallas_call(kernel, out_shape=out_shape, grid_spec=pltpu.PrefetchScala...  11.7 us
    unnamed x21, local copies, waits for them, and re-layouts  8.52 us
  transfers between devices with their start and end apart: 10, of which 6 were waited for; matrix products, arithmetic and copies ran while one was open for 4% of the time, Pallas kernels for 33%

profile of v9, /device:TPU:112, one launch (start us, length us, event | category | flops | bytes accessed | tf_op | source)
XLA Modules:
  0.0 141.2 jit_solution(6128650152108612528)
XLA Ops:
  0.0 2.6 %constant_dynamic-update-slice_fusion.1 = bf16[2,256,2560]{2,1,0:T(8,128)(2,1)} fusion(bf16[1,256,2560]{2,1,0:T(8,128)(2,1)} %param.8), kind=kLoop, calls=%fused_computation.10 | loop fusion | bytes 2621440
  3.8 1.9 %collective-permute-start.4 = (bf16[2,256,2560]{2,1,0:T(8,128)(2,1)}, bf16[2,256,2560]{2,1,0:T(8,128)(2,1)S(1)}, u32[]{:S(2)}, u32[]{:S(2)}) collective-permute-start(bf16[2,256,2560]{2,1,0:T(8,128)(2,1)} %constant_dynamic-update-slice_fusion), channel_id=1, source_target_pairs={{1,0},{2,1},{3,2},{4,3},{5,4},{6,5},{7,6},{9,8},{10,9},{11,10},{12... | collective-permute-start | bytes 7864328 | tf_op jit(solution)/shard_map/ppermute | solution.py:239
  5.7 2.4 %collective-permute-start.3 = (bf16[2,256,2560]{2,1,0:T(8,128)(2,1)}, bf16[2,256,2560]{2,1,0:T(8,128)(2,1)}, u32[]{:S(2)}, u32[]{:S(2)}) collective-permute-start(bf16[2,256,2560]{2,1,0:T(8,128)(2,1)} %constant_dynamic-update-slice_fusion), channel_id=1, source_target_pairs={{0,1},{1,2},{2,3},{3,4},{4,5},{5,6},{6,7},{8,9},{9,10},{10,11},{11... | collective-permute-start | bytes 7864328 | tf_op jit(solution)/shard_map/ppermute | solution.py:238
  9.8 4.5 %collective-permute-start = (bf16[272,1280]{1,0:T(8,128)(2,1)S(1)}, bf16[272,1280]{1,0:T(8,128)(2,1)}, u32[]{:S(2)}, u32[]{:S(2)}) collective-permute-start(bf16[272,1280]{1,0:T(8,128)(2,1)S(1)} %pad_maximum_fusion), channel_id=1, source_target_pairs={{8,0},{16,8},{24,16},{32,24},{40,32},{48,40},{56,48},{64,56},{72,6... | collective-permute-start | bytes 2088968 | tf_op jit(solution)/shard_map/ppermute | solution.py:205
  14.3 2.7 %collective-permute-start.2 = (bf16[256,1280]{1,0:T(8,128)(2,1)}, bf16[256,1280]{1,0:T(8,128)(2,1)}, u32[]{:S(2)}, u32[]{:S(2)}) collective-permute-start(bf16[256,1280]{1,0:T(8,128)(2,1)} %get-tuple-element.35), channel_id=1, source_target_pairs={{8,0},{16,8},{24,16},{32,24},{40,32},{48,40},{56,48},{64,56},{72,6... | collective-permute-start | bytes 1966088 | tf_op jit(solution)/shard_map/ppermute | solution.py:205
  17.1 13.1 %collective-permute-done.q_ref = bf16[272,1280]{1,0:T(8,128)(2,1)} collective-permute-done((bf16[272,1280]{1,0:T(8,128)(2,1)S(1)}, bf16[272,1280]{1,0:T(8,128)(2,1)}, u32[]{:S(2)}, u32[]{:S(2)}) %collective-permute-start) | collective-permute-done | bytes 696352 | tf_op jit(solution)/shard_map/ppermute | solution.py:205
  30.2 6.6 %collective-permute-start.1 = (bf16[272,1280]{1,0:T(8,128)(2,1)}, bf16[272,1280]{1,0:T(8,128)(2,1)S(1)}, u32[]{:S(2)}, u32[]{:S(2)}) collective-permute-start(bf16[272,1280]{1,0:T(8,128)(2,1)} %collective-permute-done.q_ref), channel_id=1, source_target_pairs={{8,0},{16,8},{24,16},{32,24},{40,32},{48,40},{56,48},{64,56},{72,6... | collective-permute-start | bytes 2088968 | tf_op jit(solution)/shard_map/ppermute | solution.py:205
  42.2 7.6 %shard_map.55.a_ref = bf16[272,1280]{1,0:T(8,128)(2,1)} custom-call(s32[3]{0:T(128)} %add_convert_fusion.1.flags_ref, bf16[272,1280]{1,0:T(8,128)(2,1)} %collective-permute-done.q_ref, bf16[2,256,2560]{2,1,0:T(8,128)(2,1)} %collective-permute-done.3.kl_ref.vl_ref, bf16[256,2560]{1,0:T(8,128)(2,1)} %bitcast.24, bf16[2,256,2560]{2,1,0:T(8,128)(2,1)} %copy-done, ...), custom_call_target="tpu_custom_call" | custom-call | flops 1006632960 | bytes 5242880 | tf_op jit(solution)/shard_map/pallas_call | solution.py:100
  49.7 7.6 %shard_map.56.a_ref = bf16[272,1280]{1,0:T(8,128)(2,1)} custom-call(s32[3]{0:T(128)} %add_convert_fusion.1.flags_ref, bf16[256,1280]{1,0:T(8,128)(2,1)} %collective-permute-done.2.q_ref, bf16[2,256,2560]{2,1,0:T(8,128)(2,1)} %collective-permute-done.3.kl_ref.vl_ref, bf16[256,2560]{1,0:T(8,128)(2,1)} %bitcast.25, bf16[2,256,2560]{2,1,0:T(8,128)(2,1)} %copy-done, ...), custom_call_target="tpu_custom_call" | custom-call | flops 1006632960 | bytes 5242880 | tf_op jit(solution)/shard_map/pallas_call | solution.py:100
  57.3 1.9 %collective-permute-start.5 = (bf16[256,1280]{1,0:T(8,128)(2,1)}, bf16[256,1280]{1,0:T(8,128)(2,1)S(1)}, u32[]{:S(2)}, u32[]{:S(2)}) collective-permute-start(bf16[256,1280]{1,0:T(8,128)(2,1)} %collective-permute-done.2.q_ref), channel_id=1, source_target_pairs={{8,0},{16,8},{24,16},{32,24},{40,32},{48,40},{56,48},{64,56},{72,6... | collective-permute-start | bytes 1966088 | tf_op jit(solution)/shard_map/ppermute | solution.py:205
  62.6 3.7 %shard_map.58 = bf16[272,1280]{1,0:T(8,128)(2,1)} custom-call(s32[3]{0:T(128)} %add_convert_fusion.flags_ref, bf16[272,1280]{1,0:T(8,128)(2,1)} %copy-done.3, bf16[2,256,2560]{2,1,0:T(8,128)(2,1)} %collective-permute-done.3.kl_ref.vl_ref, bf16[256,2560]{1,0:T(8,128)(2,1)} %bitcast.26, bf16[2,256,2560]{2,1,0:T(8,128)(2,1)} %copy-done, ...), custom_call_target="tpu_custom_call" | custom-call | flops 1006632960 | bytes 5242880 | tf_op jit(solution)/shard_map/pallas_call | solution.py:100
  66.4 3.9 %collective-permute-start.7 = (bf16[272,1280]{1,0:T(8,128)(2,1)}, bf16[272,1280]{1,0:T(8,128)(2,1)S(1)}, u32[]{:S(2)}, u32[]{:S(2)}) collective-permute-start(bf16[272,1280]{1,0:T(8,128)(2,1)} %shard_map.58), channel_id=1, source_target_pairs={{0,8},{8,16},{16,24},{24,32},{32,40},{40,48},{48,56},{56,64},{64,7... | collective-permute-start | bytes 2088968 | tf_op jit(solution)/shard_map/ppermute | solution.py:205
  70.2 5.8 %collective-permute-done.5.q_ref = bf16[256,1280]{1,0:T(8,128)(2,1)S(1)} collective-permute-done((bf16[256,1280]{1,0:T(8,128)(2,1)}, bf16[256,1280]{1,0:T(8,128)(2,1)S(1)}, u32[]{:S(2)}, u32[]{:S(2)}) %collective-permute-start.5) | collective-permute-done | bytes 655392 | tf_op jit(solution)/shard_map/ppermute | solution.py:205
  76.9 3.8 %shard_map.57 = bf16[272,1280]{1,0:T(8,128)(2,1)} custom-call(s32[3]{0:T(128)} %add_convert_fusion.flags_ref, bf16[256,1280]{1,0:T(8,128)(2,1)} %copy-done.8, bf16[2,256,2560]{2,1,0:T(8,128)(2,1)} %collective-permute-done.3.kl_ref.vl_ref, bf16[256,2560]{1,0:T(8,128)(2,1)} %bitcast.27, bf16[2,256,2560]{2,1,0:T(8,128)(2,1)} %copy-done, ...), custom_call_target="tpu_custom_call" | custom-call | flops 1006632960 | bytes 5242880 | tf_op jit(solution)/shard_map/pallas_call | solution.py:100
  80.7 2.1 %collective-permute-start.6 = (bf16[272,1280]{1,0:T(8,128)(2,1)}, bf16[272,1280]{1,0:T(8,128)(2,1)S(1)}, u32[]{:S(2)}, u32[]{:S(2)}) collective-permute-start(bf16[272,1280]{1,0:T(8,128)(2,1)} %shard_map.57), channel_id=1, source_target_pairs={{0,8},{8,16},{16,24},{24,32},{32,40},{40,48},{48,56},{56,64},{64,7... | collective-permute-start | bytes 2088968 | tf_op jit(solution)/shard_map/ppermute | solution.py:205
  86.1 7.6 %shard_map.59.a_ref = bf16[272,1280]{1,0:T(8,128)(2,1)} custom-call(s32[3]{0:T(128)} %add_convert_fusion.2.flags_ref, bf16[256,2560]{1,0:T(8,128)(2,1)} %bitcast.36, bf16[2,256,2560]{2,1,0:T(8,128)(2,1)} %collective-permute-done.3.kl_ref.vl_ref, bf16[256,2560]{1,0:T(8,128)(2,1)} %bitcast.28, bf16[2,256,2560]{2,1,0:T(8,128)(2,1)} %copy-done, ...), custom_call_target="tpu_custom_call" | custom-call | flops 1006632960 | bytes 5242880 | tf_op jit(solution)/shard_map/pallas_call | solution.py:100
  94.6 2.9 %shard_map.60 = bf16[272,1280]{1,0:T(8,128)(2,1)} custom-call(s32[1]{0:T(128)} %bitcast.valid_ref, bf16[272,1280]{1,0:T(8,128)(2,1)} %shard_map.55.a_ref, bf16[272,1280]{1,0:T(8,128)(2,1)} %copy-done.6), custom_call_target="tpu_custom_call" | custom-call | flops 1310720 | bytes 1966080 | tf_op jit(solution)/shard_map/pallas_call | solution.py:184
  97.5 2.0 %collective-permute-start.9 = (bf16[272,1280]{1,0:T(8,128)(2,1)}, bf16[272,1280]{1,0:T(8,128)(2,1)S(1)}, u32[]{:S(2)}, u32[]{:S(2)}) collective-permute-start(bf16[272,1280]{1,0:T(8,128)(2,1)} %shard_map.60), channel_id=1, source_target_pairs={{0,8},{8,16},{16,24},{24,32},{32,40},{40,48},{48,56},{56,64},{64,7... | collective-permute-start | bytes 2088968 | tf_op jit(solution)/shard_map/ppermute | solution.py:205
  99.5 7.6 %shard_map.61.a_ref = bf16[272,1280]{1,0:T(8,128)(2,1)} custom-call(s32[3]{0:T(128)} %add_convert_fusion.2.flags_ref, bf16[256,2560]{1,0:T(8,128)(2,1)} %bitcast.37, bf16[2,256,2560]{2,1,0:T(8,128)(2,1)} %collective-permute-done.3.kl_ref.vl_ref, bf16[256,2560]{1,0:T(8,128)(2,1)} %bitcast.29, bf16[2,256,2560]{2,1,0:T(8,128)(2,1)} %copy-done, ...), custom_call_target="tpu_custom_call" | custom-call | flops 1006632960 | bytes 5242880 | tf_op jit(solution)/shard_map/pallas_call | solution.py:100
  108.9 2.9 %shard_map.62 = bf16[272,1280]{1,0:T(8,128)(2,1)} custom-call(s32[1]{0:T(128)} %bitcast.valid_ref, bf16[272,1280]{1,0:T(8,128)(2,1)} %shard_map.56.a_ref, bf16[272,1280]{1,0:T(8,128)(2,1)} %copy-done.5), custom_call_target="tpu_custom_call" | custom-call | flops 1310720 | bytes 1966080 | tf_op jit(solution)/shard_map/pallas_call | solution.py:184
  113.8 9.2 %collective-permute-done.9.b_ref = bf16[272,1280]{1,0:T(8,128)(2,1)S(1)} collective-permute-done((bf16[272,1280]{1,0:T(8,128)(2,1)}, bf16[272,1280]{1,0:T(8,128)(2,1)S(1)}, u32[]{:S(2)}, u32[]{:S(2)}) %collective-permute-start.9) | collective-permute-done | bytes 696352 | tf_op jit(solution)/shard_map/ppermute | solution.py:205
  123.9 2.9 %shard_map.63.rest_0_ = bf16[256,2560]{1,0:T(8,128)(2,1)} custom-call(s32[1]{0:T(128)} %bitcast.valid_ref, bf16[272,1280]{1,0:T(8,128)(2,1)} %shard_map.59.a_ref, bf16[272,1280]{1,0:T(8,128)(2,1)} %copy-done.4), custom_call_target="tpu_custom_call" | custom-call | flops 1310720 | bytes 1966080 | tf_op jit(solution)/shard_map/pallas_call | solution.py:184
  126.8 10.7 %collective-permute-done.8.b_ref = bf16[272,1280]{1,0:T(8,128)(2,1)S(1)} collective-permute-done((bf16[272,1280]{1,0:T(8,128)(2,1)}, bf16[272,1280]{1,0:T(8,128)(2,1)S(1)}, u32[]{:S(2)}, u32[]{:S(2)}) %collective-permute-start.8) | collective-permute-done | bytes 696352 | tf_op jit(solution)/shard_map/ppermute | solution.py:205
  138.3 2.9 %shard_map.64 = bf16[256,2560]{1,0:T(8,128)(2,1)} custom-call(s32[1]{0:T(128)} %bitcast.valid_ref, bf16[272,1280]{1,0:T(8,128)(2,1)} %shard_map.61.a_ref, bf16[272,1280]{1,0:T(8,128)(2,1)} %copy-done.7, bf16[256,2560]{1,0:T(8,128)(2,1)} %shard_map.63.rest_0_), custom_call_target="tpu_custom_call", output_to_operand_aliasing={{}: (3, {})} | custom-call | flops 1310720 | bytes 1966080 | tf_op jit(solution)/shard_map/pallas_call | solution.py:184
  (41 shorter events, 15.7 us)
Async XLA Ops:
  0.0 2.6 %copy-start.1 = (bf16[1,256,2560]{2,1,0:T(8,128)(2,1)S(1)}, bf16[1,256,2560]{2,1,0:T(8,128)(2,1)}, u32[]{:S(2)}) copy-start(bf16[1,256,2560]{2,1,0:T(8,128)(2,1)} %param.9) | copy-start | bytes 3932164
  2.6 6.1 %copy-start.9 = (s32[1,1,2]{2,1,0:T(1,128)S(1)}, s32[1,1,2]{2,1,0:T(1,128)}, u32[]{:S(2)}) copy-start(s32[1,1,2]{2,1,0:T(1,128)} %param.11) | copy-start | bytes 28
  2.6 6.2 %copy-start.2 = (bf16[1,256,2560]{2,1,0:T(8,128)(2,1)S(1)}, bf16[1,256,2560]{2,1,0:T(8,128)(2,1)}, u32[]{:S(2)}) copy-start(bf16[1,256,2560]{2,1,0:T(8,128)(2,1)} %param.7) | copy-start | bytes 3932164
  3.8 36.8 %collective-permute-start.4 = (bf16[2,256,2560]{2,1,0:T(8,128)(2,1)}, bf16[2,256,2560]{2,1,0:T(8,128)(2,1)S(1)}, u32[]{:S(2)}, u32[]{:S(2)}) collective-permute-start(bf16[2,256,2560]{2,1,0:T(8,128)(2,1)} %constant_dynamic-update-slice_fusion), channel_id=1, source_target_pairs={{1,0},{2,1},{3,2},{4,3},{5,4},{6,5},{7,6},{9,8},{10,9},{11,10},{12... | collective-permute-start | bytes 7864328 | tf_op jit(solution)/shard_map/ppermute | solution.py:239
  5.7 34.9 %collective-permute-start.3 = (bf16[2,256,2560]{2,1,0:T(8,128)(2,1)}, bf16[2,256,2560]{2,1,0:T(8,128)(2,1)}, u32[]{:S(2)}, u32[]{:S(2)}) collective-permute-start(bf16[2,256,2560]{2,1,0:T(8,128)(2,1)} %constant_dynamic-update-slice_fusion), channel_id=1, source_target_pairs={{0,1},{1,2},{2,3},{3,4},{4,5},{5,6},{6,7},{8,9},{9,10},{10,11},{11... | collective-permute-start | bytes 7864328 | tf_op jit(solution)/shard_map/ppermute | solution.py:238
  9.8 20.4 %collective-permute-start = (bf16[272,1280]{1,0:T(8,128)(2,1)S(1)}, bf16[272,1280]{1,0:T(8,128)(2,1)}, u32[]{:S(2)}, u32[]{:S(2)}) collective-permute-start(bf16[272,1280]{1,0:T(8,128)(2,1)S(1)} %pad_maximum_fusion), channel_id=1, source_target_pairs={{8,0},{16,8},{24,16},{32,24},{40,32},{48,40},{56,48},{64,56},{72,6... | collective-permute-start | bytes 2088968 | tf_op jit(solution)/shard_map/ppermute | solution.py:205
  14.3 35.4 %collective-permute-start.2 = (bf16[256,1280]{1,0:T(8,128)(2,1)}, bf16[256,1280]{1,0:T(8,128)(2,1)}, u32[]{:S(2)}, u32[]{:S(2)}) collective-permute-start(bf16[256,1280]{1,0:T(8,128)(2,1)} %get-tuple-element.35), channel_id=1, source_target_pairs={{8,0},{16,8},{24,16},{32,24},{40,32},{48,40},{56,48},{64,56},{72,6... | collective-permute-start | bytes 1966088 | tf_op jit(solution)/shard_map/ppermute | solution.py:205
  30.2 29.1 %collective-permute-start.1 = (bf16[272,1280]{1,0:T(8,128)(2,1)}, bf16[272,1280]{1,0:T(8,128)(2,1)S(1)}, u32[]{:S(2)}, u32[]{:S(2)}) collective-permute-start(bf16[272,1280]{1,0:T(8,128)(2,1)} %collective-permute-done.q_ref), channel_id=1, source_target_pairs={{8,0},{16,8},{24,16},{32,24},{40,32},{48,40},{56,48},{64,56},{72,6... | collective-permute-start | bytes 2088968 | tf_op jit(solution)/shard_map/ppermute | solution.py:205
  40.6 1.6 %copy-start = (bf16[2,256,2560]{2,1,0:T(8,128)(2,1)}, bf16[2,256,2560]{2,1,0:T(8,128)(2,1)S(1)}, u32[]{:S(2)}) copy-start(bf16[2,256,2560]{2,1,0:T(8,128)(2,1)S(1)} %collective-permute-done.4.kr_ref.vr_ref) | copy-start | bytes 7864324
  57.3 18.8 %collective-permute-start.5 = (bf16[256,1280]{1,0:T(8,128)(2,1)}, bf16[256,1280]{1,0:T(8,128)(2,1)S(1)}, u32[]{:S(2)}, u32[]{:S(2)}) collective-permute-start(bf16[256,1280]{1,0:T(8,128)(2,1)} %collective-permute-done.2.q_ref), channel_id=1, source_target_pairs={{8,0},{16,8},{24,16},{32,24},{40,32},{48,40},{56,48},{64,56},{72,6... | collective-permute-start | bytes 1966088 | tf_op jit(solution)/shard_map/ppermute | solution.py:205
  59.3 3.3 %copy-start.3 = (bf16[272,1280]{1,0:T(8,128)(2,1)}, bf16[272,1280]{1,0:T(8,128)(2,1)S(1)}, u32[]{:S(2)}) copy-start(bf16[272,1280]{1,0:T(8,128)(2,1)S(1)} %collective-permute-done.1.q_ref) | copy-start | bytes 2088964
  66.4 27.4 %collective-permute-start.7 = (bf16[272,1280]{1,0:T(8,128)(2,1)}, bf16[272,1280]{1,0:T(8,128)(2,1)S(1)}, u32[]{:S(2)}, u32[]{:S(2)}) collective-permute-start(bf16[272,1280]{1,0:T(8,128)(2,1)} %shard_map.58), channel_id=1, source_target_pairs={{0,8},{8,16},{16,24},{24,32},{32,40},{40,48},{48,56},{56,64},{64,7... | collective-permute-start | bytes 2088968 | tf_op jit(solution)/shard_map/ppermute | solution.py:205
  76.1 0.9 copy-start.8
  80.7 27.4 %collective-permute-start.6 = (bf16[272,1280]{1,0:T(8,128)(2,1)}, bf16[272,1280]{1,0:T(8,128)(2,1)S(1)}, u32[]{:S(2)}, u32[]{:S(2)}) collective-permute-start(bf16[272,1280]{1,0:T(8,128)(2,1)} %shard_map.57), channel_id=1, source_target_pairs={{0,8},{8,16},{16,24},{24,32},{32,40},{40,48},{48,56},{56,64},{64,7... | collective-permute-start | bytes 2088968 | tf_op jit(solution)/shard_map/ppermute | solution.py:205
  93.7 0.9 copy-start.6
  97.5 25.5 %collective-permute-start.9 = (bf16[272,1280]{1,0:T(8,128)(2,1)}, bf16[272,1280]{1,0:T(8,128)(2,1)S(1)}, u32[]{:S(2)}, u32[]{:S(2)}) collective-permute-start(bf16[272,1280]{1,0:T(8,128)(2,1)} %shard_map.60), channel_id=1, source_target_pairs={{0,8},{8,16},{16,24},{24,32},{32,40},{40,48},{48,56},{56,64},{64,7... | collective-permute-start | bytes 2088968 | tf_op jit(solution)/shard_map/ppermute | solution.py:205
  108.1 0.9 copy-start.5
  111.9 25.5 %collective-permute-start.8 = (bf16[272,1280]{1,0:T(8,128)(2,1)}, bf16[272,1280]{1,0:T(8,128)(2,1)S(1)}, u32[]{:S(2)}, u32[]{:S(2)}) collective-permute-start(bf16[272,1280]{1,0:T(8,128)(2,1)} %shard_map.62), channel_id=1, source_target_pairs={{0,8},{8,16},{16,24},{24,32},{32,40},{40,48},{48,56},{56,64},{64,7... | collective-permute-start | bytes 2088968 | tf_op jit(solution)/shard_map/ppermute | solution.py:205
  123.0 0.9 copy-start.4
  137.4 0.9 copy-start.7

commit v10 on v9

--- a/solution.py
+++ b/solution.py
@@ -252,17 +252,19 @@
     f2 = flags_for(q2s[0][rows, 0:3], 2)
     p2s = [attend(f2, q2s[c], k, v, kv_l, kv_r, chunk_w, c * groups_c, 0) for c in range(CHUNKS)]
     p2_ins = [shift_tm(p2, 1) for p2 in p2s]
-    after = p2s[-1]
     result = None
+    p_self = None
     for c in range(CHUNKS):
         base = c * groups_c
-        q_self, _ = lax.optimization_barrier((q, after))
+        p2_in = p2_ins[c]
+        if p_self is not None:
+            p2_in, p_self = lax.optimization_barrier((p2_in, p_self))
+            result = merge(valid, p_self, pcs_in, base - groups_c, final=True, buf=result, out_width=width)
+        pc = merge(valid, p1s[c], p2_in, 0)
+        pcs_in = shift_tm(pc, 1)
+        q_self, _ = lax.optimization_barrier((q, pc))
         p_self = attend(f0, q_self, k, v, kv_l, kv_r, chunk_w, base, base)
-        p2_in, p_self = lax.optimization_barrier((p2_ins[c], p_self))
-        pc = merge(valid, p1s[c], p2_in, 0)
-        after = pc
-        pc_in = shift_tm(pc, 1)
-        result = merge(valid, p_self, pc_in, base, final=True, buf=result, out_width=width)
+    result = merge(valid, p_self, pcs_in, (CHUNKS - 1) * groups_c, final=True, buf=result, out_width=width)
     return result.reshape(1, rows, width)
 
 

time: 142 us -> 142 us (level)
  the two profiles are of different devices: /device:TPU:112 before, /device:TPU:72 now
where the time goes in v10:
time: 142 us; the launch traced here: 140 us
  Pallas kernels  57.1 us (40%)
  waiting for transfers between devices  32.5 us (23%)
  starting transfers between devices  28.5 us (20%)
  local copies, waits for them, and re-layouts  12.7 us (9%)
  between operations  6.62 us (5%)
  other arithmetic  2.73 us (2%)
    pallas_call x6, Pallas kernels, attend(): pl.pallas_call(_attn_kernel, out_shape=jax.ShapeDtypeStruct((rows + EXTRA...  45.5 us
    ppermute x8, waiting for transfers between devices, shift_tm(): return lax.ppermute(x, 'tm', pairs)  32.5 us
    ppermute x8, starting transfers between devices, shift_tm(): return lax.ppermute(x, 'tm', pairs)  23 us
    pallas_call x4, Pallas kernels, merge(): pl.pallas_call(kernel, out_shape=out_shape, grid_spec=pltpu.PrefetchScala...  11.7 us
    unnamed x21, local copies, waits for them, and re-layouts  8.51 us
    ppermute x1, starting transfers between devices, on_device(): kv_r = lax.ppermute(kv, 'space', [(i + 1, i) for i in range(tiles - 1)])  3.64 us
  transfers between devices with their start and end apart: 10, of which 6 were waited for; matrix products, arithmetic and copies ran while one was open for 4% of the time, Pallas kernels for 39%

profile of v10, /device:TPU:72, one launch (start us, length us, event | category | flops | bytes accessed | tf_op | source)
XLA Modules:
  0.0 140.2 jit_solution(14548309137589783815)
XLA Ops:
  0.0 2.6 %constant_dynamic-update-slice_fusion.1 = bf16[2,256,2560]{2,1,0:T(8,128)(2,1)} fusion(bf16[1,256,2560]{2,1,0:T(8,128)(2,1)} %param.8), kind=kLoop, calls=%fused_computation.10 | loop fusion | bytes 2621440
  3.8 1.9 %collective-permute-start.2 = (bf16[2,256,2560]{2,1,0:T(8,128)(2,1)}, bf16[2,256,2560]{2,1,0:T(8,128)(2,1)S(1)}, u32[]{:S(2)}, u32[]{:S(2)}) collective-permute-start(bf16[2,256,2560]{2,1,0:T(8,128)(2,1)} %constant_dynamic-update-slice_fusion), channel_id=1, source_target_pairs={{0,1},{1,2},{2,3},{3,4},{4,5},{5,6},{6,7},{8,9},{9,10},{10,11},{11... | collective-permute-start | bytes 7864328 | tf_op jit(solution)/shard_map/ppermute | solution.py:238
  5.7 3.6 %collective-permute-start.3 = (bf16[2,256,2560]{2,1,0:T(8,128)(2,1)}, bf16[2,256,2560]{2,1,0:T(8,128)(2,1)}, u32[]{:S(2)}, u32[]{:S(2)}) collective-permute-start(bf16[2,256,2560]{2,1,0:T(8,128)(2,1)} %constant_dynamic-update-slice_fusion), channel_id=1, source_target_pairs={{1,0},{2,1},{3,2},{4,3},{5,4},{6,5},{7,6},{9,8},{10,9},{11,10},{12... | collective-permute-start | bytes 7864328 | tf_op jit(solution)/shard_map/ppermute | solution.py:239
  11.1 4.2 %collective-permute-start.1 = (bf16[272,1280]{1,0:T(8,128)(2,1)S(1)}, bf16[272,1280]{1,0:T(8,128)(2,1)}, u32[]{:S(2)}, u32[]{:S(2)}) collective-permute-start(bf16[272,1280]{1,0:T(8,128)(2,1)S(1)} %pad_maximum_fusion), channel_id=1, source_target_pairs={{8,0},{16,8},{24,16},{32,24},{40,32},{48,40},{56,48},{64,56},{72,6... | collective-permute-start | bytes 2088968 | tf_op jit(solution)/shard_map/ppermute | solution.py:205
  15.3 2.7 %collective-permute-start = (bf16[256,1280]{1,0:T(8,128)(2,1)}, bf16[256,1280]{1,0:T(8,128)(2,1)}, u32[]{:S(2)}, u32[]{:S(2)}) collective-permute-start(bf16[256,1280]{1,0:T(8,128)(2,1)} %get-tuple-element.32), channel_id=1, source_target_pairs={{8,0},{16,8},{24,16},{32,24},{40,32},{48,40},{56,48},{64,56},{72,6... | collective-permute-start | bytes 1966088 | tf_op jit(solution)/shard_map/ppermute | solution.py:205
  18.0 13.5 %collective-permute-done.1.q_ref = bf16[272,1280]{1,0:T(8,128)(2,1)} collective-permute-done((bf16[272,1280]{1,0:T(8,128)(2,1)S(1)}, bf16[272,1280]{1,0:T(8,128)(2,1)}, u32[]{:S(2)}, u32[]{:S(2)}) %collective-permute-start.1) | collective-permute-done | bytes 696352 | tf_op jit(solution)/shard_map/ppermute | solution.py:205
  31.5 6.3 %collective-permute-start.4 = (bf16[272,1280]{1,0:T(8,128)(2,1)}, bf16[272,1280]{1,0:T(8,128)(2,1)S(1)}, u32[]{:S(2)}, u32[]{:S(2)}) collective-permute-start(bf16[272,1280]{1,0:T(8,128)(2,1)} %collective-permute-done.1.q_ref), channel_id=1, source_target_pairs={{8,0},{16,8},{24,16},{32,24},{40,32},{48,40},{56,48},{64,56},{72,6... | collective-permute-start | bytes 2088968 | tf_op jit(solution)/shard_map/ppermute | solution.py:205
  43.3 7.6 %shard_map.55.a_ref = bf16[272,1280]{1,0:T(8,128)(2,1)} custom-call(s32[3]{0:T(128)} %add_convert_fusion.1.flags_ref, bf16[272,1280]{1,0:T(8,128)(2,1)} %collective-permute-done.1.q_ref, bf16[2,256,2560]{2,1,0:T(8,128)(2,1)} %copy-done, bf16[256,2560]{1,0:T(8,128)(2,1)} %bitcast.24, bf16[2,256,2560]{2,1,0:T(8,128)(2,1)} %collective-permute-done.3.kr_ref.vr_ref, ...), custom_call_target="tpu_custom_call" | custom-call | flops 1006632960 | bytes 5242880 | tf_op jit(solution)/shard_map/pallas_call | solution.py:100
  50.8 7.6 %shard_map.56.a_ref = bf16[272,1280]{1,0:T(8,128)(2,1)} custom-call(s32[3]{0:T(128)} %add_convert_fusion.1.flags_ref, bf16[256,1280]{1,0:T(8,128)(2,1)} %collective-permute-done.q_ref, bf16[2,256,2560]{2,1,0:T(8,128)(2,1)} %copy-done, bf16[256,2560]{1,0:T(8,128)(2,1)} %bitcast.25, bf16[2,256,2560]{2,1,0:T(8,128)(2,1)} %collective-permute-done.3.kr_ref.vr_ref, ...), custom_call_target="tpu_custom_call" | custom-call | flops 1006632960 | bytes 5242880 | tf_op jit(solution)/shard_map/pallas_call | solution.py:100
  58.4 1.9 %collective-permute-start.5 = (bf16[256,1280]{1,0:T(8,128)(2,1)}, bf16[256,1280]{1,0:T(8,128)(2,1)S(1)}, u32[]{:S(2)}, u32[]{:S(2)}) collective-permute-start(bf16[256,1280]{1,0:T(8,128)(2,1)} %collective-permute-done.q_ref), channel_id=1, source_target_pairs={{8,0},{16,8},{24,16},{32,24},{40,32},{48,40},{56,48},{64,56},{72,6... | collective-permute-start | bytes 1966088 | tf_op jit(solution)/shard_map/ppermute | solution.py:205
  63.7 7.6 %shard_map.58 = bf16[272,1280]{1,0:T(8,128)(2,1)} custom-call(s32[3]{0:T(128)} %add_convert_fusion.2.flags_ref, bf16[272,1280]{1,0:T(8,128)(2,1)} %copy-done.3, bf16[2,256,2560]{2,1,0:T(8,128)(2,1)} %copy-done, bf16[256,2560]{1,0:T(8,128)(2,1)} %bitcast.26, bf16[2,256,2560]{2,1,0:T(8,128)(2,1)} %collective-permute-done.3.kr_ref.vr_ref, ...), custom_call_target="tpu_custom_call" | custom-call | flops 1006632960 | bytes 5242880 | tf_op jit(solution)/shard_map/pallas_call | solution.py:100
  71.2 1.9 %collective-permute-start.7 = (bf16[272,1280]{1,0:T(8,128)(2,1)}, bf16[272,1280]{1,0:T(8,128)(2,1)S(1)}, u32[]{:S(2)}, u32[]{:S(2)}) collective-permute-start(bf16[272,1280]{1,0:T(8,128)(2,1)} %shard_map.58), channel_id=1, source_target_pairs={{0,8},{8,16},{16,24},{24,32},{32,40},{40,48},{48,56},{56,64},{64,7... | collective-permute-start | bytes 2088968 | tf_op jit(solution)/shard_map/ppermute | solution.py:205
  75.8 7.6 %shard_map.57 = bf16[272,1280]{1,0:T(8,128)(2,1)} custom-call(s32[3]{0:T(128)} %add_convert_fusion.2.flags_ref, bf16[256,1280]{1,0:T(8,128)(2,1)} %copy-done.8, bf16[2,256,2560]{2,1,0:T(8,128)(2,1)} %copy-done, bf16[256,2560]{1,0:T(8,128)(2,1)} %bitcast.27, bf16[2,256,2560]{2,1,0:T(8,128)(2,1)} %collective-permute-done.3.kr_ref.vr_ref, ...), custom_call_target="tpu_custom_call" | custom-call | flops 1006632960 | bytes 5242880 | tf_op jit(solution)/shard_map/pallas_call | solution.py:100
  83.4 1.9 %collective-permute-start.6 = (bf16[272,1280]{1,0:T(8,128)(2,1)}, bf16[272,1280]{1,0:T(8,128)(2,1)S(1)}, u32[]{:S(2)}, u32[]{:S(2)}) collective-permute-start(bf16[272,1280]{1,0:T(8,128)(2,1)} %shard_map.57), channel_id=1, source_target_pairs={{0,8},{8,16},{16,24},{24,32},{32,40},{40,48},{48,56},{56,64},{64,7... | collective-permute-start | bytes 2088968 | tf_op jit(solution)/shard_map/ppermute | solution.py:205
  88.7 5.3 %collective-permute-done.7.b_ref = bf16[272,1280]{1,0:T(8,128)(2,1)S(1)} collective-permute-done((bf16[272,1280]{1,0:T(8,128)(2,1)}, bf16[272,1280]{1,0:T(8,128)(2,1)S(1)}, u32[]{:S(2)}, u32[]{:S(2)}) %collective-permute-start.7) | collective-permute-done | bytes 696352 | tf_op jit(solution)/shard_map/ppermute | solution.py:205
  94.9 2.9 %shard_map.59 = bf16[272,1280]{1,0:T(8,128)(2,1)} custom-call(s32[1]{0:T(128)} %bitcast.valid_ref, bf16[272,1280]{1,0:T(8,128)(2,1)} %shard_map.55.a_ref, bf16[272,1280]{1,0:T(8,128)(2,1)} %copy-done.6), custom_call_target="tpu_custom_call" | custom-call | flops 1310720 | bytes 1966080 | tf_op jit(solution)/shard_map/pallas_call | solution.py:184
  97.8 2.1 %collective-permute-start.9 = (bf16[272,1280]{1,0:T(8,128)(2,1)}, bf16[272,1280]{1,0:T(8,128)(2,1)S(1)}, u32[]{:S(2)}, u32[]{:S(2)}) collective-permute-start(bf16[272,1280]{1,0:T(8,128)(2,1)} %shard_map.59), channel_id=1, source_target_pairs={{0,8},{8,16},{16,24},{24,32},{32,40},{40,48},{48,56},{56,64},{64,7... | collective-permute-start | bytes 2088968 | tf_op jit(solution)/shard_map/ppermute | solution.py:205
  99.9 7.6 %shard_map.60.a_ref = bf16[272,1280]{1,0:T(8,128)(2,1)} custom-call(s32[3]{0:T(128)} %add_convert_fusion.flags_ref, bf16[256,2560]{1,0:T(8,128)(2,1)} %bitcast.36, bf16[2,256,2560]{2,1,0:T(8,128)(2,1)} %copy-done, bf16[256,2560]{1,0:T(8,128)(2,1)} %bitcast.28, bf16[2,256,2560]{2,1,0:T(8,128)(2,1)} %collective-permute-done.3.kr_ref.vr_ref, ...), custom_call_target="tpu_custom_call" | custom-call | flops 1006632960 | bytes 5242880 | tf_op jit(solution)/shard_map/pallas_call | solution.py:100
  109.8 2.9 %shard_map.61 = bf16[272,1280]{1,0:T(8,128)(2,1)} custom-call(s32[1]{0:T(128)} %bitcast.valid_ref, bf16[272,1280]{1,0:T(8,128)(2,1)} %shard_map.56.a_ref, bf16[272,1280]{1,0:T(8,128)(2,1)} %copy-done.5), custom_call_target="tpu_custom_call" | custom-call | flops 1310720 | bytes 1966080 | tf_op jit(solution)/shard_map/pallas_call | solution.py:184
  112.7 1.9 %collective-permute-start.8 = (bf16[272,1280]{1,0:T(8,128)(2,1)}, bf16[272,1280]{1,0:T(8,128)(2,1)S(1)}, u32[]{:S(2)}, u32[]{:S(2)}) collective-permute-start(bf16[272,1280]{1,0:T(8,128)(2,1)} %shard_map.61), channel_id=1, source_target_pairs={{0,8},{8,16},{16,24},{24,32},{32,40},{40,48},{48,56},{56,64},{64,7... | collective-permute-start | bytes 2088968 | tf_op jit(solution)/shard_map/ppermute | solution.py:205
  114.6 7.6 %shard_map.62.a_ref = bf16[272,1280]{1,0:T(8,128)(2,1)} custom-call(s32[3]{0:T(128)} %add_convert_fusion.flags_ref, bf16[256,2560]{1,0:T(8,128)(2,1)} %bitcast.37, bf16[2,256,2560]{2,1,0:T(8,128)(2,1)} %copy-done, bf16[256,2560]{1,0:T(8,128)(2,1)} %bitcast.29, bf16[2,256,2560]{2,1,0:T(8,128)(2,1)} %collective-permute-done.3.kr_ref.vr_ref, ...), custom_call_target="tpu_custom_call" | custom-call | flops 1006632960 | bytes 5242880 | tf_op jit(solution)/shard_map/pallas_call | solution.py:100
  124.7 2.9 %shard_map.63.rest_0_ = bf16[256,2560]{1,0:T(8,128)(2,1)} custom-call(s32[1]{0:T(128)} %bitcast.valid_ref, bf16[272,1280]{1,0:T(8,128)(2,1)} %shard_map.60.a_ref, bf16[272,1280]{1,0:T(8,128)(2,1)} %copy-done.4), custom_call_target="tpu_custom_call" | custom-call | flops 1310720 | bytes 1966080 | tf_op jit(solution)/shard_map/pallas_call | solution.py:184
  127.6 8.9 %collective-permute-done.8.b_ref = bf16[272,1280]{1,0:T(8,128)(2,1)S(1)} collective-permute-done((bf16[272,1280]{1,0:T(8,128)(2,1)}, bf16[272,1280]{1,0:T(8,128)(2,1)S(1)}, u32[]{:S(2)}, u32[]{:S(2)}) %collective-permute-start.8) | collective-permute-done | bytes 696352 | tf_op jit(solution)/shard_map/ppermute | solution.py:205
  137.3 2.9 %shard_map.64 = bf16[256,2560]{1,0:T(8,128)(2,1)} custom-call(s32[1]{0:T(128)} %bitcast.valid_ref, bf16[272,1280]{1,0:T(8,128)(2,1)} %shard_map.62.a_ref, bf16[272,1280]{1,0:T(8,128)(2,1)} %copy-done.7, bf16[256,2560]{1,0:T(8,128)(2,1)} %shard_map.63.rest_0_), custom_call_target="tpu_custom_call", output_to_operand_aliasing={{}: (3, {})} | custom-call | flops 1310720 | bytes 1966080 | tf_op jit(solution)/shard_map/pallas_call | solution.py:184
  (41 shorter events, 17.6 us)
Async XLA Ops:
  0.0 2.6 %copy-start.1 = (bf16[1,256,2560]{2,1,0:T(8,128)(2,1)S(1)}, bf16[1,256,2560]{2,1,0:T(8,128)(2,1)}, u32[]{:S(2)}) copy-start(bf16[1,256,2560]{2,1,0:T(8,128)(2,1)} %param.9) | copy-start | bytes 3932164
  2.6 7.4 %copy-start.9 = (s32[1,1,2]{2,1,0:T(1,128)S(1)}, s32[1,1,2]{2,1,0:T(1,128)}, u32[]{:S(2)}) copy-start(s32[1,1,2]{2,1,0:T(1,128)} %param.11) | copy-start | bytes 28
  2.6 7.5 %copy-start.2 = (bf16[1,256,2560]{2,1,0:T(8,128)(2,1)S(1)}, bf16[1,256,2560]{2,1,0:T(8,128)(2,1)}, u32[]{:S(2)}) copy-start(bf16[1,256,2560]{2,1,0:T(8,128)(2,1)} %param.7) | copy-start | bytes 3932164
  3.8 37.9 %collective-permute-start.2 = (bf16[2,256,2560]{2,1,0:T(8,128)(2,1)}, bf16[2,256,2560]{2,1,0:T(8,128)(2,1)S(1)}, u32[]{:S(2)}, u32[]{:S(2)}) collective-permute-start(bf16[2,256,2560]{2,1,0:T(8,128)(2,1)} %constant_dynamic-update-slice_fusion), channel_id=1, source_target_pairs={{0,1},{1,2},{2,3},{3,4},{4,5},{5,6},{6,7},{8,9},{9,10},{10,11},{11... | collective-permute-start | bytes 7864328 | tf_op jit(solution)/shard_map/ppermute | solution.py:238
  5.7 36.0 %collective-permute-start.3 = (bf16[2,256,2560]{2,1,0:T(8,128)(2,1)}, bf16[2,256,2560]{2,1,0:T(8,128)(2,1)}, u32[]{:S(2)}, u32[]{:S(2)}) collective-permute-start(bf16[2,256,2560]{2,1,0:T(8,128)(2,1)} %constant_dynamic-update-slice_fusion), channel_id=1, source_target_pairs={{1,0},{2,1},{3,2},{4,3},{5,4},{6,5},{7,6},{9,8},{10,9},{11,10},{12... | collective-permute-start | bytes 7864328 | tf_op jit(solution)/shard_map/ppermute | solution.py:239
  11.1 20.5 %collective-permute-start.1 = (bf16[272,1280]{1,0:T(8,128)(2,1)S(1)}, bf16[272,1280]{1,0:T(8,128)(2,1)}, u32[]{:S(2)}, u32[]{:S(2)}) collective-permute-start(bf16[272,1280]{1,0:T(8,128)(2,1)S(1)} %pad_maximum_fusion), channel_id=1, source_target_pairs={{8,0},{16,8},{24,16},{32,24},{40,32},{48,40},{56,48},{64,56},{72,6... | collective-permute-start | bytes 2088968 | tf_op jit(solution)/shard_map/ppermute | solution.py:205
  15.3 35.6 %collective-permute-start = (bf16[256,1280]{1,0:T(8,128)(2,1)}, bf16[256,1280]{1,0:T(8,128)(2,1)}, u32[]{:S(2)}, u32[]{:S(2)}) collective-permute-start(bf16[256,1280]{1,0:T(8,128)(2,1)} %get-tuple-element.32), channel_id=1, source_target_pairs={{8,0},{16,8},{24,16},{32,24},{40,32},{48,40},{56,48},{64,56},{72,6... | collective-permute-start | bytes 1966088 | tf_op jit(solution)/shard_map/ppermute | solution.py:205
  31.5 28.8 %collective-permute-start.4 = (bf16[272,1280]{1,0:T(8,128)(2,1)}, bf16[272,1280]{1,0:T(8,128)(2,1)S(1)}, u32[]{:S(2)}, u32[]{:S(2)}) collective-permute-start(bf16[272,1280]{1,0:T(8,128)(2,1)} %collective-permute-done.1.q_ref), channel_id=1, source_target_pairs={{8,0},{16,8},{24,16},{32,24},{40,32},{48,40},{56,48},{64,56},{72,6... | collective-permute-start | bytes 2088968 | tf_op jit(solution)/shard_map/ppermute | solution.py:205
  41.7 1.6 %copy-start = (bf16[2,256,2560]{2,1,0:T(8,128)(2,1)}, bf16[2,256,2560]{2,1,0:T(8,128)(2,1)S(1)}, u32[]{:S(2)}) copy-start(bf16[2,256,2560]{2,1,0:T(8,128)(2,1)S(1)} %collective-permute-done.2.kl_ref.vl_ref) | copy-start | bytes 7864324
  58.4 16.5 %collective-permute-start.5 = (bf16[256,1280]{1,0:T(8,128)(2,1)}, bf16[256,1280]{1,0:T(8,128)(2,1)S(1)}, u32[]{:S(2)}, u32[]{:S(2)}) collective-permute-start(bf16[256,1280]{1,0:T(8,128)(2,1)} %collective-permute-done.q_ref), channel_id=1, source_target_pairs={{8,0},{16,8},{24,16},{32,24},{40,32},{48,40},{56,48},{64,56},{72,6... | collective-permute-start | bytes 1966088 | tf_op jit(solution)/shard_map/ppermute | solution.py:205
  60.3 3.3 %copy-start.3 = (bf16[272,1280]{1,0:T(8,128)(2,1)}, bf16[272,1280]{1,0:T(8,128)(2,1)S(1)}, u32[]{:S(2)}) copy-start(bf16[272,1280]{1,0:T(8,128)(2,1)S(1)} %collective-permute-done.4.q_ref) | copy-start | bytes 2088964
  71.2 22.8 %collective-permute-start.7 = (bf16[272,1280]{1,0:T(8,128)(2,1)}, bf16[272,1280]{1,0:T(8,128)(2,1)S(1)}, u32[]{:S(2)}, u32[]{:S(2)}) collective-permute-start(bf16[272,1280]{1,0:T(8,128)(2,1)} %shard_map.58), channel_id=1, source_target_pairs={{0,8},{8,16},{16,24},{24,32},{32,40},{40,48},{48,56},{56,64},{64,7... | collective-permute-start | bytes 2088968 | tf_op jit(solution)/shard_map/ppermute | solution.py:205
  74.9 0.9 copy-start.8
  83.4 25.5 %collective-permute-start.6 = (bf16[272,1280]{1,0:T(8,128)(2,1)}, bf16[272,1280]{1,0:T(8,128)(2,1)S(1)}, u32[]{:S(2)}, u32[]{:S(2)}) collective-permute-start(bf16[272,1280]{1,0:T(8,128)(2,1)} %shard_map.57), channel_id=1, source_target_pairs={{0,8},{8,16},{16,24},{24,32},{32,40},{40,48},{48,56},{56,64},{64,7... | collective-permute-start | bytes 2088968 | tf_op jit(solution)/shard_map/ppermute | solution.py:205
  94.0 0.9 copy-start.6
  97.8 26.0 %collective-permute-start.9 = (bf16[272,1280]{1,0:T(8,128)(2,1)}, bf16[272,1280]{1,0:T(8,128)(2,1)S(1)}, u32[]{:S(2)}, u32[]{:S(2)}) collective-permute-start(bf16[272,1280]{1,0:T(8,128)(2,1)} %shard_map.59), channel_id=1, source_target_pairs={{0,8},{8,16},{16,24},{24,32},{32,40},{40,48},{48,56},{56,64},{64,7... | collective-permute-start | bytes 2088968 | tf_op jit(solution)/shard_map/ppermute | solution.py:205
  108.9 0.9 copy-start.5
  112.7 23.7 %collective-permute-start.8 = (bf16[272,1280]{1,0:T(8,128)(2,1)}, bf16[272,1280]{1,0:T(8,128)(2,1)S(1)}, u32[]{:S(2)}, u32[]{:S(2)}) collective-permute-start(bf16[272,1280]{1,0:T(8,128)(2,1)} %shard_map.61), channel_id=1, source_target_pairs={{0,8},{8,16},{16,24},{24,32},{32,40},{40,48},{48,56},{56,64},{64,7... | collective-permute-start | bytes 2088968 | tf_op jit(solution)/shard_map/ppermute | solution.py:205
  123.8 0.9 copy-start.4
  136.4 0.9 copy-start.7

commit v11 on v9

--- a/solution.py
+++ b/solution.py
@@ -252,16 +252,13 @@
     f2 = flags_for(q2s[0][rows, 0:3], 2)
     p2s = [attend(f2, q2s[c], k, v, kv_l, kv_r, chunk_w, c * groups_c, 0) for c in range(CHUNKS)]
     p2_ins = [shift_tm(p2, 1) for p2 in p2s]
-    after = p2s[-1]
     result = None
     for c in range(CHUNKS):
         base = c * groups_c
-        q_self, _ = lax.optimization_barrier((q, after))
+        pc = merge(valid, p1s[c], p2_ins[c], 0)
+        pc_in = shift_tm(pc, 1)
+        q_self, _ = lax.optimization_barrier((q, pc))
         p_self = attend(f0, q_self, k, v, kv_l, kv_r, chunk_w, base, base)
-        p2_in, p_self = lax.optimization_barrier((p2_ins[c], p_self))
-        pc = merge(valid, p1s[c], p2_in, 0)
-        after = pc
-        pc_in = shift_tm(pc, 1)
         result = merge(valid, p_self, pc_in, base, final=True, buf=result, out_width=width)
     return result.reshape(1, rows, width)
 

time: 142 us -> 143 us (level)
  the two profiles are of different devices: /device:TPU:112 before, /device:TPU:30 now
where the time goes in v11:
time: 143 us
  Pallas kernels  49.5 us (35%)
  waiting for transfers between devices  42.2 us (30%)
  starting transfers between devices  28.9 us (20%)
  local copies, waits for them, and re-layouts  12.7 us (9%)
  between operations  6.63 us (5%)
  other arithmetic  2.79 us (2%)
    ppermute x8, waiting for transfers between devices, shift_tm(): return lax.ppermute(x, 'tm', pairs)  42.2 us
    pallas_call x6, Pallas kernels, attend(): pl.pallas_call(_attn_kernel, out_shape=jax.ShapeDtypeStruct((rows + EXTRA...  37.8 us
    ppermute x8, starting transfers between devices, shift_tm(): return lax.ppermute(x, 'tm', pairs)  23.4 us
    pallas_call x4, Pallas kernels, merge(): pl.pallas_call(kernel, out_shape=out_shape, grid_spec=pltpu.PrefetchScala...  11.7 us
    unnamed x21, local copies, waits for them, and re-layouts  8.5 us
    ppermute x1, starting transfers between devices, on_device(): kv_r = lax.ppermute(kv, 'space', [(i + 1, i) for i in range(tiles - 1)])  3.64 us
  transfers between devices with their start and end apart: 10, of which 6 were waited for; matrix products, arithmetic and copies ran while one was open for 4% of the time, Pallas kernels for 33%

profile of v11, /device:TPU:30, one launch (start us, length us, event | category | flops | bytes accessed | tf_op | source)
XLA Modules:
  0.0 142.7 jit_solution(17175391420183167259)
XLA Ops:
  0.0 2.6 %constant_dynamic-update-slice_fusion.1 = bf16[2,256,2560]{2,1,0:T(8,128)(2,1)} fusion(bf16[1,256,2560]{2,1,0:T(8,128)(2,1)} %param.8), kind=kLoop, calls=%fused_computation.10 | loop fusion | bytes 2621440
  5.7 3.6 %collective-permute-start.3 = (bf16[2,256,2560]{2,1,0:T(8,128)(2,1)}, bf16[2,256,2560]{2,1,0:T(8,128)(2,1)}, u32[]{:S(2)}, u32[]{:S(2)}) collective-permute-start(bf16[2,256,2560]{2,1,0:T(8,128)(2,1)} %constant_dynamic-update-slice_fusion), channel_id=1, source_target_pairs={{1,0},{2,1},{3,2},{4,3},{5,4},{6,5},{7,6},{9,8},{10,9},{11,10},{12... | collective-permute-start | bytes 7864328 | tf_op jit(solution)/shard_map/ppermute | solution.py:239
  11.1 2.7 %collective-permute-start.1 = (bf16[272,1280]{1,0:T(8,128)(2,1)S(1)}, bf16[272,1280]{1,0:T(8,128)(2,1)}, u32[]{:S(2)}, u32[]{:S(2)}) collective-permute-start(bf16[272,1280]{1,0:T(8,128)(2,1)S(1)} %pad_maximum_fusion), channel_id=1, source_target_pairs={{8,0},{16,8},{24,16},{32,24},{40,32},{48,40},{56,48},{64,56},{72,6... | collective-permute-start | bytes 2088968 | tf_op jit(solution)/shard_map/ppermute | solution.py:205
  13.8 2.4 %collective-permute-start = (bf16[256,1280]{1,0:T(8,128)(2,1)}, bf16[256,1280]{1,0:T(8,128)(2,1)}, u32[]{:S(2)}, u32[]{:S(2)}) collective-permute-start(bf16[256,1280]{1,0:T(8,128)(2,1)} %get-tuple-element.28), channel_id=1, source_target_pairs={{8,0},{16,8},{24,16},{32,24},{40,32},{48,40},{56,48},{64,56},{72,6... | collective-permute-start | bytes 1966088 | tf_op jit(solution)/shard_map/ppermute | solution.py:205
  16.3 17.3 %collective-permute-done.1.q_ref = bf16[272,1280]{1,0:T(8,128)(2,1)} collective-permute-done((bf16[272,1280]{1,0:T(8,128)(2,1)S(1)}, bf16[272,1280]{1,0:T(8,128)(2,1)}, u32[]{:S(2)}, u32[]{:S(2)}) %collective-permute-start.1) | collective-permute-done | bytes 696352 | tf_op jit(solution)/shard_map/ppermute | solution.py:205
  33.6 1.9 %collective-permute-start.4 = (bf16[272,1280]{1,0:T(8,128)(2,1)}, bf16[272,1280]{1,0:T(8,128)(2,1)S(1)}, u32[]{:S(2)}, u32[]{:S(2)}) collective-permute-start(bf16[272,1280]{1,0:T(8,128)(2,1)} %collective-permute-done.1.q_ref), channel_id=1, source_target_pairs={{8,0},{16,8},{24,16},{32,24},{40,32},{48,40},{56,48},{64,56},{72,6... | collective-permute-start | bytes 2088968 | tf_op jit(solution)/shard_map/ppermute | solution.py:205
  40.9 3.7 %shard_map.55.a_ref = bf16[272,1280]{1,0:T(8,128)(2,1)} custom-call(s32[3]{0:T(128)} %add_convert_fusion.1.flags_ref, bf16[272,1280]{1,0:T(8,128)(2,1)} %collective-permute-done.1.q_ref, bf16[2,256,2560]{2,1,0:T(8,128)(2,1)} %copy-done, bf16[256,2560]{1,0:T(8,128)(2,1)} %bitcast.24, bf16[2,256,2560]{2,1,0:T(8,128)(2,1)} %collective-permute-done.3.kr_ref.vr_ref, ...), custom_call_target="tpu_custom_call" | custom-call | flops 1006632960 | bytes 5242880 | tf_op jit(solution)/shard_map/pallas_call | solution.py:100
  44.7 3.0 %collective-permute-done.q_ref = bf16[256,1280]{1,0:T(8,128)(2,1)} collective-permute-done((bf16[256,1280]{1,0:T(8,128)(2,1)}, bf16[256,1280]{1,0:T(8,128)(2,1)}, u32[]{:S(2)}, u32[]{:S(2)}) %collective-permute-start) | collective-permute-done | bytes 655392 | tf_op jit(solution)/shard_map/ppermute | solution.py:205
  47.6 3.7 %shard_map.56.a_ref = bf16[272,1280]{1,0:T(8,128)(2,1)} custom-call(s32[3]{0:T(128)} %add_convert_fusion.1.flags_ref, bf16[256,1280]{1,0:T(8,128)(2,1)} %collective-permute-done.q_ref, bf16[2,256,2560]{2,1,0:T(8,128)(2,1)} %copy-done, bf16[256,2560]{1,0:T(8,128)(2,1)} %bitcast.25, bf16[2,256,2560]{2,1,0:T(8,128)(2,1)} %collective-permute-done.3.kr_ref.vr_ref, ...), custom_call_target="tpu_custom_call" | custom-call | flops 1006632960 | bytes 5242880 | tf_op jit(solution)/shard_map/pallas_call | solution.py:100
  53.3 8.6 %collective-permute-done.4.q_ref = bf16[272,1280]{1,0:T(8,128)(2,1)S(1)} collective-permute-done((bf16[272,1280]{1,0:T(8,128)(2,1)}, bf16[272,1280]{1,0:T(8,128)(2,1)S(1)}, u32[]{:S(2)}, u32[]{:S(2)}) %collective-permute-start.4) | collective-permute-done | bytes 696352 | tf_op jit(solution)/shard_map/ppermute | solution.py:205
  65.3 7.6 %shard_map.60 = bf16[272,1280]{1,0:T(8,128)(2,1)} custom-call(s32[3]{0:T(128)} %add_convert_fusion.2.flags_ref, bf16[272,1280]{1,0:T(8,128)(2,1)} %copy-done.3, bf16[2,256,2560]{2,1,0:T(8,128)(2,1)} %copy-done, bf16[256,2560]{1,0:T(8,128)(2,1)} %bitcast.26, bf16[2,256,2560]{2,1,0:T(8,128)(2,1)} %collective-permute-done.3.kr_ref.vr_ref, ...), custom_call_target="tpu_custom_call" | custom-call | flops 1006632960 | bytes 5242880 | tf_op jit(solution)/shard_map/pallas_call | solution.py:100
  72.9 2.2 %collective-permute-start.8 = (bf16[272,1280]{1,0:T(8,128)(2,1)}, bf16[272,1280]{1,0:T(8,128)(2,1)S(1)}, u32[]{:S(2)}, u32[]{:S(2)}) collective-permute-start(bf16[272,1280]{1,0:T(8,128)(2,1)} %shard_map.60), channel_id=1, source_target_pairs={{0,8},{8,16},{16,24},{24,32},{32,40},{40,48},{48,56},{56,64},{64,7... | collective-permute-start | bytes 2088968 | tf_op jit(solution)/shard_map/ppermute | solution.py:205
  76.7 7.6 %shard_map.57 = bf16[272,1280]{1,0:T(8,128)(2,1)} custom-call(s32[3]{0:T(128)} %add_convert_fusion.2.flags_ref, bf16[256,1280]{1,0:T(8,128)(2,1)} %copy-done.8, bf16[2,256,2560]{2,1,0:T(8,128)(2,1)} %copy-done, bf16[256,2560]{1,0:T(8,128)(2,1)} %bitcast.27, bf16[2,256,2560]{2,1,0:T(8,128)(2,1)} %collective-permute-done.3.kr_ref.vr_ref, ...), custom_call_target="tpu_custom_call" | custom-call | flops 1006632960 | bytes 5242880 | tf_op jit(solution)/shard_map/pallas_call | solution.py:100
  84.3 3.5 %collective-permute-start.6 = (bf16[272,1280]{1,0:T(8,128)(2,1)}, bf16[272,1280]{1,0:T(8,128)(2,1)S(1)}, u32[]{:S(2)}, u32[]{:S(2)}) collective-permute-start(bf16[272,1280]{1,0:T(8,128)(2,1)} %shard_map.57), channel_id=1, source_target_pairs={{0,8},{8,16},{16,24},{24,32},{32,40},{40,48},{48,56},{56,64},{64,7... | collective-permute-start | bytes 2088968 | tf_op jit(solution)/shard_map/ppermute | solution.py:205
  87.8 5.7 %collective-permute-done.8.b_ref = bf16[272,1280]{1,0:T(8,128)(2,1)S(1)} collective-permute-done((bf16[272,1280]{1,0:T(8,128)(2,1)}, bf16[272,1280]{1,0:T(8,128)(2,1)S(1)}, u32[]{:S(2)}, u32[]{:S(2)}) %collective-permute-start.8) | collective-permute-done | bytes 696352 | tf_op jit(solution)/shard_map/ppermute | solution.py:205
  94.4 2.9 %shard_map.61 = bf16[272,1280]{1,0:T(8,128)(2,1)} custom-call(s32[1]{0:T(128)} %bitcast.valid_ref, bf16[272,1280]{1,0:T(8,128)(2,1)} %shard_map.55.a_ref, bf16[272,1280]{1,0:T(8,128)(2,1)} %copy-done.5), custom_call_target="tpu_custom_call" | custom-call | flops 1310720 | bytes 1966080 | tf_op jit(solution)/shard_map/pallas_call | solution.py:184
  97.3 4.3 %collective-permute-start.9 = (bf16[272,1280]{1,0:T(8,128)(2,1)}, bf16[272,1280]{1,0:T(8,128)(2,1)S(1)}, u32[]{:S(2)}, u32[]{:S(2)}) collective-permute-start(bf16[272,1280]{1,0:T(8,128)(2,1)} %shard_map.61), channel_id=1, source_target_pairs={{0,8},{8,16},{16,24},{24,32},{32,40},{40,48},{48,56},{56,64},{64,7... | collective-permute-start | bytes 2088968 | tf_op jit(solution)/shard_map/ppermute | solution.py:205
  101.6 6.8 %collective-permute-done.6.b_ref = bf16[272,1280]{1,0:T(8,128)(2,1)S(1)} collective-permute-done((bf16[272,1280]{1,0:T(8,128)(2,1)}, bf16[272,1280]{1,0:T(8,128)(2,1)S(1)}, u32[]{:S(2)}, u32[]{:S(2)}) %collective-permute-start.6) | collective-permute-done | bytes 696352 | tf_op jit(solution)/shard_map/ppermute | solution.py:205
  109.3 2.9 %shard_map.58 = bf16[272,1280]{1,0:T(8,128)(2,1)} custom-call(s32[1]{0:T(128)} %bitcast.valid_ref, bf16[272,1280]{1,0:T(8,128)(2,1)} %shard_map.56.a_ref, bf16[272,1280]{1,0:T(8,128)(2,1)} %copy-done.6), custom_call_target="tpu_custom_call" | custom-call | flops 1310720 | bytes 1966080 | tf_op jit(solution)/shard_map/pallas_call | solution.py:184
  112.2 4.5 %collective-permute-start.7 = (bf16[272,1280]{1,0:T(8,128)(2,1)}, bf16[272,1280]{1,0:T(8,128)(2,1)S(1)}, u32[]{:S(2)}, u32[]{:S(2)}) collective-permute-start(bf16[272,1280]{1,0:T(8,128)(2,1)} %shard_map.58), channel_id=1, source_target_pairs={{0,8},{8,16},{16,24},{24,32},{32,40},{40,48},{48,56},{56,64},{64,7... | collective-permute-start | bytes 2088968 | tf_op jit(solution)/shard_map/ppermute | solution.py:205
  120.0 7.6 %shard_map.62.a_ref = bf16[272,1280]{1,0:T(8,128)(2,1)} custom-call(s32[3]{0:T(128)} %add_convert_fusion.flags_ref, bf16[256,2560]{1,0:T(8,128)(2,1)} %bitcast.36, bf16[2,256,2560]{2,1,0:T(8,128)(2,1)} %copy-done, bf16[256,2560]{1,0:T(8,128)(2,1)} %bitcast.28, bf16[2,256,2560]{2,1,0:T(8,128)(2,1)} %collective-permute-done.3.kr_ref.vr_ref, ...), custom_call_target="tpu_custom_call" | custom-call | flops 1006632960 | bytes 5242880 | tf_op jit(solution)/shard_map/pallas_call | solution.py:100
  127.6 7.6 %shard_map.59.a_ref = bf16[272,1280]{1,0:T(8,128)(2,1)} custom-call(s32[3]{0:T(128)} %add_convert_fusion.flags_ref, bf16[256,2560]{1,0:T(8,128)(2,1)} %bitcast.37, bf16[2,256,2560]{2,1,0:T(8,128)(2,1)} %copy-done, bf16[256,2560]{1,0:T(8,128)(2,1)} %bitcast.29, bf16[2,256,2560]{2,1,0:T(8,128)(2,1)} %collective-permute-done.3.kr_ref.vr_ref, ...), custom_call_target="tpu_custom_call" | custom-call | flops 1006632960 | bytes 5242880 | tf_op jit(solution)/shard_map/pallas_call | solution.py:100
  136.1 2.9 %shard_map.63.rest_0_ = bf16[256,2560]{1,0:T(8,128)(2,1)} custom-call(s32[1]{0:T(128)} %bitcast.valid_ref, bf16[272,1280]{1,0:T(8,128)(2,1)} %shard_map.62.a_ref, bf16[272,1280]{1,0:T(8,128)(2,1)} %copy-done.4), custom_call_target="tpu_custom_call" | custom-call | flops 1310720 | bytes 1966080 | tf_op jit(solution)/shard_map/pallas_call | solution.py:184
  139.8 2.9 %shard_map.64 = bf16[256,2560]{1,0:T(8,128)(2,1)} custom-call(s32[1]{0:T(128)} %bitcast.valid_ref, bf16[272,1280]{1,0:T(8,128)(2,1)} %shard_map.59.a_ref, bf16[272,1280]{1,0:T(8,128)(2,1)} %copy-done.7, bf16[256,2560]{1,0:T(8,128)(2,1)} %shard_map.63.rest_0_), custom_call_target="tpu_custom_call", output_to_operand_aliasing={{}: (3, {})} | custom-call | flops 1310720 | bytes 1966080 | tf_op jit(solution)/shard_map/pallas_call | solution.py:184
  (41 shorter events, 17.5 us)
Async XLA Ops:
  0.0 2.6 %copy-start.1 = (bf16[1,256,2560]{2,1,0:T(8,128)(2,1)S(1)}, bf16[1,256,2560]{2,1,0:T(8,128)(2,1)}, u32[]{:S(2)}) copy-start(bf16[1,256,2560]{2,1,0:T(8,128)(2,1)} %param.9) | copy-start | bytes 3932164
  2.6 7.4 %copy-start.9 = (s32[1,1,2]{2,1,0:T(1,128)S(1)}, s32[1,1,2]{2,1,0:T(1,128)}, u32[]{:S(2)}) copy-start(s32[1,1,2]{2,1,0:T(1,128)} %param.11) | copy-start | bytes 28
  2.6 7.5 %copy-start.2 = (bf16[1,256,2560]{2,1,0:T(8,128)(2,1)S(1)}, bf16[1,256,2560]{2,1,0:T(8,128)(2,1)}, u32[]{:S(2)}) copy-start(bf16[1,256,2560]{2,1,0:T(8,128)(2,1)} %param.7) | copy-start | bytes 3932164
  3.8 35.6 %collective-permute-start.2 = (bf16[2,256,2560]{2,1,0:T(8,128)(2,1)}, bf16[2,256,2560]{2,1,0:T(8,128)(2,1)S(1)}, u32[]{:S(2)}, u32[]{:S(2)}) collective-permute-start(bf16[2,256,2560]{2,1,0:T(8,128)(2,1)} %constant_dynamic-update-slice_fusion), channel_id=1, source_target_pairs={{0,1},{1,2},{2,3},{3,4},{4,5},{5,6},{6,7},{8,9},{9,10},{10,11},{11... | collective-permute-start | bytes 7864328 | tf_op jit(solution)/shard_map/ppermute | solution.py:238
  5.7 33.7 %collective-permute-start.3 = (bf16[2,256,2560]{2,1,0:T(8,128)(2,1)}, bf16[2,256,2560]{2,1,0:T(8,128)(2,1)}, u32[]{:S(2)}, u32[]{:S(2)}) collective-permute-start(bf16[2,256,2560]{2,1,0:T(8,128)(2,1)} %constant_dynamic-update-slice_fusion), channel_id=1, source_target_pairs={{1,0},{2,1},{3,2},{4,3},{5,4},{6,5},{7,6},{9,8},{10,9},{11,10},{12... | collective-permute-start | bytes 7864328 | tf_op jit(solution)/shard_map/ppermute | solution.py:239
  11.1 22.5 %collective-permute-start.1 = (bf16[272,1280]{1,0:T(8,128)(2,1)S(1)}, bf16[272,1280]{1,0:T(8,128)(2,1)}, u32[]{:S(2)}, u32[]{:S(2)}) collective-permute-start(bf16[272,1280]{1,0:T(8,128)(2,1)S(1)} %pad_maximum_fusion), channel_id=1, source_target_pairs={{8,0},{16,8},{24,16},{32,24},{40,32},{48,40},{56,48},{64,56},{72,6... | collective-permute-start | bytes 2088968 | tf_op jit(solution)/shard_map/ppermute | solution.py:205
  13.8 33.8 %collective-permute-start = (bf16[256,1280]{1,0:T(8,128)(2,1)}, bf16[256,1280]{1,0:T(8,128)(2,1)}, u32[]{:S(2)}, u32[]{:S(2)}) collective-permute-start(bf16[256,1280]{1,0:T(8,128)(2,1)} %get-tuple-element.28), channel_id=1, source_target_pairs={{8,0},{16,8},{24,16},{32,24},{40,32},{48,40},{56,48},{64,56},{72,6... | collective-permute-start | bytes 1966088 | tf_op jit(solution)/shard_map/ppermute | solution.py:205
  33.6 28.3 %collective-permute-start.4 = (bf16[272,1280]{1,0:T(8,128)(2,1)}, bf16[272,1280]{1,0:T(8,128)(2,1)S(1)}, u32[]{:S(2)}, u32[]{:S(2)}) collective-permute-start(bf16[272,1280]{1,0:T(8,128)(2,1)} %collective-permute-done.1.q_ref), channel_id=1, source_target_pairs={{8,0},{16,8},{24,16},{32,24},{40,32},{48,40},{56,48},{64,56},{72,6... | collective-permute-start | bytes 2088968 | tf_op jit(solution)/shard_map/ppermute | solution.py:205
  39.4 1.6 %copy-start = (bf16[2,256,2560]{2,1,0:T(8,128)(2,1)}, bf16[2,256,2560]{2,1,0:T(8,128)(2,1)S(1)}, u32[]{:S(2)}) copy-start(bf16[2,256,2560]{2,1,0:T(8,128)(2,1)S(1)} %collective-permute-done.2.kl_ref.vl_ref) | copy-start | bytes 7864324
  51.4 24.5 %collective-permute-start.5 = (bf16[256,1280]{1,0:T(8,128)(2,1)}, bf16[256,1280]{1,0:T(8,128)(2,1)S(1)}, u32[]{:S(2)}, u32[]{:S(2)}) collective-permute-start(bf16[256,1280]{1,0:T(8,128)(2,1)} %collective-permute-done.q_ref), channel_id=1, source_target_pairs={{8,0},{16,8},{24,16},{32,24},{40,32},{48,40},{56,48},{64,56},{72,6... | collective-permute-start | bytes 1966088 | tf_op jit(solution)/shard_map/ppermute | solution.py:205
  61.9 3.4 %copy-start.3 = (bf16[272,1280]{1,0:T(8,128)(2,1)}, bf16[272,1280]{1,0:T(8,128)(2,1)S(1)}, u32[]{:S(2)}) copy-start(bf16[272,1280]{1,0:T(8,128)(2,1)S(1)} %collective-permute-done.4.q_ref) | copy-start | bytes 2088964
  72.9 20.6 %collective-permute-start.8 = (bf16[272,1280]{1,0:T(8,128)(2,1)}, bf16[272,1280]{1,0:T(8,128)(2,1)S(1)}, u32[]{:S(2)}, u32[]{:S(2)}) collective-permute-start(bf16[272,1280]{1,0:T(8,128)(2,1)} %shard_map.60), channel_id=1, source_target_pairs={{0,8},{8,16},{16,24},{24,32},{32,40},{40,48},{48,56},{56,64},{64,7... | collective-permute-start | bytes 2088968 | tf_op jit(solution)/shard_map/ppermute | solution.py:205
  75.9 0.9 copy-start.8
  84.3 24.1 %collective-permute-start.6 = (bf16[272,1280]{1,0:T(8,128)(2,1)}, bf16[272,1280]{1,0:T(8,128)(2,1)S(1)}, u32[]{:S(2)}, u32[]{:S(2)}) collective-permute-start(bf16[272,1280]{1,0:T(8,128)(2,1)} %shard_map.57), channel_id=1, source_target_pairs={{0,8},{8,16},{16,24},{24,32},{32,40},{40,48},{48,56},{56,64},{64,7... | collective-permute-start | bytes 2088968 | tf_op jit(solution)/shard_map/ppermute | solution.py:205
  93.5 0.9 copy-start.5
  97.3 37.9 %collective-permute-start.9 = (bf16[272,1280]{1,0:T(8,128)(2,1)}, bf16[272,1280]{1,0:T(8,128)(2,1)S(1)}, u32[]{:S(2)}, u32[]{:S(2)}) collective-permute-start(bf16[272,1280]{1,0:T(8,128)(2,1)} %shard_map.61), channel_id=1, source_target_pairs={{0,8},{8,16},{16,24},{24,32},{32,40},{40,48},{48,56},{56,64},{64,7... | collective-permute-start | bytes 2088968 | tf_op jit(solution)/shard_map/ppermute | solution.py:205
  108.4 0.9 copy-start.6
  112.2 26.8 %collective-permute-start.7 = (bf16[272,1280]{1,0:T(8,128)(2,1)}, bf16[272,1280]{1,0:T(8,128)(2,1)S(1)}, u32[]{:S(2)}, u32[]{:S(2)}) collective-permute-start(bf16[272,1280]{1,0:T(8,128)(2,1)} %shard_map.58), channel_id=1, source_target_pairs={{0,8},{8,16},{16,24},{24,32},{32,40},{40,48},{48,56},{56,64},{64,7... | collective-permute-start | bytes 2088968 | tf_op jit(solution)/shard_map/ppermute | solution.py:205
  135.2 0.9 copy-start.4
  139.0 0.9 copy-start.7

commit v12 on v10

--- a/solution.py
+++ b/solution.py
@@ -244,12 +244,13 @@
         p1s.append(attend(f1, q1s[c], k, v, kv_l, kv_r, chunk_w, c * groups_c, 0))
         relay = q1s[c]
         if c > 0:
-            relay, p1s[0], p1s[c] = lax.optimization_barrier((relay, p1s[0], p1s[c]))
+            relay, p1s[0] = lax.optimization_barrier((relay, p1s[0]))
         q2s.append(shift_tm(relay, -1))
 
     valid = (seg >= 1).astype(jnp.int32).reshape(1)
     f0 = flags_for(meta, 0)
     f2 = flags_for(q2s[0][rows, 0:3], 2)
+    q2s[0], p1s[1] = lax.optimization_barrier((q2s[0], p1s[1]))
     p2s = [attend(f2, q2s[c], k, v, kv_l, kv_r, chunk_w, c * groups_c, 0) for c in range(CHUNKS)]
     p2_ins = [shift_tm(p2, 1) for p2 in p2s]
     result = None

time: 142 us -> 160 us (1.13)
  the two profiles are of different devices: /device:TPU:72 before, /device:TPU:56 now
where the time goes in v12:
time: 160 us; the launch traced here: 159 us
  Pallas kernels  57.1 us (36%)
  waiting for transfers between devices  48.3 us (30%)
  starting transfers between devices  32.3 us (20%)
  local copies, waits for them, and re-layouts  12.6 us (8%)
  between operations  6.46 us (4%)
  other arithmetic  2.72 us (2%)
    ppermute x8, waiting for transfers between devices, shift_tm(): return lax.ppermute(x, 'tm', pairs)  48.3 us
    pallas_call x6, Pallas kernels, attend(): pl.pallas_call(_attn_kernel, out_shape=jax.ShapeDtypeStruct((rows + EXTRA...  45.5 us
    ppermute x8, starting transfers between devices, shift_tm(): return lax.ppermute(x, 'tm', pairs)  26.7 us
    pallas_call x4, Pallas kernels, merge(): pl.pallas_call(kernel, out_shape=out_shape, grid_spec=pltpu.PrefetchScala...  11.7 us
    unnamed x21, local copies, waits for them, and re-layouts  8.5 us
    ppermute x1, starting transfers between devices, on_device(): kv_r = lax.ppermute(kv, 'space', [(i + 1, i) for i in range(tiles - 1)])  3.64 us
  transfers between devices with their start and end apart: 10, of which 6 were waited for; matrix products, arithmetic and copies ran while one was open for 4% of the time, Pallas kernels for 34%

profile of v12, /device:TPU:56, one launch (start us, length us, event | category | flops | bytes accessed | tf_op | source)
XLA Modules:
  0.0 159.4 jit_solution(6928562795934238901)
XLA Ops:
  0.0 2.6 %constant_dynamic-update-slice_fusion.1 = bf16[2,256,2560]{2,1,0:T(8,128)(2,1)} fusion(bf16[1,256,2560]{2,1,0:T(8,128)(2,1)} %param.8), kind=kLoop, calls=%fused_computation.10 | loop fusion | bytes 2621440
  3.8 1.9 %collective-permute-start.3 = (bf16[2,256,2560]{2,1,0:T(8,128)(2,1)}, bf16[2,256,2560]{2,1,0:T(8,128)(2,1)S(1)}, u32[]{:S(2)}, u32[]{:S(2)}) collective-permute-start(bf16[2,256,2560]{2,1,0:T(8,128)(2,1)} %constant_dynamic-update-slice_fusion), channel_id=1, source_target_pairs={{0,1},{1,2},{2,3},{3,4},{4,5},{5,6},{6,7},{8,9},{9,10},{10,11},{11... | collective-permute-start | bytes 7864328 | tf_op jit(solution)/shard_map/ppermute | solution.py:238
  5.7 3.6 %collective-permute-start.4 = (bf16[2,256,2560]{2,1,0:T(8,128)(2,1)}, bf16[2,256,2560]{2,1,0:T(8,128)(2,1)}, u32[]{:S(2)}, u32[]{:S(2)}) collective-permute-start(bf16[2,256,2560]{2,1,0:T(8,128)(2,1)} %constant_dynamic-update-slice_fusion), channel_id=1, source_target_pairs={{1,0},{2,1},{3,2},{4,3},{5,4},{6,5},{7,6},{9,8},{10,9},{11,10},{12... | collective-permute-start | bytes 7864328 | tf_op jit(solution)/shard_map/ppermute | solution.py:239
  11.1 4.2 %collective-permute-start = (bf16[272,1280]{1,0:T(8,128)(2,1)S(1)}, bf16[272,1280]{1,0:T(8,128)(2,1)}, u32[]{:S(2)}, u32[]{:S(2)}) collective-permute-start(bf16[272,1280]{1,0:T(8,128)(2,1)S(1)} %pad_maximum_fusion), channel_id=1, source_target_pairs={{8,0},{16,8},{24,16},{32,24},{40,32},{48,40},{56,48},{64,56},{72,6... | collective-permute-start | bytes 2088968 | tf_op jit(solution)/shard_map/ppermute | solution.py:205
  15.3 15.6 %collective-permute-done.q_ref = bf16[272,1280]{1,0:T(8,128)(2,1)} collective-permute-done((bf16[272,1280]{1,0:T(8,128)(2,1)S(1)}, bf16[272,1280]{1,0:T(8,128)(2,1)}, u32[]{:S(2)}, u32[]{:S(2)}) %collective-permute-start) | collective-permute-done | bytes 696352 | tf_op jit(solution)/shard_map/ppermute | solution.py:205
  30.9 6.3 %collective-permute-start.1 = (bf16[272,1280]{1,0:T(8,128)(2,1)}, bf16[272,1280]{1,0:T(8,128)(2,1)S(1)}, u32[]{:S(2)}, u32[]{:S(2)}) collective-permute-start(bf16[272,1280]{1,0:T(8,128)(2,1)} %collective-permute-done.q_ref), channel_id=1, source_target_pairs={{8,0},{16,8},{24,16},{32,24},{40,32},{48,40},{56,48},{64,56},{72,6... | collective-permute-start | bytes 2088968 | tf_op jit(solution)/shard_map/ppermute | solution.py:205
  37.2 1.9 %collective-permute-start.2 = (bf16[256,1280]{1,0:T(8,128)(2,1)}, bf16[256,1280]{1,0:T(8,128)(2,1)}, u32[]{:S(2)}, u32[]{:S(2)}) collective-permute-start(bf16[256,1280]{1,0:T(8,128)(2,1)} %get-tuple-element.33), channel_id=1, source_target_pairs={{8,0},{16,8},{24,16},{32,24},{40,32},{48,40},{56,48},{64,56},{72,6... | collective-permute-start | bytes 1966088 | tf_op jit(solution)/shard_map/ppermute | solution.py:205
  44.3 7.6 %shard_map.56.a_ref = bf16[272,1280]{1,0:T(8,128)(2,1)} custom-call(s32[3]{0:T(128)} %add_convert_fusion.1.flags_ref, bf16[272,1280]{1,0:T(8,128)(2,1)} %collective-permute-done.q_ref, bf16[2,256,2560]{2,1,0:T(8,128)(2,1)} %copy-done, bf16[256,2560]{1,0:T(8,128)(2,1)} %bitcast.24, bf16[2,256,2560]{2,1,0:T(8,128)(2,1)} %collective-permute-done.4.kr_ref.vr_ref, ...), custom_call_target="tpu_custom_call" | custom-call | flops 1006632960 | bytes 5242880 | tf_op jit(solution)/shard_map/pallas_call | solution.py:100
  51.9 14.1 %collective-permute-done.2.q_ref = bf16[256,1280]{1,0:T(8,128)(2,1)} collective-permute-done((bf16[256,1280]{1,0:T(8,128)(2,1)}, bf16[256,1280]{1,0:T(8,128)(2,1)}, u32[]{:S(2)}, u32[]{:S(2)}) %collective-permute-start.2) | collective-permute-done | bytes 655392 | tf_op jit(solution)/shard_map/ppermute | solution.py:205
  66.0 6.5 %collective-permute-start.5 = (bf16[256,1280]{1,0:T(8,128)(2,1)}, bf16[256,1280]{1,0:T(8,128)(2,1)S(1)}, u32[]{:S(2)}, u32[]{:S(2)}) collective-permute-start(bf16[256,1280]{1,0:T(8,128)(2,1)} %collective-permute-done.2.q_ref), channel_id=1, source_target_pairs={{8,0},{16,8},{24,16},{32,24},{40,32},{48,40},{56,48},{64,56},{72,6... | collective-permute-start | bytes 1966088 | tf_op jit(solution)/shard_map/ppermute | solution.py:205
  75.8 7.6 %shard_map.55.a_ref = bf16[272,1280]{1,0:T(8,128)(2,1)} custom-call(s32[3]{0:T(128)} %add_convert_fusion.1.flags_ref, bf16[256,1280]{1,0:T(8,128)(2,1)} %collective-permute-done.2.q_ref, bf16[2,256,2560]{2,1,0:T(8,128)(2,1)} %copy-done, bf16[256,2560]{1,0:T(8,128)(2,1)} %bitcast.25, bf16[2,256,2560]{2,1,0:T(8,128)(2,1)} %collective-permute-done.4.kr_ref.vr_ref, ...), custom_call_target="tpu_custom_call" | custom-call | flops 1006632960 | bytes 5242880 | tf_op jit(solution)/shard_map/pallas_call | solution.py:100
  83.4 7.6 %shard_map.58 = bf16[272,1280]{1,0:T(8,128)(2,1)} custom-call(s32[3]{0:T(128)} %add_convert_fusion.2.flags_ref, bf16[272,1280]{1,0:T(8,128)(2,1)} %copy-done.3, bf16[2,256,2560]{2,1,0:T(8,128)(2,1)} %copy-done, bf16[256,2560]{1,0:T(8,128)(2,1)} %bitcast.26, bf16[2,256,2560]{2,1,0:T(8,128)(2,1)} %collective-permute-done.4.kr_ref.vr_ref, ...), custom_call_target="tpu_custom_call" | custom-call | flops 1006632960 | bytes 5242880 | tf_op jit(solution)/shard_map/pallas_call | solution.py:100
  90.9 1.9 %collective-permute-start.7 = (bf16[272,1280]{1,0:T(8,128)(2,1)}, bf16[272,1280]{1,0:T(8,128)(2,1)S(1)}, u32[]{:S(2)}, u32[]{:S(2)}) collective-permute-start(bf16[272,1280]{1,0:T(8,128)(2,1)} %shard_map.58), channel_id=1, source_target_pairs={{0,8},{8,16},{16,24},{24,32},{32,40},{40,48},{48,56},{56,64},{64,7... | collective-permute-start | bytes 2088968 | tf_op jit(solution)/shard_map/ppermute | solution.py:205
  93.7 7.6 %shard_map.57 = bf16[272,1280]{1,0:T(8,128)(2,1)} custom-call(s32[3]{0:T(128)} %add_convert_fusion.2.flags_ref, bf16[256,1280]{1,0:T(8,128)(2,1)} %copy-done.8, bf16[2,256,2560]{2,1,0:T(8,128)(2,1)} %copy-done, bf16[256,2560]{1,0:T(8,128)(2,1)} %bitcast.27, bf16[2,256,2560]{2,1,0:T(8,128)(2,1)} %collective-permute-done.4.kr_ref.vr_ref, ...), custom_call_target="tpu_custom_call" | custom-call | flops 1006632960 | bytes 5242880 | tf_op jit(solution)/shard_map/pallas_call | solution.py:100
  101.3 1.9 %collective-permute-start.6 = (bf16[272,1280]{1,0:T(8,128)(2,1)}, bf16[272,1280]{1,0:T(8,128)(2,1)S(1)}, u32[]{:S(2)}, u32[]{:S(2)}) collective-permute-start(bf16[272,1280]{1,0:T(8,128)(2,1)} %shard_map.57), channel_id=1, source_target_pairs={{0,8},{8,16},{16,24},{24,32},{32,40},{40,48},{48,56},{56,64},{64,7... | collective-permute-start | bytes 2088968 | tf_op jit(solution)/shard_map/ppermute | solution.py:205
  106.6 7.1 %collective-permute-done.7.b_ref = bf16[272,1280]{1,0:T(8,128)(2,1)S(1)} collective-permute-done((bf16[272,1280]{1,0:T(8,128)(2,1)}, bf16[272,1280]{1,0:T(8,128)(2,1)S(1)}, u32[]{:S(2)}, u32[]{:S(2)}) %collective-permute-start.7) | collective-permute-done | bytes 696352 | tf_op jit(solution)/shard_map/ppermute | solution.py:205
  114.6 2.9 %shard_map.59 = bf16[272,1280]{1,0:T(8,128)(2,1)} custom-call(s32[1]{0:T(128)} %bitcast.valid_ref, bf16[272,1280]{1,0:T(8,128)(2,1)} %shard_map.56.a_ref, bf16[272,1280]{1,0:T(8,128)(2,1)} %copy-done.6), custom_call_target="tpu_custom_call" | custom-call | flops 1310720 | bytes 1966080 | tf_op jit(solution)/shard_map/pallas_call | solution.py:184
  117.5 2.1 %collective-permute-start.9 = (bf16[272,1280]{1,0:T(8,128)(2,1)}, bf16[272,1280]{1,0:T(8,128)(2,1)S(1)}, u32[]{:S(2)}, u32[]{:S(2)}) collective-permute-start(bf16[272,1280]{1,0:T(8,128)(2,1)} %shard_map.59), channel_id=1, source_target_pairs={{0,8},{8,16},{16,24},{24,32},{32,40},{40,48},{48,56},{56,64},{64,7... | collective-permute-start | bytes 2088968 | tf_op jit(solution)/shard_map/ppermute | solution.py:205
  119.6 7.6 %shard_map.60.a_ref = bf16[272,1280]{1,0:T(8,128)(2,1)} custom-call(s32[3]{0:T(128)} %add_convert_fusion.flags_ref, bf16[256,2560]{1,0:T(8,128)(2,1)} %bitcast.36, bf16[2,256,2560]{2,1,0:T(8,128)(2,1)} %copy-done, bf16[256,2560]{1,0:T(8,128)(2,1)} %bitcast.28, bf16[2,256,2560]{2,1,0:T(8,128)(2,1)} %collective-permute-done.4.kr_ref.vr_ref, ...), custom_call_target="tpu_custom_call" | custom-call | flops 1006632960 | bytes 5242880 | tf_op jit(solution)/shard_map/pallas_call | solution.py:100
  129.4 2.9 %shard_map.61 = bf16[272,1280]{1,0:T(8,128)(2,1)} custom-call(s32[1]{0:T(128)} %bitcast.valid_ref, bf16[272,1280]{1,0:T(8,128)(2,1)} %shard_map.55.a_ref, bf16[272,1280]{1,0:T(8,128)(2,1)} %copy-done.5), custom_call_target="tpu_custom_call" | custom-call | flops 1310720 | bytes 1966080 | tf_op jit(solution)/shard_map/pallas_call | solution.py:184
  134.3 7.6 %shard_map.62.a_ref = bf16[272,1280]{1,0:T(8,128)(2,1)} custom-call(s32[3]{0:T(128)} %add_convert_fusion.flags_ref, bf16[256,2560]{1,0:T(8,128)(2,1)} %bitcast.37, bf16[2,256,2560]{2,1,0:T(8,128)(2,1)} %copy-done, bf16[256,2560]{1,0:T(8,128)(2,1)} %bitcast.29, bf16[2,256,2560]{2,1,0:T(8,128)(2,1)} %collective-permute-done.4.kr_ref.vr_ref, ...), custom_call_target="tpu_custom_call" | custom-call | flops 1006632960 | bytes 5242880 | tf_op jit(solution)/shard_map/pallas_call | solution.py:100
  144.4 2.9 %shard_map.63.rest_0_ = bf16[256,2560]{1,0:T(8,128)(2,1)} custom-call(s32[1]{0:T(128)} %bitcast.valid_ref, bf16[272,1280]{1,0:T(8,128)(2,1)} %shard_map.60.a_ref, bf16[272,1280]{1,0:T(8,128)(2,1)} %copy-done.4), custom_call_target="tpu_custom_call" | custom-call | flops 1310720 | bytes 1966080 | tf_op jit(solution)/shard_map/pallas_call | solution.py:184
  147.3 8.4 %collective-permute-done.8.b_ref = bf16[272,1280]{1,0:T(8,128)(2,1)S(1)} collective-permute-done((bf16[272,1280]{1,0:T(8,128)(2,1)}, bf16[272,1280]{1,0:T(8,128)(2,1)S(1)}, u32[]{:S(2)}, u32[]{:S(2)}) %collective-permute-start.8) | collective-permute-done | bytes 696352 | tf_op jit(solution)/shard_map/ppermute | solution.py:205
  156.5 2.9 %shard_map.64 = bf16[256,2560]{1,0:T(8,128)(2,1)} custom-call(s32[1]{0:T(128)} %bitcast.valid_ref, bf16[272,1280]{1,0:T(8,128)(2,1)} %shard_map.62.a_ref, bf16[272,1280]{1,0:T(8,128)(2,1)} %copy-done.7, bf16[256,2560]{1,0:T(8,128)(2,1)} %shard_map.63.rest_0_), custom_call_target="tpu_custom_call", output_to_operand_aliasing={{}: (3, {})} | custom-call | flops 1310720 | bytes 1966080 | tf_op jit(solution)/shard_map/pallas_call | solution.py:184
  (41 shorter events, 17.6 us)
Async XLA Ops:
  0.0 2.6 %copy-start.1 = (bf16[1,256,2560]{2,1,0:T(8,128)(2,1)S(1)}, bf16[1,256,2560]{2,1,0:T(8,128)(2,1)}, u32[]{:S(2)}) copy-start(bf16[1,256,2560]{2,1,0:T(8,128)(2,1)} %param.9) | copy-start | bytes 3932164
  2.6 7.4 %copy-start.9 = (s32[1,1,2]{2,1,0:T(1,128)S(1)}, s32[1,1,2]{2,1,0:T(1,128)}, u32[]{:S(2)}) copy-start(s32[1,1,2]{2,1,0:T(1,128)} %param.11) | copy-start | bytes 28
  2.6 7.5 %copy-start.2 = (bf16[1,256,2560]{2,1,0:T(8,128)(2,1)S(1)}, bf16[1,256,2560]{2,1,0:T(8,128)(2,1)}, u32[]{:S(2)}) copy-start(bf16[1,256,2560]{2,1,0:T(8,128)(2,1)} %param.7) | copy-start | bytes 3932164
  3.8 39.0 %collective-permute-start.3 = (bf16[2,256,2560]{2,1,0:T(8,128)(2,1)}, bf16[2,256,2560]{2,1,0:T(8,128)(2,1)S(1)}, u32[]{:S(2)}, u32[]{:S(2)}) collective-permute-start(bf16[2,256,2560]{2,1,0:T(8,128)(2,1)} %constant_dynamic-update-slice_fusion), channel_id=1, source_target_pairs={{0,1},{1,2},{2,3},{3,4},{4,5},{5,6},{6,7},{8,9},{9,10},{10,11},{11... | collective-permute-start | bytes 7864328 | tf_op jit(solution)/shard_map/ppermute | solution.py:238
  5.7 37.1 %collective-permute-start.4 = (bf16[2,256,2560]{2,1,0:T(8,128)(2,1)}, bf16[2,256,2560]{2,1,0:T(8,128)(2,1)}, u32[]{:S(2)}, u32[]{:S(2)}) collective-permute-start(bf16[2,256,2560]{2,1,0:T(8,128)(2,1)} %constant_dynamic-update-slice_fusion), channel_id=1, source_target_pairs={{1,0},{2,1},{3,2},{4,3},{5,4},{6,5},{7,6},{9,8},{10,9},{11,10},{12... | collective-permute-start | bytes 7864328 | tf_op jit(solution)/shard_map/ppermute | solution.py:239
  11.1 19.8 %collective-permute-start = (bf16[272,1280]{1,0:T(8,128)(2,1)S(1)}, bf16[272,1280]{1,0:T(8,128)(2,1)}, u32[]{:S(2)}, u32[]{:S(2)}) collective-permute-start(bf16[272,1280]{1,0:T(8,128)(2,1)S(1)} %pad_maximum_fusion), channel_id=1, source_target_pairs={{8,0},{16,8},{24,16},{32,24},{40,32},{48,40},{56,48},{64,56},{72,6... | collective-permute-start | bytes 2088968 | tf_op jit(solution)/shard_map/ppermute | solution.py:205
  30.9 41.7 %collective-permute-start.1 = (bf16[272,1280]{1,0:T(8,128)(2,1)}, bf16[272,1280]{1,0:T(8,128)(2,1)S(1)}, u32[]{:S(2)}, u32[]{:S(2)}) collective-permute-start(bf16[272,1280]{1,0:T(8,128)(2,1)} %collective-permute-done.q_ref), channel_id=1, source_target_pairs={{8,0},{16,8},{24,16},{32,24},{40,32},{48,40},{56,48},{64,56},{72,6... | collective-permute-start | bytes 2088968 | tf_op jit(solution)/shard_map/ppermute | solution.py:205
  37.2 28.8 %collective-permute-start.2 = (bf16[256,1280]{1,0:T(8,128)(2,1)}, bf16[256,1280]{1,0:T(8,128)(2,1)}, u32[]{:S(2)}, u32[]{:S(2)}) collective-permute-start(bf16[256,1280]{1,0:T(8,128)(2,1)} %get-tuple-element.33), channel_id=1, source_target_pairs={{8,0},{16,8},{24,16},{32,24},{40,32},{48,40},{56,48},{64,56},{72,6... | collective-permute-start | bytes 1966088 | tf_op jit(solution)/shard_map/ppermute | solution.py:205
  42.8 1.6 copy-start
  66.0 26.8 %collective-permute-start.5 = (bf16[256,1280]{1,0:T(8,128)(2,1)}, bf16[256,1280]{1,0:T(8,128)(2,1)S(1)}, u32[]{:S(2)}, u32[]{:S(2)}) collective-permute-start(bf16[256,1280]{1,0:T(8,128)(2,1)} %collective-permute-done.2.q_ref), channel_id=1, source_target_pairs={{8,0},{16,8},{24,16},{32,24},{40,32},{48,40},{56,48},{64,56},{72,6... | collective-permute-start | bytes 1966088 | tf_op jit(solution)/shard_map/ppermute | solution.py:205
  72.5 10.8 %copy-start.3 = (bf16[272,1280]{1,0:T(8,128)(2,1)}, bf16[272,1280]{1,0:T(8,128)(2,1)S(1)}, u32[]{:S(2)}) copy-start(bf16[272,1280]{1,0:T(8,128)(2,1)S(1)} %collective-permute-done.1.q_ref) | copy-start | bytes 2088964
  90.9 22.7 %collective-permute-start.7 = (bf16[272,1280]{1,0:T(8,128)(2,1)}, bf16[272,1280]{1,0:T(8,128)(2,1)S(1)}, u32[]{:S(2)}, u32[]{:S(2)}) collective-permute-start(bf16[272,1280]{1,0:T(8,128)(2,1)} %shard_map.58), channel_id=1, source_target_pairs={{0,8},{8,16},{16,24},{24,32},{32,40},{40,48},{48,56},{56,64},{64,7... | collective-permute-start | bytes 2088968 | tf_op jit(solution)/shard_map/ppermute | solution.py:205
  92.8 0.9 copy-start.8
  101.3 27.3 %collective-permute-start.6 = (bf16[272,1280]{1,0:T(8,128)(2,1)}, bf16[272,1280]{1,0:T(8,128)(2,1)S(1)}, u32[]{:S(2)}, u32[]{:S(2)}) collective-permute-start(bf16[272,1280]{1,0:T(8,128)(2,1)} %shard_map.57), channel_id=1, source_target_pairs={{0,8},{8,16},{16,24},{24,32},{32,40},{40,48},{48,56},{56,64},{64,7... | collective-permute-start | bytes 2088968 | tf_op jit(solution)/shard_map/ppermute | solution.py:205
  113.7 0.9 copy-start.6
  117.5 26.0 %collective-permute-start.9 = (bf16[272,1280]{1,0:T(8,128)(2,1)}, bf16[272,1280]{1,0:T(8,128)(2,1)S(1)}, u32[]{:S(2)}, u32[]{:S(2)}) collective-permute-start(bf16[272,1280]{1,0:T(8,128)(2,1)} %shard_map.59), channel_id=1, source_target_pairs={{0,8},{8,16},{16,24},{24,32},{32,40},{40,48},{48,56},{56,64},{64,7... | collective-permute-start | bytes 2088968 | tf_op jit(solution)/shard_map/ppermute | solution.py:205
  128.6 0.9 copy-start.5
  132.4 23.3 %collective-permute-start.8 = (bf16[272,1280]{1,0:T(8,128)(2,1)}, bf16[272,1280]{1,0:T(8,128)(2,1)S(1)}, u32[]{:S(2)}, u32[]{:S(2)}) collective-permute-start(bf16[272,1280]{1,0:T(8,128)(2,1)} %shard_map.61), channel_id=1, source_target_pairs={{0,8},{8,16},{16,24},{24,32},{32,40},{40,48},{48,56},{56,64},{64,7... | collective-permute-start | bytes 2088968 | tf_op jit(solution)/shard_map/ppermute | solution.py:205
  143.5 0.9 copy-start.4
  155.7 0.9 copy-start.7

commit v13 on v10

--- a/solution.py
+++ b/solution.py
@@ -199,6 +199,25 @@
     )(*operands)
 
 
+def _stack_kernel(k_ref, v_ref, o_ref):
+    o_ref[0] = k_ref[...]
+    o_ref[1] = v_ref[...]
+
+
+def stack_kv(k, v):
+    rows, width = k.shape
+    lanes = width // 2
+    spec = pl.BlockSpec((rows, lanes), lambda g: (0, g))
+    return pl.pallas_call(
+        _stack_kernel,
+        out_shape=jax.ShapeDtypeStruct((2, rows, width), k.dtype),
+        grid=(2,),
+        in_specs=[spec, spec],
+        out_specs=pl.BlockSpec((2, rows, lanes), lambda g: (0, 0, g)),
+        cost_estimate=pl.CostEstimate(flops=0, transcendentals=0, bytes_accessed=4 * rows * width * 2),
+    )(k, v)
+
+
 def shift_tm(x, by):
     size = lax.axis_size("tm")
     pairs = [(i, i + by) for i in range(size) if 0 <= i + by < size]
@@ -234,7 +253,7 @@
     sends += [q[:, c * chunk_w : (c + 1) * chunk_w] for c in range(1, CHUNKS)]
     q1s = [shift_tm(x, -1) for x in sends]
 
-    kv = jnp.stack([k, v])
+    kv = stack_kv(k, v)
     kv_l = lax.ppermute(kv, "space", [(i, i + 1) for i in range(tiles - 1)])
     kv_r = lax.ppermute(kv, "space", [(i + 1, i) for i in range(tiles - 1)])
 

time: 142 us -> 142 us (level)
  the two profiles are of different devices: /device:TPU:72 before, /device:TPU:112 now
where the time goes in v13:
time: 142 us; the launch traced here: 140 us
  Pallas kernels  52.4 us (37%)
  waiting for transfers between devices  37.4 us (26%)
  starting transfers between devices  31.3 us (22%)
  local copies, waits for them, and re-layouts  10.1 us (7%)
  between operations  6.54 us (5%)
  other arithmetic  2.6 us (2%)
    pallas_call x6, Pallas kernels, attend(): pl.pallas_call(_attn_kernel, out_shape=jax.ShapeDtypeStruct((rows + EXTRA...  37.9 us
    ppermute x8, waiting for transfers between devices, shift_tm(): return lax.ppermute(x, 'tm', pairs)  37.4 us
    ppermute x8, starting transfers between devices, shift_tm(): return lax.ppermute(x, 'tm', pairs)  25.7 us
    pallas_call x4, Pallas kernels, merge(): pl.pallas_call(kernel, out_shape=out_shape, grid_spec=pltpu.PrefetchScala...  11.7 us
    unnamed x16, local copies, waits for them, and re-layouts  5.86 us
    ppermute x1, starting transfers between devices, on_device(): kv_r = lax.ppermute(kv, 'space', [(i + 1, i) for i in range(tiles - 1)])  3.64 us
    pallas_call x1, Pallas kernels, stack_kv(): pl.pallas_call(_stack_kernel, out_shape=jax.ShapeDtypeStruct((2, rows, wi...  2.91 us
  transfers between devices with their start and end apart: 10, of which 6 were waited for; matrix products, arithmetic and copies ran while one was open for 5% of the time, Pallas kernels for 33%

profile of v13, /device:TPU:112, one launch (start us, length us, event | category | flops | bytes accessed | tf_op | source)
XLA Modules:
  0.0 140.3 jit_solution(12019536865280841328)
XLA Ops:
  0.0 2.9 %shard_map.55 = bf16[2,256,2560]{2,1,0:T(8,128)(2,1)} custom-call(bf16[256,2560]{1,0:T(8,128)(2,1)} %bitcast.24, bf16[256,2560]{1,0:T(8,128)(2,1)} %bitcast.31), custom_call_target="tpu_custom_call" | custom-call | bytes 5242880 | tf_op jit(solution)/shard_map/pallas_call | solution.py:211
  2.9 1.9 %collective-permute-start.2 = (bf16[2,256,2560]{2,1,0:T(8,128)(2,1)}, bf16[2,256,2560]{2,1,0:T(8,128)(2,1)S(1)}, u32[]{:S(2)}, u32[]{:S(2)}) collective-permute-start(bf16[2,256,2560]{2,1,0:T(8,128)(2,1)} %shard_map.55), channel_id=1, source_target_pairs={{0,1},{1,2},{2,3},{3,4},{4,5},{5,6},{6,7},{8,9},{9,10},{10,11},{11... | collective-permute-start | bytes 7864328 | tf_op jit(solution)/shard_map/ppermute | solution.py:257
  4.8 3.6 %collective-permute-start.3 = (bf16[2,256,2560]{2,1,0:T(8,128)(2,1)}, bf16[2,256,2560]{2,1,0:T(8,128)(2,1)}, u32[]{:S(2)}, u32[]{:S(2)}) collective-permute-start(bf16[2,256,2560]{2,1,0:T(8,128)(2,1)} %shard_map.55), channel_id=1, source_target_pairs={{1,0},{2,1},{3,2},{4,3},{5,4},{6,5},{7,6},{9,8},{10,9},{11,10},{12... | collective-permute-start | bytes 7864328 | tf_op jit(solution)/shard_map/ppermute | solution.py:258
  9.2 2.2 %fusion.6 = (bf16[256,1280]{1,0:T(8,128)(2,1)S(1)}, bf16[256,1280]{1,0:T(8,128)(2,1)}) fusion(bf16[256,2560]{1,0:T(8,128)(2,1)} %bitcast.38), kind=kLoop, calls=%fused_computation.17 | loop fusion | bytes 2621440 | tf_op jit(solution)/shard_map/slice | solution.py:252
  11.5 4.5 %collective-permute-start.1 = (bf16[272,1280]{1,0:T(8,128)(2,1)S(1)}, bf16[272,1280]{1,0:T(8,128)(2,1)}, u32[]{:S(2)}, u32[]{:S(2)}) collective-permute-start(bf16[272,1280]{1,0:T(8,128)(2,1)S(1)} %pad_maximum_fusion), channel_id=1, source_target_pairs={{8,0},{16,8},{24,16},{32,24},{40,32},{48,40},{56,48},{64,56},{72,6... | collective-permute-start | bytes 2088968 | tf_op jit(solution)/shard_map/ppermute | solution.py:224
  16.0 2.7 %collective-permute-start = (bf16[256,1280]{1,0:T(8,128)(2,1)}, bf16[256,1280]{1,0:T(8,128)(2,1)}, u32[]{:S(2)}, u32[]{:S(2)}) collective-permute-start(bf16[256,1280]{1,0:T(8,128)(2,1)} %get-tuple-element.32), channel_id=1, source_target_pairs={{8,0},{16,8},{24,16},{32,24},{40,32},{48,40},{56,48},{64,56},{72,6... | collective-permute-start | bytes 1966088 | tf_op jit(solution)/shard_map/ppermute | solution.py:224
  18.8 13.3 %collective-permute-done.1.q_ref = bf16[272,1280]{1,0:T(8,128)(2,1)} collective-permute-done((bf16[272,1280]{1,0:T(8,128)(2,1)S(1)}, bf16[272,1280]{1,0:T(8,128)(2,1)}, u32[]{:S(2)}, u32[]{:S(2)}) %collective-permute-start.1) | collective-permute-done | bytes 696352 | tf_op jit(solution)/shard_map/ppermute | solution.py:224
  32.0 6.6 %collective-permute-start.4 = (bf16[272,1280]{1,0:T(8,128)(2,1)}, bf16[272,1280]{1,0:T(8,128)(2,1)S(1)}, u32[]{:S(2)}, u32[]{:S(2)}) collective-permute-start(bf16[272,1280]{1,0:T(8,128)(2,1)} %collective-permute-done.1.q_ref), channel_id=1, source_target_pairs={{8,0},{16,8},{24,16},{32,24},{40,32},{48,40},{56,48},{64,56},{72,6... | collective-permute-start | bytes 2088968 | tf_op jit(solution)/shard_map/ppermute | solution.py:224
  43.9 7.6 %shard_map.56.a_ref = bf16[272,1280]{1,0:T(8,128)(2,1)} custom-call(s32[3]{0:T(128)} %add_convert_fusion.1.flags_ref, bf16[272,1280]{1,0:T(8,128)(2,1)} %collective-permute-done.1.q_ref, bf16[2,256,2560]{2,1,0:T(8,128)(2,1)} %copy-done, bf16[256,2560]{1,0:T(8,128)(2,1)} %bitcast.25, bf16[2,256,2560]{2,1,0:T(8,128)(2,1)} %collective-permute-done.3.kr_ref.vr_ref, ...), custom_call_target="tpu_custom_call" | custom-call | flops 1006632960 | bytes 5242880 | tf_op jit(solution)/shard_map/pallas_call | solution.py:100
  51.5 7.6 %shard_map.57.a_ref = bf16[272,1280]{1,0:T(8,128)(2,1)} custom-call(s32[3]{0:T(128)} %add_convert_fusion.1.flags_ref, bf16[256,1280]{1,0:T(8,128)(2,1)} %collective-permute-done.q_ref, bf16[2,256,2560]{2,1,0:T(8,128)(2,1)} %copy-done, bf16[256,2560]{1,0:T(8,128)(2,1)} %bitcast.26, bf16[2,256,2560]{2,1,0:T(8,128)(2,1)} %collective-permute-done.3.kr_ref.vr_ref, ...), custom_call_target="tpu_custom_call" | custom-call | flops 1006632960 | bytes 5242880 | tf_op jit(solution)/shard_map/pallas_call | solution.py:100
  64.3 3.8 %shard_map.59 = bf16[272,1280]{1,0:T(8,128)(2,1)} custom-call(s32[3]{0:T(128)} %add_convert_fusion.2.flags_ref, bf16[272,1280]{1,0:T(8,128)(2,1)} %copy-done.1, bf16[2,256,2560]{2,1,0:T(8,128)(2,1)} %copy-done, bf16[256,2560]{1,0:T(8,128)(2,1)} %bitcast.27, bf16[2,256,2560]{2,1,0:T(8,128)(2,1)} %collective-permute-done.3.kr_ref.vr_ref, ...), custom_call_target="tpu_custom_call" | custom-call | flops 1006632960 | bytes 5242880 | tf_op jit(solution)/shard_map/pallas_call | solution.py:100
  68.0 3.9 %collective-permute-start.7 = (bf16[272,1280]{1,0:T(8,128)(2,1)}, bf16[272,1280]{1,0:T(8,128)(2,1)S(1)}, u32[]{:S(2)}, u32[]{:S(2)}) collective-permute-start(bf16[272,1280]{1,0:T(8,128)(2,1)} %shard_map.59), channel_id=1, source_target_pairs={{0,8},{8,16},{16,24},{24,32},{32,40},{40,48},{48,56},{56,64},{64,7... | collective-permute-start | bytes 2088968 | tf_op jit(solution)/shard_map/ppermute | solution.py:224
  72.0 2.9 %collective-permute-done.5.q_ref = bf16[256,1280]{1,0:T(8,128)(2,1)S(1)} collective-permute-done((bf16[256,1280]{1,0:T(8,128)(2,1)}, bf16[256,1280]{1,0:T(8,128)(2,1)S(1)}, u32[]{:S(2)}, u32[]{:S(2)}) %collective-permute-start.5) | collective-permute-done | bytes 655392 | tf_op jit(solution)/shard_map/ppermute | solution.py:224
  75.8 3.7 %shard_map.58 = bf16[272,1280]{1,0:T(8,128)(2,1)} custom-call(s32[3]{0:T(128)} %add_convert_fusion.2.flags_ref, bf16[256,1280]{1,0:T(8,128)(2,1)} %copy-done.6, bf16[2,256,2560]{2,1,0:T(8,128)(2,1)} %copy-done, bf16[256,2560]{1,0:T(8,128)(2,1)} %bitcast.28, bf16[2,256,2560]{2,1,0:T(8,128)(2,1)} %collective-permute-done.3.kr_ref.vr_ref, ...), custom_call_target="tpu_custom_call" | custom-call | flops 1006632960 | bytes 5242880 | tf_op jit(solution)/shard_map/pallas_call | solution.py:100
  79.5 2.1 %collective-permute-start.6 = (bf16[272,1280]{1,0:T(8,128)(2,1)}, bf16[272,1280]{1,0:T(8,128)(2,1)S(1)}, u32[]{:S(2)}, u32[]{:S(2)}) collective-permute-start(bf16[272,1280]{1,0:T(8,128)(2,1)} %shard_map.58), channel_id=1, source_target_pairs={{0,8},{8,16},{16,24},{24,32},{32,40},{40,48},{48,56},{56,64},{64,7... | collective-permute-start | bytes 2088968 | tf_op jit(solution)/shard_map/ppermute | solution.py:224
  84.8 9.9 %collective-permute-done.7.b_ref = bf16[272,1280]{1,0:T(8,128)(2,1)S(1)} collective-permute-done((bf16[272,1280]{1,0:T(8,128)(2,1)}, bf16[272,1280]{1,0:T(8,128)(2,1)S(1)}, u32[]{:S(2)}, u32[]{:S(2)}) %collective-permute-start.7) | collective-permute-done | bytes 696352 | tf_op jit(solution)/shard_map/ppermute | solution.py:224
  95.6 2.9 %shard_map.60 = bf16[272,1280]{1,0:T(8,128)(2,1)} custom-call(s32[1]{0:T(128)} %bitcast.valid_ref, bf16[272,1280]{1,0:T(8,128)(2,1)} %shard_map.56.a_ref, bf16[272,1280]{1,0:T(8,128)(2,1)} %copy-done.4), custom_call_target="tpu_custom_call" | custom-call | flops 1310720 | bytes 1966080 | tf_op jit(solution)/shard_map/pallas_call | solution.py:184
  98.5 2.1 %collective-permute-start.9 = (bf16[272,1280]{1,0:T(8,128)(2,1)}, bf16[272,1280]{1,0:T(8,128)(2,1)S(1)}, u32[]{:S(2)}, u32[]{:S(2)}) collective-permute-start(bf16[272,1280]{1,0:T(8,128)(2,1)} %shard_map.60), channel_id=1, source_target_pairs={{0,8},{8,16},{16,24},{24,32},{32,40},{40,48},{48,56},{56,64},{64,7... | collective-permute-start | bytes 2088968 | tf_op jit(solution)/shard_map/ppermute | solution.py:224
  100.6 7.6 %shard_map.61.a_ref = bf16[272,1280]{1,0:T(8,128)(2,1)} custom-call(s32[3]{0:T(128)} %add_convert_fusion.flags_ref, bf16[256,2560]{1,0:T(8,128)(2,1)} %bitcast.39, bf16[2,256,2560]{2,1,0:T(8,128)(2,1)} %copy-done, bf16[256,2560]{1,0:T(8,128)(2,1)} %bitcast.29, bf16[2,256,2560]{2,1,0:T(8,128)(2,1)} %collective-permute-done.3.kr_ref.vr_ref, ...), custom_call_target="tpu_custom_call" | custom-call | flops 1006632960 | bytes 5242880 | tf_op jit(solution)/shard_map/pallas_call | solution.py:100
  110.5 2.9 %shard_map.62 = bf16[272,1280]{1,0:T(8,128)(2,1)} custom-call(s32[1]{0:T(128)} %bitcast.valid_ref, bf16[272,1280]{1,0:T(8,128)(2,1)} %shard_map.57.a_ref, bf16[272,1280]{1,0:T(8,128)(2,1)} %copy-done.3), custom_call_target="tpu_custom_call" | custom-call | flops 1310720 | bytes 1966080 | tf_op jit(solution)/shard_map/pallas_call | solution.py:184
  115.3 7.6 %shard_map.63.a_ref = bf16[272,1280]{1,0:T(8,128)(2,1)} custom-call(s32[3]{0:T(128)} %add_convert_fusion.flags_ref, bf16[256,2560]{1,0:T(8,128)(2,1)} %bitcast.40, bf16[2,256,2560]{2,1,0:T(8,128)(2,1)} %copy-done, bf16[256,2560]{1,0:T(8,128)(2,1)} %bitcast.30, bf16[2,256,2560]{2,1,0:T(8,128)(2,1)} %collective-permute-done.3.kr_ref.vr_ref, ...), custom_call_target="tpu_custom_call" | custom-call | flops 1006632960 | bytes 5242880 | tf_op jit(solution)/shard_map/pallas_call | solution.py:100
  125.4 2.9 %shard_map.64.rest_0_ = bf16[256,2560]{1,0:T(8,128)(2,1)} custom-call(s32[1]{0:T(128)} %bitcast.valid_ref, bf16[272,1280]{1,0:T(8,128)(2,1)} %shard_map.61.a_ref, bf16[272,1280]{1,0:T(8,128)(2,1)} %copy-done.2), custom_call_target="tpu_custom_call" | custom-call | flops 1310720 | bytes 1966080 | tf_op jit(solution)/shard_map/pallas_call | solution.py:184
  128.3 8.3 %collective-permute-done.8.b_ref = bf16[272,1280]{1,0:T(8,128)(2,1)S(1)} collective-permute-done((bf16[272,1280]{1,0:T(8,128)(2,1)}, bf16[272,1280]{1,0:T(8,128)(2,1)S(1)}, u32[]{:S(2)}, u32[]{:S(2)}) %collective-permute-start.8) | collective-permute-done | bytes 696352 | tf_op jit(solution)/shard_map/ppermute | solution.py:224
  137.4 2.9 %shard_map.65 = bf16[256,2560]{1,0:T(8,128)(2,1)} custom-call(s32[1]{0:T(128)} %bitcast.valid_ref, bf16[272,1280]{1,0:T(8,128)(2,1)} %shard_map.63.a_ref, bf16[272,1280]{1,0:T(8,128)(2,1)} %copy-done.5, bf16[256,2560]{1,0:T(8,128)(2,1)} %shard_map.64.rest_0_), custom_call_target="tpu_custom_call", output_to_operand_aliasing={{}: (3, {})} | custom-call | flops 1310720 | bytes 1966080 | tf_op jit(solution)/shard_map/pallas_call | solution.py:184
  (36 shorter events, 17.3 us)
Async XLA Ops:
  0.0 9.1 %copy-start.7 = (s32[1,1,2]{2,1,0:T(1,128)S(1)}, s32[1,1,2]{2,1,0:T(1,128)}, u32[]{:S(2)}) copy-start(s32[1,1,2]{2,1,0:T(1,128)} %param.11) | copy-start | bytes 28
  2.9 39.4 %collective-permute-start.2 = (bf16[2,256,2560]{2,1,0:T(8,128)(2,1)}, bf16[2,256,2560]{2,1,0:T(8,128)(2,1)S(1)}, u32[]{:S(2)}, u32[]{:S(2)}) collective-permute-start(bf16[2,256,2560]{2,1,0:T(8,128)(2,1)} %shard_map.55), channel_id=1, source_target_pairs={{0,1},{1,2},{2,3},{3,4},{4,5},{5,6},{6,7},{8,9},{9,10},{10,11},{11... | collective-permute-start | bytes 7864328 | tf_op jit(solution)/shard_map/ppermute | solution.py:257
  4.8 37.5 %collective-permute-start.3 = (bf16[2,256,2560]{2,1,0:T(8,128)(2,1)}, bf16[2,256,2560]{2,1,0:T(8,128)(2,1)}, u32[]{:S(2)}, u32[]{:S(2)}) collective-permute-start(bf16[2,256,2560]{2,1,0:T(8,128)(2,1)} %shard_map.55), channel_id=1, source_target_pairs={{1,0},{2,1},{3,2},{4,3},{5,4},{6,5},{7,6},{9,8},{10,9},{11,10},{12... | collective-permute-start | bytes 7864328 | tf_op jit(solution)/shard_map/ppermute | solution.py:258
  11.5 20.5 %collective-permute-start.1 = (bf16[272,1280]{1,0:T(8,128)(2,1)S(1)}, bf16[272,1280]{1,0:T(8,128)(2,1)}, u32[]{:S(2)}, u32[]{:S(2)}) collective-permute-start(bf16[272,1280]{1,0:T(8,128)(2,1)S(1)} %pad_maximum_fusion), channel_id=1, source_target_pairs={{8,0},{16,8},{24,16},{32,24},{40,32},{48,40},{56,48},{64,56},{72,6... | collective-permute-start | bytes 2088968 | tf_op jit(solution)/shard_map/ppermute | solution.py:224
  16.0 35.5 %collective-permute-start = (bf16[256,1280]{1,0:T(8,128)(2,1)}, bf16[256,1280]{1,0:T(8,128)(2,1)}, u32[]{:S(2)}, u32[]{:S(2)}) collective-permute-start(bf16[256,1280]{1,0:T(8,128)(2,1)} %get-tuple-element.32), channel_id=1, source_target_pairs={{8,0},{16,8},{24,16},{32,24},{40,32},{48,40},{56,48},{64,56},{72,6... | collective-permute-start | bytes 1966088 | tf_op jit(solution)/shard_map/ppermute | solution.py:224
  32.0 28.9 %collective-permute-start.4 = (bf16[272,1280]{1,0:T(8,128)(2,1)}, bf16[272,1280]{1,0:T(8,128)(2,1)S(1)}, u32[]{:S(2)}, u32[]{:S(2)}) collective-permute-start(bf16[272,1280]{1,0:T(8,128)(2,1)} %collective-permute-done.1.q_ref), channel_id=1, source_target_pairs={{8,0},{16,8},{24,16},{32,24},{40,32},{48,40},{56,48},{64,56},{72,6... | collective-permute-start | bytes 2088968 | tf_op jit(solution)/shard_map/ppermute | solution.py:224
  42.3 1.5 %copy-start = (bf16[2,256,2560]{2,1,0:T(8,128)(2,1)}, bf16[2,256,2560]{2,1,0:T(8,128)(2,1)S(1)}, u32[]{:S(2)}) copy-start(bf16[2,256,2560]{2,1,0:T(8,128)(2,1)S(1)} %collective-permute-done.2.kl_ref.vl_ref) | copy-start | bytes 7864324
  59.0 15.9 %collective-permute-start.5 = (bf16[256,1280]{1,0:T(8,128)(2,1)}, bf16[256,1280]{1,0:T(8,128)(2,1)S(1)}, u32[]{:S(2)}, u32[]{:S(2)}) collective-permute-start(bf16[256,1280]{1,0:T(8,128)(2,1)} %collective-permute-done.q_ref), channel_id=1, source_target_pairs={{8,0},{16,8},{24,16},{32,24},{40,32},{48,40},{56,48},{64,56},{72,6... | collective-permute-start | bytes 1966088 | tf_op jit(solution)/shard_map/ppermute | solution.py:224
  61.0 3.3 %copy-start.1 = (bf16[272,1280]{1,0:T(8,128)(2,1)}, bf16[272,1280]{1,0:T(8,128)(2,1)S(1)}, u32[]{:S(2)}) copy-start(bf16[272,1280]{1,0:T(8,128)(2,1)S(1)} %collective-permute-done.4.q_ref) | copy-start | bytes 2088964
  68.0 26.6 %collective-permute-start.7 = (bf16[272,1280]{1,0:T(8,128)(2,1)}, bf16[272,1280]{1,0:T(8,128)(2,1)S(1)}, u32[]{:S(2)}, u32[]{:S(2)}) collective-permute-start(bf16[272,1280]{1,0:T(8,128)(2,1)} %shard_map.59), channel_id=1, source_target_pairs={{0,8},{8,16},{16,24},{24,32},{32,40},{40,48},{48,56},{56,64},{64,7... | collective-permute-start | bytes 2088968 | tf_op jit(solution)/shard_map/ppermute | solution.py:224
  74.9 0.8 copy-start.6
  79.5 30.1 %collective-permute-start.6 = (bf16[272,1280]{1,0:T(8,128)(2,1)}, bf16[272,1280]{1,0:T(8,128)(2,1)S(1)}, u32[]{:S(2)}, u32[]{:S(2)}) collective-permute-start(bf16[272,1280]{1,0:T(8,128)(2,1)} %shard_map.58), channel_id=1, source_target_pairs={{0,8},{8,16},{16,24},{24,32},{32,40},{40,48},{48,56},{56,64},{64,7... | collective-permute-start | bytes 2088968 | tf_op jit(solution)/shard_map/ppermute | solution.py:224
  94.7 0.9 copy-start.4
  98.5 26.0 %collective-permute-start.9 = (bf16[272,1280]{1,0:T(8,128)(2,1)}, bf16[272,1280]{1,0:T(8,128)(2,1)S(1)}, u32[]{:S(2)}, u32[]{:S(2)}) collective-permute-start(bf16[272,1280]{1,0:T(8,128)(2,1)} %shard_map.60), channel_id=1, source_target_pairs={{0,8},{8,16},{16,24},{24,32},{32,40},{40,48},{48,56},{56,64},{64,7... | collective-permute-start | bytes 2088968 | tf_op jit(solution)/shard_map/ppermute | solution.py:224
  109.6 0.9 copy-start.3
  113.4 23.1 %collective-permute-start.8 = (bf16[272,1280]{1,0:T(8,128)(2,1)}, bf16[272,1280]{1,0:T(8,128)(2,1)S(1)}, u32[]{:S(2)}, u32[]{:S(2)}) collective-permute-start(bf16[272,1280]{1,0:T(8,128)(2,1)} %shard_map.62), channel_id=1, source_target_pairs={{0,8},{8,16},{16,24},{24,32},{32,40},{40,48},{48,56},{56,64},{64,7... | collective-permute-start | bytes 2088968 | tf_op jit(solution)/shard_map/ppermute | solution.py:224
  124.5 0.8 copy-start.2
  136.6 0.9 copy-start.5
